TPU v7x, 32 devices: a whole 2x2x4 slice. The times are simulated.
32 devices in a mesh: mol: 2 (over x), occ: 16 (over z, y, core).
Axes of the slice: x: 2, y: 2, z: 4, core: 2. Of those that a mesh axis runs over, the one named last changes fastest.
Arguments:
- integrals: bfloat16 [512, 128, 2048], P(('mol', 'occ')), parts along dimension 0, may hold values from -6 to 6
- orbitals: bfloat16 [4096, 1536], P('mol'), parts along dimension 0
- occ_energy: float32 [256], P('mol'), parts along dimension 0, may hold values from -2 to -0.3
- vir_energy: float32 [3072], P('mol'), parts along dimension 0, may hold values from 0.1 to 3
- owner: int32 [16], P('mol'), parts along dimension 0, may hold values from 0 to 127
- vblock: int32 [16], P('mol'), parts along dimension 0, may hold values from 0 to 7
Outputs:
- factors: bfloat16 [512, 128, 1536], P('mol', 'occ'), parts along dimension 0
- pair_energy: float32 [256, 8], P(('mol', 'occ')), parts along dimension 0
There are 2 independent parts, one for each index of `mol`. A program takes and returns all parts, laid end to end along the dimension named above; each array names one. Nothing has to cross between parts.
Inputs may be any that keep to these rules, and one draw needn't show every extreme that they name: `owner`: each step names one occupied orbital and one virtual block; steps may repeat.
All inputs are finite; a program needn't handle non-finite values.
Results may differ from a plain program's by a relative error of at most 0.001.
Values may be sent and summed in bfloat16 or wider, within the bound.
No kernel may reach another device: no remote copies, remote signals or barrier semaphores. Data moves between devices by JAX's collectives and lax.ppermute only.
A program may use at most 128 MiB of HBM per device.

v0:
```python
import jax
import jax.numpy as jnp
from jax import lax
from jax.sharding import PartitionSpec as P

VBLK = 192


def from_root(x, axis, root):
    mine = lax.axis_index(axis) == root
    return lax.psum(jnp.where(mine, x, jnp.zeros_like(x)), axis)


def pick_block(factors, orbital_j, block_id):
    local_count = factors.shape[1]
    row = orbital_j % local_count
    piece = lax.dynamic_slice(
        factors, (jnp.int32(0), row, block_id * VBLK), (factors.shape[0], 1, VBLK)
    )
    return (piece[:, 0, :], orbital_j // local_count)


def pair_column(factors, block, occ_here, occ_energy, vir_energy, orbital_j, block_id):
    coulomb = lax.dot_general(
        factors, block, (((0,), (0,)), ((), ())), preferred_element_type=jnp.float32
    )
    vir_block = lax.dynamic_slice(vir_energy, (block_id * VBLK,), (VBLK,))
    occ_j = occ_energy[orbital_j]
    denom = vir_energy[None, :, None] + vir_block[None, None, :] - occ_here[:, None, None] - occ_j
    scale = 1.0 / (factors.shape[0] * vir_energy.shape[0] * VBLK)
    return -jnp.sum(coulomb * coulomb / denom, axis=(1, 2)) * scale


def per_device(integrals, orbitals, occ_energy, vir_energy, owner, vblock):
    aux_here, occ_total, basis_count = integrals.shape
    step_count = owner.shape[0]
    flat = integrals.reshape(aux_here * occ_total, basis_count)
    product = jnp.dot(flat, orbitals, preferred_element_type=jnp.float32).astype(jnp.bfloat16)
    product = product.reshape(aux_here, occ_total, orbitals.shape[1])
    factors = lax.all_to_all(product, "occ", split_axis=1, concat_axis=0, tiled=True)
    local_count = factors.shape[1]
    occ_here = lax.dynamic_slice(occ_energy, (lax.axis_index("occ") * local_count,), (local_count,))
    energies = jnp.zeros((local_count, step_count), jnp.float32)

    def step_body(step, energies):
        orbital_j = owner[step]
        block_id = vblock[step]
        piece, root = pick_block(factors, orbital_j, block_id)
        block = from_root(piece, "occ", root)
        column = pair_column(factors, block, occ_here, occ_energy, vir_energy, orbital_j, block_id)
        return lax.dynamic_update_slice(energies, column[:, None], (jnp.int32(0), step))

    energies = lax.fori_loop(0, step_count, step_body, energies)
    return (factors, energies)


def solution(mesh):
    placed = (P(("mol", "occ"), None, None), P("mol", None), P("mol"), P("mol"), P("mol"), P("mol"))
    return jax.shard_map(
        per_device,
        mesh=mesh,
        in_specs=placed,
        out_specs=(P("mol", "occ", None), P(("mol", "occ"), None)),
        check_vma=False,
    )
```

profile of v0, /device:TPU:13, one launch (start us, length us, event | category | flops | bytes accessed | tf_op | source)
XLA Modules:
  0.0 987.8 jit_solution(14299061636335354797)
XLA Ops:
  7.2 17.3 %convolution_convert_fusion = bf16[2048,1536]{1,0:T(8,128)(2,1)S(1)} fusion(bf16[2048,2048]{1,0:T(8,128)(2,1)} %bitcast.42, bf16[2048,1536]{1,0:T(8,128)(2,1)} %param.9), kind=kOutput, calls=%fused_computation.6 | convolution fusion | flops 12888047616 | bytes 20971520 | tf_op jit(solution)/shard_map/dot_general | solution.py:38
  24.4 6.2 copy.13
  30.6 6.7 all-to-all-start
  37.4 137.3 %all-to-all-done = bf16[16,128,1536]{2,0,1:T(8,128)(2,1)} async-done(((bf16[16,128,1536]{2,0,1:T(8,128)(2,1)}), bf16[16,128,1536]{2,0,1:T(8,128)(2,1)}, u32[]{:S(2)}, u32[]{:S(2)}) %all-to-all-start) | async-done | bytes 6291488 | tf_op jit(solution)/shard_map/all_to_all | solution.py:40
  174.7 9.6 copy.14
  184.3 9.1 copy.15
  193.5 786.8 %while.15 = (s32[]{:T(128)}, f32[8,8]{0,1:T(8,128)S(1)}, s32[8]{0:T(128)S(1)}, s32[8]{0:T(128)S(1)}, bf16[256,8,1536]{0,2,1:T(8,128)(2,1)}, /*index=5*/f32[1536]...) while((s32[]{:T(128)}, f32[8,8]{0,1:T(8,128)S(1)}, ...), condition=%wide.region_3.4_spmd, body=%wide.region_0.3_spmd.sunk | while | flops 1220149248 | bytes 9544719 | solution.py:53
  198.0 1.6 select_bitcast_fusion.2
  201.7 82.4 %all-reduce.2.cloned.1.call-done = bf16[256,192]{0,1:T(8,128)(2,1)} async-done(((bf16[256,192]{0,1:T(8,128)(2,1)}), bf16[256,192]{0,1:T(8,128)(2,1)}) %all-reduce.2.cloned.1.call-update) | async-done | bytes 98320 | tf_op jit(solution)/shard_map/while/body/eval_jaxpr/psum | solution.py:11
  284.1 6.1 fusion.10
  298.5 84.2 %all-reduce.2.cloned.1.call-done = bf16[256,192]{0,1:T(8,128)(2,1)} async-done(((bf16[256,192]{0,1:T(8,128)(2,1)}), bf16[256,192]{0,1:T(8,128)(2,1)}) %all-reduce.2.cloned.1.call-update) | async-done | bytes 98320 | tf_op jit(solution)/shard_map/while/body/eval_jaxpr/psum | solution.py:11
  382.7 6.2 fusion.10
  397.1 84.2 %all-reduce.2.cloned.1.call-done = bf16[256,192]{0,1:T(8,128)(2,1)} async-done(((bf16[256,192]{0,1:T(8,128)(2,1)}), bf16[256,192]{0,1:T(8,128)(2,1)}) %all-reduce.2.cloned.1.call-update) | async-done | bytes 98320 | tf_op jit(solution)/shard_map/while/body/eval_jaxpr/psum | solution.py:11
  481.3 6.2 fusion.10
  495.6 84.2 %all-reduce.2.cloned.1.call-done = bf16[256,192]{0,1:T(8,128)(2,1)} async-done(((bf16[256,192]{0,1:T(8,128)(2,1)}), bf16[256,192]{0,1:T(8,128)(2,1)}) %all-reduce.2.cloned.1.call-update) | async-done | bytes 98320 | tf_op jit(solution)/shard_map/while/body/eval_jaxpr/psum | solution.py:11
  579.8 6.2 fusion.10
  594.2 84.2 %all-reduce.2.cloned.1.call-done = bf16[256,192]{0,1:T(8,128)(2,1)} async-done(((bf16[256,192]{0,1:T(8,128)(2,1)}), bf16[256,192]{0,1:T(8,128)(2,1)}) %all-reduce.2.cloned.1.call-update) | async-done | bytes 98320 | tf_op jit(solution)/shard_map/while/body/eval_jaxpr/psum | solution.py:11
  678.4 6.2 fusion.10
  692.8 84.2 %all-reduce.2.cloned.1.call-done = bf16[256,192]{0,1:T(8,128)(2,1)} async-done(((bf16[256,192]{0,1:T(8,128)(2,1)}), bf16[256,192]{0,1:T(8,128)(2,1)}) %all-reduce.2.cloned.1.call-update) | async-done | bytes 98320 | tf_op jit(solution)/shard_map/while/body/eval_jaxpr/psum | solution.py:11
  776.9 6.2 fusion.10
  791.3 84.2 %all-reduce.2.cloned.1.call-done = bf16[256,192]{0,1:T(8,128)(2,1)} async-done(((bf16[256,192]{0,1:T(8,128)(2,1)}), bf16[256,192]{0,1:T(8,128)(2,1)}) %all-reduce.2.cloned.1.call-update) | async-done | bytes 98320 | tf_op jit(solution)/shard_map/while/body/eval_jaxpr/psum | solution.py:11
  875.5 6.2 fusion.10
  889.9 84.2 %all-reduce.2.cloned.1.call-done = bf16[256,192]{0,1:T(8,128)(2,1)} async-done(((bf16[256,192]{0,1:T(8,128)(2,1)}), bf16[256,192]{0,1:T(8,128)(2,1)}) %all-reduce.2.cloned.1.call-update) | async-done | bytes 98320 | tf_op jit(solution)/shard_map/while/body/eval_jaxpr/psum | solution.py:11
  974.1 6.2 fusion.10
  (90 shorter events, 29.4 us)
Async XLA Ops:
  30.6 6.7 copy-start.3
  30.6 144.1 %all-to-all-start = ((bf16[16,128,1536]{2,0,1:T(8,128)(2,1)}), bf16[16,128,1536]{2,0,1:T(8,128)(2,1)}, u32[]{:S(2)}, u32[]{:S(2)}) async-start(bf16[16,128,1536]{2,0,1:T(8,128)(2,1)} %copy.13), calls=%async_computation | async-start | bytes 12582912 | tf_op jit(solution)/shard_map/all_to_all | solution.py:40
  184.3 9.1 copy-start
  184.3 9.1 copy-start.1
  184.3 9.1 copy-start.2
  193.5 90.6 %all-reduce.2.cloned.1.call-start = ((), (), s32[]{:S(2)}) async-start(), calls=%async_computation.1 | async-start | bytes 196608 | tf_op jit(solution)/shard_map/while/body/eval_jaxpr/psum | solution.py:11
  290.3 92.4 %all-reduce.2.cloned.1.call-start = ((), (), s32[]{:S(2)}) async-start(), calls=%async_computation.1 | async-start | bytes 196608 | tf_op jit(solution)/shard_map/while/body/eval_jaxpr/psum | solution.py:11
  388.9 92.4 %all-reduce.2.cloned.1.call-start = ((), (), s32[]{:S(2)}) async-start(), calls=%async_computation.1 | async-start | bytes 196608 | tf_op jit(solution)/shard_map/while/body/eval_jaxpr/psum | solution.py:11
  487.5 92.4 %all-reduce.2.cloned.1.call-start = ((), (), s32[]{:S(2)}) async-start(), calls=%async_computation.1 | async-start | bytes 196608 | tf_op jit(solution)/shard_map/while/body/eval_jaxpr/psum | solution.py:11
  586.0 92.4 %all-reduce.2.cloned.1.call-start = ((), (), s32[]{:S(2)}) async-start(), calls=%async_computation.1 | async-start | bytes 196608 | tf_op jit(solution)/shard_map/while/body/eval_jaxpr/psum | solution.py:11
  684.6 92.4 %all-reduce.2.cloned.1.call-start = ((), (), s32[]{:S(2)}) async-start(), calls=%async_computation.1 | async-start | bytes 196608 | tf_op jit(solution)/shard_map/while/body/eval_jaxpr/psum | solution.py:11
  783.1 92.4 %all-reduce.2.cloned.1.call-start = ((), (), s32[]{:S(2)}) async-start(), calls=%async_computation.1 | async-start | bytes 196608 | tf_op jit(solution)/shard_map/while/body/eval_jaxpr/psum | solution.py:11
  881.7 92.4 %all-reduce.2.cloned.1.call-start = ((), (), s32[]{:S(2)}) async-start(), calls=%async_computation.1 | async-start | bytes 196608 | tf_op jit(solution)/shard_map/while/body/eval_jaxpr/psum | solution.py:11
Sparse Core Ops, SparseCore 0:
  199.7 84.3 all-reduce.1
  296.5 86.1 all-reduce.1
  395.1 86.1 all-reduce.1
  493.6 86.1 all-reduce.1
  592.2 86.1 all-reduce.1
  690.8 86.1 all-reduce.1
  789.3 86.1 all-reduce.1
  887.9 86.1 all-reduce.1
where the time goes:
time: 993 us; the launch traced here: 988 us
  waiting for transfers between devices  809 us (81%)
  matrix products  66.5 us (7%)
  local copies, waits for them, and re-layouts  41.6 us (4%)
  loops' own time  35.7 us (4%)
  between operations  14 us (1%)
  other arithmetic  13.8 us (1%)
    psum x8, waiting for transfers between devices, from_root(): return lax.psum(jnp.where(mine, x, jnp.zeros_like(x)), axis)  672 us
    all_to_all x1, waiting for transfers between devices, per_device(): lax.all_to_all(product, 'occ', split_axis=1, concat_axis=0, tiled=True)  137 us
    dot_general x8, matrix products, pair_column(): lax.dot_general(factors, block, (((0,), (0,)), ((), ())), preferred_eleme...  49.2 us
    another operation x1, loops' own time, per_device(): energies = lax.fori_loop(0, step_count, step_body, energies)  35.7 us
  transfers between devices with their start and end apart: 9, of which 9 were waited for; matrix products, arithmetic and copies ran while one was open for 1% of the time, Pallas kernels for 0%

commit v1 on v0

--- a/solution.py
+++ b/solution.py
@@ -4,20 +4,6 @@
 from jax.sharding import PartitionSpec as P
 
 VBLK = 192
-
-
-def from_root(x, axis, root):
-    mine = lax.axis_index(axis) == root
-    return lax.psum(jnp.where(mine, x, jnp.zeros_like(x)), axis)
-
-
-def pick_block(factors, orbital_j, block_id):
-    local_count = factors.shape[1]
-    row = orbital_j % local_count
-    piece = lax.dynamic_slice(
-        factors, (jnp.int32(0), row, block_id * VBLK), (factors.shape[0], 1, VBLK)
-    )
-    return (piece[:, 0, :], orbital_j // local_count)
 
 
 def pair_column(factors, block, occ_here, occ_energy, vir_energy, orbital_j, block_id):
@@ -37,6 +23,15 @@
     flat = integrals.reshape(aux_here * occ_total, basis_count)
     product = jnp.dot(flat, orbitals, preferred_element_type=jnp.float32).astype(jnp.bfloat16)
     product = product.reshape(aux_here, occ_total, orbitals.shape[1])
+
+    def own_piece(step):
+        piece = lax.dynamic_slice(
+            product, (jnp.int32(0), owner[step], vblock[step] * VBLK), (aux_here, 1, VBLK)
+        )
+        return piece[:, 0, :]
+
+    pieces = jnp.stack([own_piece(step) for step in range(step_count)], axis=1)
+    blocks = lax.all_gather(pieces, "occ", axis=0, tiled=True)
     factors = lax.all_to_all(product, "occ", split_axis=1, concat_axis=0, tiled=True)
     local_count = factors.shape[1]
     occ_here = lax.dynamic_slice(occ_energy, (lax.axis_index("occ") * local_count,), (local_count,))
@@ -45,8 +40,7 @@
     def step_body(step, energies):
         orbital_j = owner[step]
         block_id = vblock[step]
-        piece, root = pick_block(factors, orbital_j, block_id)
-        block = from_root(piece, "occ", root)
+        block = lax.dynamic_index_in_dim(blocks, step, axis=1, keepdims=False)
         column = pair_column(factors, block, occ_here, occ_energy, vir_energy, orbital_j, block_id)
         return lax.dynamic_update_slice(energies, column[:, None], (jnp.int32(0), step))
 

time: 993 us -> 287 us (0.29)
  waiting for transfers between devices: 809 us -> 0.01 us
  blocking collectives: 0 us -> 127 us
  loops' own time: 35.7 us -> 20.6 us
  other arithmetic: 13.8 us -> 1.21 us
    psum x8 -> x0, waiting for transfers between devices: 672 us -> none  [from_root(): return lax.psum(jnp.where(mine, x, jnp.zeros_like(x)), axis)]
    all_to_all x1, waiting for transfers between devices: 137 us -> 0.01 us  [per_device(): lax.all_to_all(product, 'occ', split_axis=1, concat_axis=0, tiled=True)]
    all_gather x0 -> x1, blocking collectives: none -> 127 us  [per_device(): blocks = lax.all_gather(pieces, 'occ', axis=0, tiled=True)]
    another operation x1, loops' own time: 35.7 us -> 20.6 us  [per_device(): energies = lax.fori_loop(0, step_count, step_body, energies)]
    select_n x8 -> x0, other arithmetic: 12.6 us -> none  [from_root(): return lax.psum(jnp.where(mine, x, jnp.zeros_like(x)), axis)]
  transfers between devices with their start and end apart: 9 -> 1, of which waited for: 9 -> 0; matrix products, arithmetic and copies ran while one was open for 1% -> 1% of each run, Pallas kernels for 0% -> 0%
where the time goes in v1:
time: 287 us; the launch traced here: 285 us
  blocking collectives  127 us (44%)
  matrix products  67.4 us (23%)
  local copies, waits for them, and re-layouts  40.8 us (14%)
  between operations  21.1 us (7%)
  loops' own time  20.6 us (7%)
  starting transfers between devices  6.69 us (2%)
    all_gather x1, blocking collectives, per_device(): blocks = lax.all_gather(pieces, 'occ', axis=0, tiled=True)  127 us
    dot_general x8, matrix products, pair_column(): lax.dot_general(factors, block, (((0,), (0,)), ((), ())), preferred_eleme...  50.1 us
    another operation x1, loops' own time, per_device(): energies = lax.fori_loop(0, step_count, step_body, energies)  20.6 us
    dot_general x1, matrix products, per_device(): jnp.dot(flat, orbitals, preferred_element_type=jnp.float32)  17.3 us
    all_to_all x1, local copies, waits for them, and re-layouts, per_device(): lax.all_to_all(product, 'occ', split_axis=1, concat_axis=0, tiled=True)  6.9 us
    all_to_all x1, starting transfers between devices, per_device(): lax.all_to_all(product, 'occ', split_axis=1, concat_axis=0, tiled=True)  6.69 us
    reshape x1, local copies, waits for them, and re-layouts, per_device(): product = product.reshape(aux_here, occ_total, orbitals.shape[1])  6.2 us
  transfers between devices with their start and end apart: 1, of which 0 were waited for; matrix products, arithmetic and copies ran while one was open for 1% of the time, Pallas kernels for 0%

profile of v1, /device:TPU:13, one launch (start us, length us, event | category | flops | bytes accessed | tf_op | source)
XLA Modules:
  0.0 284.5 jit_solution(6650717841820332586)
XLA Ops:
  0.6 17.3 %convolution_convert_fusion = bf16[2048,1536]{1,0:T(8,128)(2,1)S(1)} fusion(bf16[2048,2048]{1,0:T(8,128)(2,1)} %bitcast.56, bf16[2048,1536]{1,0:T(8,128)(2,1)} %param.9), kind=kOutput, calls=%fused_computation.7 | convolution fusion | flops 12888047616 | bytes 20971520 | tf_op jit(solution)/shard_map/dot_general | solution.py:24
  17.9 2.6 copy-done.1
  20.5 6.2 %copy.19 = bf16[16,128,1536]{2,0,1:T(8,128)(2,1)} copy(bf16[16,128,1536]{2,1,0:T(8,128)(2,1)S(1)} %bitcast.54) | data formatting | bytes 12582912 | tf_op jit(solution)/shard_map/reshape | solution.py:25
  26.8 6.7 %all-to-all-start = ((bf16[16,128,1536]{2,0,1:T(8,128)(2,1)}), bf16[16,128,1536]{2,0,1:T(8,128)(2,1)}, u32[]{:S(2)}, u32[]{:S(2)}) async-start(bf16[16,128,1536]{2,0,1:T(8,128)(2,1)} %copy.19), calls=%async_computation | async-start | bytes 12582912 | tf_op jit(solution)/shard_map/all_to_all | solution.py:35
  33.4 0.7 fusion.4
  39.2 0.7 fusion.5
  55.2 1.6 constant_dynamic-slice_fusion
  56.9 126.8 %all_gather.3 = bf16[256,8,192]{2,1,0:T(8,128)(2,1)S(1)} all-gather(bf16[16,8,192]{2,1,0:T(8,128)(2,1)S(1)} %stack.3), channel_id=1, replica_groups=mesh['mol'=2,'occ'=16] {'occ'}, dimensions={0}, use_global_device_ids=true | all-gather | bytes 835584 | tf_op jit(solution)/shard_map/all_gather | solution.py:34
  183.7 1.0 copy.21
  184.8 6.9 %copy.20 = bf16[16,16,8,1536]{3,2,1,0:T(8,128)(2,1)S(1)} copy(bf16[16,16,8,1536]{3,1,2,0:T(8,128)(2,1)} %bitcast.10) | data formatting | bytes 12582912 | tf_op jit(solution)/shard_map/all_to_all | solution.py:35
  191.7 4.7 %copy.22 = bf16[256,8,1536]{2,0,1:T(8,128)(2,1)} copy(bf16[256,8,1536]{2,1,0:T(8,128)(2,1)S(1)} %bitcast.52) | data formatting | bytes 12582912 | tf_op jit(solution)/shard_map/while | solution.py:47
  196.4 87.4 %while.13 = (s32[]{:T(128)}, f32[8,8]{0,1:T(8,128)S(1)}, bf16[256,8,192]{0,2,1:T(8,128)(2,1)S(1)}, bf16[256,8,1536]{2,0,1:T(8,128)(2,1)}, f32[1536]{0:T(1024)S(1...) while((s32[]{:T(128)}, f32[8,8]{0,1:T(8,128)S(1)}, ...), condition=%wide.region_2.3_spmd, body=%wide.region_0.2_spmd.sunk | while | flops 1220050944 | bytes 8758441 | solution.py:47
  197.9 0.6 dynamic_slice.90
  201.1 6.3 %fusion.14 = f32[8]{0:T(128)S(1)} fusion(bf16[256,8,1536]{2,0,1:T(8,128)(2,1)} %get-tuple-element.307, f32[]{:T(128)} %bitcast.50, f32[8]{0:T(128)S(1)} %get-tuple-element.310, f32[1536,192]{0,1:T(8,128)S(1)} %broadcast_add_fusion.2, bf16[256,8,192]{0,2,1:T(8,128)(2,1)S(1)} %get-tuple-element.306, s32[]{:T(128)} %get-tuple-element.290), kind=kOutput, calls=%fused_computation.1.clone.1 | convolution fusion | flops 1219756032 | bytes 7569960 | tf_op jit(solution)/shard_map/while/body/eval_jaxpr/dot_general | solution.py:10
  208.9 0.6 dynamic_slice.90
  212.0 6.3 %fusion.14 = f32[8]{0:T(128)S(1)} fusion(bf16[256,8,1536]{2,0,1:T(8,128)(2,1)} %get-tuple-element.307, f32[]{:T(128)} %bitcast.50, f32[8]{0:T(128)S(1)} %get-tuple-element.310, f32[1536,192]{0,1:T(8,128)S(1)} %broadcast_add_fusion.2, bf16[256,8,192]{0,2,1:T(8,128)(2,1)S(1)} %get-tuple-element.306, s32[]{:T(128)} %get-tuple-element.290), kind=kOutput, calls=%fused_computation.1.clone.1 | convolution fusion | flops 1219756032 | bytes 7569960 | tf_op jit(solution)/shard_map/while/body/eval_jaxpr/dot_general | solution.py:10
  222.9 6.3 %fusion.14 = f32[8]{0:T(128)S(1)} fusion(bf16[256,8,1536]{2,0,1:T(8,128)(2,1)} %get-tuple-element.307, f32[]{:T(128)} %bitcast.50, f32[8]{0:T(128)S(1)} %get-tuple-element.310, f32[1536,192]{0,1:T(8,128)S(1)} %broadcast_add_fusion.2, bf16[256,8,192]{0,2,1:T(8,128)(2,1)S(1)} %get-tuple-element.306, s32[]{:T(128)} %get-tuple-element.290), kind=kOutput, calls=%fused_computation.1.clone.1 | convolution fusion | flops 1219756032 | bytes 7569960 | tf_op jit(solution)/shard_map/while/body/eval_jaxpr/dot_general | solution.py:10
  233.9 6.3 %fusion.14 = f32[8]{0:T(128)S(1)} fusion(bf16[256,8,1536]{2,0,1:T(8,128)(2,1)} %get-tuple-element.307, f32[]{:T(128)} %bitcast.50, f32[8]{0:T(128)S(1)} %get-tuple-element.310, f32[1536,192]{0,1:T(8,128)S(1)} %broadcast_add_fusion.2, bf16[256,8,192]{0,2,1:T(8,128)(2,1)S(1)} %get-tuple-element.306, s32[]{:T(128)} %get-tuple-element.290), kind=kOutput, calls=%fused_computation.1.clone.1 | convolution fusion | flops 1219756032 | bytes 7569960 | tf_op jit(solution)/shard_map/while/body/eval_jaxpr/dot_general | solution.py:10
  241.6 0.6 dynamic_slice.90
  244.8 6.3 %fusion.14 = f32[8]{0:T(128)S(1)} fusion(bf16[256,8,1536]{2,0,1:T(8,128)(2,1)} %get-tuple-element.307, f32[]{:T(128)} %bitcast.50, f32[8]{0:T(128)S(1)} %get-tuple-element.310, f32[1536,192]{0,1:T(8,128)S(1)} %broadcast_add_fusion.2, bf16[256,8,192]{0,2,1:T(8,128)(2,1)S(1)} %get-tuple-element.306, s32[]{:T(128)} %get-tuple-element.290), kind=kOutput, calls=%fused_computation.1.clone.1 | convolution fusion | flops 1219756032 | bytes 7569960 | tf_op jit(solution)/shard_map/while/body/eval_jaxpr/dot_general | solution.py:10
  255.7 6.3 %fusion.14 = f32[8]{0:T(128)S(1)} fusion(bf16[256,8,1536]{2,0,1:T(8,128)(2,1)} %get-tuple-element.307, f32[]{:T(128)} %bitcast.50, f32[8]{0:T(128)S(1)} %get-tuple-element.310, f32[1536,192]{0,1:T(8,128)S(1)} %broadcast_add_fusion.2, bf16[256,8,192]{0,2,1:T(8,128)(2,1)S(1)} %get-tuple-element.306, s32[]{:T(128)} %get-tuple-element.290), kind=kOutput, calls=%fused_computation.1.clone.1 | convolution fusion | flops 1219756032 | bytes 7569960 | tf_op jit(solution)/shard_map/while/body/eval_jaxpr/dot_general | solution.py:10
  266.6 6.3 %fusion.14 = f32[8]{0:T(128)S(1)} fusion(bf16[256,8,1536]{2,0,1:T(8,128)(2,1)} %get-tuple-element.307, f32[]{:T(128)} %bitcast.50, f32[8]{0:T(128)S(1)} %get-tuple-element.310, f32[1536,192]{0,1:T(8,128)S(1)} %broadcast_add_fusion.2, bf16[256,8,192]{0,2,1:T(8,128)(2,1)S(1)} %get-tuple-element.306, s32[]{:T(128)} %get-tuple-element.290), kind=kOutput, calls=%fused_computation.1.clone.1 | convolution fusion | flops 1219756032 | bytes 7569960 | tf_op jit(solution)/shard_map/while/body/eval_jaxpr/dot_general | solution.py:10
  277.6 6.3 %fusion.14 = f32[8]{0:T(128)S(1)} fusion(bf16[256,8,1536]{2,0,1:T(8,128)(2,1)} %get-tuple-element.307, f32[]{:T(128)} %bitcast.50, f32[8]{0:T(128)S(1)} %get-tuple-element.310, f32[1536,192]{0,1:T(8,128)S(1)} %broadcast_add_fusion.2, bf16[256,8,192]{0,2,1:T(8,128)(2,1)S(1)} %get-tuple-element.306, s32[]{:T(128)} %get-tuple-element.290), kind=kOutput, calls=%fused_computation.1.clone.1 | convolution fusion | flops 1219756032 | bytes 7569960 | tf_op jit(solution)/shard_map/while/body/eval_jaxpr/dot_general | solution.py:10
  283.9 0.7 copy.23
  (68 shorter events, 15.2 us)
Async XLA Ops:
  17.9 2.6 copy-start.1
  26.7 6.7 %copy-start.4 = (s32[8]{0:T(128)S(1)}, s32[8]{0:T(128)}, u32[]{:S(2)}) copy-start(s32[8]{0:T(128)} %param.13) | copy-start | bytes 100
  26.7 12.4 %copy-start.3 = (s32[8]{0:T(128)S(1)}, s32[8]{0:T(128)}, u32[]{:S(2)}) copy-start(s32[8]{0:T(128)} %param.12) | copy-start | bytes 100
  26.7 158.0 %copy-start.5 = (f32[128]{0:T(128)S(1)}, f32[128]{0:T(128)}, u32[]{:S(2)}) copy-start(f32[128]{0:T(128)} %param.10) | copy-start | bytes 1540
  26.8 158.0 %all-to-all-start = ((bf16[16,128,1536]{2,0,1:T(8,128)(2,1)}), bf16[16,128,1536]{2,0,1:T(8,128)(2,1)}, u32[]{:S(2)}, u32[]{:S(2)}) async-start(bf16[16,128,1536]{2,0,1:T(8,128)(2,1)} %copy.19), calls=%async_computation | async-start | bytes 12582912 | tf_op jit(solution)/shard_map/all_to_all | solution.py:35
  191.7 4.7 %copy-start = (bf16[16,16,8,1536]{3,2,1,0:T(8,128)(2,1)}, bf16[16,16,8,1536]{3,2,1,0:T(8,128)(2,1)S(1)}, u32[]{:S(2)}) copy-start(bf16[16,16,8,1536]{3,2,1,0:T(8,128)(2,1)S(1)} %copy.20) | copy-start | bytes 18874372
  191.7 4.7 %copy-start.2 = (f32[1536]{0:T(1024)S(1)}, f32[1536]{0:T(1024)}, u32[]{:S(2)}) copy-start(f32[1536]{0:T(1024)} %param.11) | copy-start | bytes 18436

commit v2 on v1

v2 whole, which is shorter than its diff:
```python
import jax
import jax.numpy as jnp
from jax import lax
from jax.sharding import PartitionSpec as P

VBLK = 192
CHUNKS = 4


def chunk_energies(factors, blocks, occ_rows, occ_cols, vir_energy, vir_blocks, scale):
    coulomb = lax.dot_general(
        factors, blocks, (((0,), (0,)), ((), ())), preferred_element_type=jnp.float32
    )
    denom = (
        vir_energy[None, :, None, None]
        + vir_blocks[None, None, :, :]
        - occ_rows[:, None, None, None]
        - occ_cols[None, None, :, None]
    )
    return -jnp.sum(coulomb * coulomb / denom, axis=(1, 3)) * scale


def per_device(integrals, orbitals, occ_energy, vir_energy, owner, vblock):
    aux_here, occ_total, basis_count = integrals.shape
    nvir = orbitals.shape[1]
    step_count = owner.shape[0]
    groups = lax.psum(1, "occ")
    local_count = occ_total // groups
    chunks = CHUNKS
    while local_count % chunks:
        chunks -= 1
    width = local_count // chunks
    flat = integrals.reshape(aux_here * occ_total, basis_count)
    product = jnp.dot(flat, orbitals, preferred_element_type=jnp.float32).astype(jnp.bfloat16)
    product = product.reshape(aux_here, groups, local_count, nvir)

    def own_piece(step):
        piece = lax.dynamic_slice(
            product.reshape(aux_here, occ_total, nvir),
            (jnp.int32(0), owner[step], vblock[step] * VBLK),
            (aux_here, 1, VBLK),
        )
        return piece[:, 0, :]

    pieces = jnp.stack([own_piece(step) for step in range(step_count)], axis=1)
    pieces = pieces.reshape(aux_here, 1, 1, step_count * VBLK)
    extra = jnp.broadcast_to(pieces, (aux_here, groups, 1, step_count * VBLK))

    me = lax.axis_index("occ")
    occ_here = lax.dynamic_slice(occ_energy, (me * local_count,), (local_count,))
    occ_cols = occ_energy[owner]
    vir_blocks = jnp.stack(
        [lax.dynamic_slice(vir_energy, (vblock[s] * VBLK,), (VBLK,)) for s in range(step_count)]
    )
    scale = 1.0 / (aux_here * groups * nvir * VBLK)

    parts = []
    columns = []
    blocks = None
    for c in range(chunks):
        payload = product[:, :, c * width:(c + 1) * width, :]
        if c == 0 and step_count * VBLK == nvir:
            payload = jnp.concatenate([payload, extra], axis=2)
        payload = payload.reshape(aux_here, groups * payload.shape[2], nvir)
        if c >= 1:
            held = (parts[-1],) + tuple(columns[-2:-1])
            payload, _ = lax.optimization_barrier((payload, held))
        got = lax.all_to_all(payload, "occ", split_axis=1, concat_axis=0, tiled=True)
        if c == 0:
            if step_count * VBLK == nvir:
                blocks = got[:, width, :].reshape(aux_here * groups, step_count, VBLK)
                got = got[:, :width, :]
            else:
                blocks = lax.all_gather(
                    pieces.reshape(aux_here, step_count, VBLK), "occ", axis=0, tiled=True
                )
        parts.append(got)
        columns.append(
            chunk_energies(
                got, blocks, occ_here[c * width:(c + 1) * width], occ_cols,
                vir_energy, vir_blocks, scale,
            )
        )
    factors = jnp.concatenate(parts, axis=1)
    energies = jnp.concatenate(columns, axis=0)
    return (factors, energies)


def solution(mesh):
    placed = (P(("mol", "occ"), None, None), P("mol", None), P("mol"), P("mol"), P("mol"), P("mol"))
    return jax.shard_map(
        per_device,
        mesh=mesh,
        in_specs=placed,
        out_specs=(P("mol", "occ", None), P(("mol", "occ"), None)),
        check_vma=False,
    )
```

time: 287 us -> 271 us (0.944)
  blocking collectives: 127 us -> 0 us
  waiting for transfers between devices: 0.01 us -> 124 us
  matrix products: 67.4 us -> 43 us
  loops' own time: 20.6 us -> 0 us
  starting transfers between devices: 6.69 us -> 21.6 us
  other arithmetic: 1.21 us -> 10.1 us
  local copies, waits for them, and re-layouts: 40.8 us -> 49.6 us
    all_gather x1 -> x0, blocking collectives: 127 us -> none  [per_device(): blocks = lax.all_gather(pieces, 'occ', axis=0, tiled=True)]
    all_to_all x1 -> x4, waiting for transfers between devices: 0.01 us -> 124 us  [per_device(): lax.all_to_all(payload, 'occ', split_axis=1, concat_axis=0, tiled=True)]
    slice x0 -> x8, local copies, waits for them, and re-layouts: none -> 26.5 us  [the longest x4 22.9 us: per_device(): payload = product[:, :, c * width:(c + 1) * width, :]]
    dot_general x8 -> x4, matrix products: 50.1 us -> 25.7 us  [chunk_energies(): lax.dot_general(factors, blocks, (((0,), (0,)), ((), ())), preferred_elem...]
    another operation x1 -> x0, loops' own time: 20.6 us -> none  [per_device(): energies = lax.fori_loop(0, step_count, step_body, energies)]
    dynamic_slice x34 -> x3, local copies, waits for them, and re-layouts: 16.9 us -> 0.5 us  [the longest x1 0.32 us: own_piece(): lax.dynamic_slice(product.reshape(aux_here, occ_total, nvir), (jnp.int32(...]
    all_to_all x1 -> x4, starting transfers between devices: 6.69 us -> 21.6 us  [per_device(): lax.all_to_all(payload, 'occ', split_axis=1, concat_axis=0, tiled=True)]
    unnamed x13 -> x30, local copies, waits for them, and re-layouts: 3.32 us -> 12.4 us
  transfers between devices with their start and end apart: 1 -> 4, of which waited for: 0 -> 4; matrix products, arithmetic and copies ran while one was open for 1% -> 14% of each run, Pallas kernels for 0% -> 0%
where the time goes in v2:
time: 271 us; the launch traced here: 270 us
  waiting for transfers between devices  124 us (46%)
  local copies, waits for them, and re-layouts  49.6 us (18%)
  matrix products  43 us (16%)
  starting transfers between devices  21.6 us (8%)
  between operations  21.5 us (8%)
  other arithmetic  10.1 us (4%)
    all_to_all x4, waiting for transfers between devices, per_device(): lax.all_to_all(payload, 'occ', split_axis=1, concat_axis=0, tiled=True)  124 us
    dot_general x4, matrix products, chunk_energies(): lax.dot_general(factors, blocks, (((0,), (0,)), ((), ())), preferred_elem...  25.7 us
    slice x4, local copies, waits for them, and re-layouts, per_device(): payload = product[:, :, c * width:(c + 1) * width, :]  22.9 us
    all_to_all x4, starting transfers between devices, per_device(): lax.all_to_all(payload, 'occ', split_axis=1, concat_axis=0, tiled=True)  21.6 us
    dot_general x1, matrix products, per_device(): jnp.dot(flat, orbitals, preferred_element_type=jnp.float32)  17.3 us
    unnamed x30, local copies, waits for them, and re-layouts  12.4 us
    all_to_all x4, local copies, waits for them, and re-layouts, per_device(): lax.all_to_all(payload, 'occ', split_axis=1, concat_axis=0, tiled=True)  5.87 us
  transfers between devices with their start and end apart: 4, of which 4 were waited for; matrix products, arithmetic and copies ran while one was open for 14% of the time, Pallas kernels for 0%

profile of v2, /device:TPU:13, one launch (start us, length us, event | category | flops | bytes accessed | tf_op | source)
XLA Modules:
  0.0 269.9 jit_solution(10730175310295168167)
XLA Ops:
  0.6 1.6 fusion.9
  7.5 1.6 fusion.10
  24.6 17.3 %convolution_convert_fusion = bf16[2048,1536]{1,0:T(8,128)(2,1)S(1)} fusion(bf16[2048,2048]{1,0:T(8,128)(2,1)} %bitcast.105, bf16[2048,1536]{1,0:T(8,128)(2,1)} %param.7), kind=kOutput, calls=%fused_computation.9 | convolution fusion | flops 12888047616 | bytes 20971520 | tf_op jit(solution)/shard_map/dot_general | solution.py:34
  41.9 2.7 copy-done.3
  45.2 14.0 %fusion.6 = (bf16[16,16,2,1536]{3,2,1,0:T(2,128)(2,1)S(1)}, bf16[16,16,2,1536]{3,2,1,0:T(2,128)(2,1)}, bf16[16,16,2,1536]{3,2,1,0:T(2,128)(2,1)}, bf16[16,16,2,1536]{3,2,1,0:T(2,128)(2,1)}) fusion(bf16[16,16,8,1536]{3,2,1,0:T(8,128)(2,1)} %bitcast.84), kind=kLoop, calls=%fused_computation.30 | loop fusion | bytes 12582912 | tf_op jit(solution)/shard_map/slice | solution.py:61
  61.8 6.7 %all-to-all-start = ((bf16[16,48,1536]{2,0,1:T(8,128)(2,1)}), bf16[16,48,1536]{2,0,1:T(8,128)(2,1)S(1)}, u32[]{:S(2)}, u32[]{:S(2)}) async-start(bf16[16,48,1536]{2,0,1:T(8,128)(2,1)} %bitcast.79), calls=%async_computation | async-start | bytes 4718592 | tf_op jit(solution)/shard_map/all_to_all | solution.py:68
  69.2 3.4 %copy.12 = bf16[16,16,2,1536]{3,0,2,1:T(8,128)(2,1)} copy(bf16[16,16,2,1536]{3,2,1,0:T(2,128)(2,1)} %get-tuple-element.15) | data formatting | bytes 3145728 | tf_op jit(solution)/shard_map/slice | solution.py:61
  72.6 3.5 %copy.14 = bf16[16,16,2,1536]{3,0,2,1:T(8,128)(2,1)} copy(bf16[16,16,2,1536]{3,2,1,0:T(2,128)(2,1)} %get-tuple-element.14) | data formatting | bytes 3145728 | tf_op jit(solution)/shard_map/slice | solution.py:61
  76.2 4.3 %broadcast_add_fusion = f32[1536,8,192]{0,2,1:T(8,128)} fusion(f32[8,192]{1,0:T(8,128)S(1)} %stack.39, f32[1536]{0:T(1024)S(1)} %copy-done.9), kind=kLoop, calls=%fused_computation.11 | loop fusion | flops 2359296 | bytes 9449472 | tf_op jit(solution)/shard_map/add | solution.py:15
  80.5 40.9 %all-to-all-done = bf16[16,48,1536]{2,0,1:T(8,128)(2,1)S(1)} async-done(((bf16[16,48,1536]{2,0,1:T(8,128)(2,1)}), bf16[16,48,1536]{2,0,1:T(8,128)(2,1)S(1)}, u32[]{:S(2)}, u32[]{:S(2)}) %all-to-all-start) | async-done | bytes 2359328 | tf_op jit(solution)/shard_map/all_to_all | solution.py:68
  124.3 5.0 %all-to-all-start.1 = ((bf16[16,32,1536]{2,0,1:T(8,128)(2,1)}), bf16[16,32,1536]{2,0,1:T(8,128)(2,1)}, u32[]{:S(2)}, u32[]{:S(2)}) async-start(bf16[16,32,1536]{2,0,1:T(8,128)(2,1)} %bitcast.86), calls=%async_computation.1 | async-start | bytes 3145728 | tf_op jit(solution)/shard_map/all_to_all | solution.py:68
  131.8 6.9 %fusion = f32[2,8]{1,0:T(2,128)S(1)} fusion(bf16[256,8,192,1]{0,2,1,3:T(8,128)(2,1)} %bitcast.93, f32[8]{0:T(128)S(1)} %gather_fusion, f32[2]{0:T(128)S(1)} %get-tuple-element.35, f32[1536,8,192]{0,2,1:T(8,128)} %broadcast_add_fusion, bf16[256,3,1536]{2,0,1:T(8,128)(2,1)S(1)} %bitcast.82), kind=kOutput, calls=%fused_computation.5 | convolution fusion | flops 2439512064 | bytes 11797568 | tf_op jit(solution)/shard_map/dot_general | solution.py:11
  138.7 26.9 %all-to-all-done.1 = bf16[16,32,1536]{2,0,1:T(8,128)(2,1)} async-done(((bf16[16,32,1536]{2,0,1:T(8,128)(2,1)}), bf16[16,32,1536]{2,0,1:T(8,128)(2,1)}, u32[]{:S(2)}, u32[]{:S(2)}) %all-to-all-start.1) | async-done | bytes 1572896 | tf_op jit(solution)/shard_map/all_to_all | solution.py:68
  167.1 4.9 %all-to-all-start.2 = ((bf16[16,32,1536]{2,0,1:T(8,128)(2,1)}), bf16[16,32,1536]{2,0,1:T(8,128)(2,1)}, u32[]{:S(2)}, u32[]{:S(2)}) async-start(bf16[16,32,1536]{2,0,1:T(8,128)(2,1)} %bitcast.85), calls=%async_computation.2 | async-start | bytes 3145728 | tf_op jit(solution)/shard_map/all_to_all | solution.py:68
  172.1 2.0 copy.17
  174.1 6.9 %fusion.1 = f32[2,8]{1,0:T(2,128)S(1)} fusion(bf16[256,2,1536,1]{2,0,3,1:T(8,128)(2,1)S(1)} %bitcast.87, bf16[256,8,192,1]{0,2,1,3:T(8,128)(2,1)} %bitcast.94, f32[2]{0:T(128)S(1)} %get-tuple-element.34, f32[8]{0:T(128)S(1)} %gather_fusion, f32[1536,8,192]{0,2,1:T(8,128)} %broadcast_add_fusion), kind=kOutput, calls=%fused_computation.6 | convolution fusion | flops 2439512064 | bytes 11796584 | tf_op jit(solution)/shard_map/dot_general | solution.py:11
  181.0 27.4 %all-to-all-done.2 = bf16[16,32,1536]{2,0,1:T(8,128)(2,1)} async-done(((bf16[16,32,1536]{2,0,1:T(8,128)(2,1)}), bf16[16,32,1536]{2,0,1:T(8,128)(2,1)}, u32[]{:S(2)}, u32[]{:S(2)}) %all-to-all-start.2) | async-done | bytes 1572896 | tf_op jit(solution)/shard_map/all_to_all | solution.py:68
  208.3 2.7 copy.16
  211.0 4.9 %all-to-all-start.3 = ((bf16[16,32,1536]{2,0,1:T(8,128)(2,1)}), bf16[16,32,1536]{2,0,1:T(8,128)(2,1)}, u32[]{:S(2)}, u32[]{:S(2)}) async-start(bf16[16,32,1536]{2,0,1:T(8,128)(2,1)} %bitcast.43), calls=%async_computation.3 | async-start | bytes 3145728 | tf_op jit(solution)/shard_map/all_to_all | solution.py:68
  215.9 7.2 %fusion.2 = f32[2,8]{1,0:T(2,128)S(1)} fusion(bf16[256,2,1536,1]{2,0,3,1:T(8,128)(2,1)} %bitcast.89, bf16[256,8,192,1]{0,2,1,3:T(8,128)(2,1)} %bitcast.95, f32[2]{0:T(128)S(1)} %get-tuple-element.32, f32[8]{0:T(128)S(1)} %gather_fusion, f32[1536,8,192]{0,2,1:T(8,128)} %broadcast_add_fusion), kind=kOutput, calls=%fused_computation.7 | convolution fusion | flops 2439512064 | bytes 11796584 | tf_op jit(solution)/shard_map/dot_general | solution.py:11
  223.2 29.1 %all-to-all-done.3 = bf16[16,32,1536]{2,0,1:T(8,128)(2,1)} async-done(((bf16[16,32,1536]{2,0,1:T(8,128)(2,1)}), bf16[16,32,1536]{2,0,1:T(8,128)(2,1)}, u32[]{:S(2)}, u32[]{:S(2)}) %all-to-all-start.3) | async-done | bytes 1572896 | tf_op jit(solution)/shard_map/all_to_all | solution.py:68
  254.9 3.5 %pad_maximum_fusion = bf16[256,8,1536]{2,0,1:T(8,128)(2,1)S(1)} fusion(bf16[256,2,1536]{2,0,1:T(8,128)(2,1)S(1)} %bitcast.91, bf16[256,2,1536]{2,0,1:T(8,128)(2,1)} %bitcast.90, bf16[256,2,1536]{2,0,1:T(8,128)(2,1)S(1)} %bitcast.88, bf16[256,2,1536]{2,0,1:T(8,128)(2,1)S(1)} %copy-done.5), kind=kLoop, calls=%fused_computation.10 | loop fusion | flops 9437184 | bytes 12582912 | tf_op jit(solution)/shard_map/concatenate | solution.py:84
  258.5 6.2 %copy.19 = bf16[256,8,1536]{2,1,0:T(8,128)(2,1)} copy(bf16[256,8,1536]{2,0,1:T(8,128)(2,1)S(1)} %pad_maximum_fusion) | data formatting | bytes 12582912
  264.7 4.6 %fusion.3 = f32[2,8]{1,0:T(2,128)S(1)} fusion(bf16[256,2,1536,1]{2,0,3,1:T(8,128)(2,1)S(1)} %bitcast.92, bf16[256,8,192,1]{0,2,1,3:T(8,128)(2,1)S(1)} %bitcast.96, f32[2]{0:T(128)S(1)} %get-tuple-element.33, f32[8]{0:T(128)S(1)} %gather_fusion, f32[1536,8,192]{0,2,1:T(8,128)S(1)} %bitcast.77), kind=kOutput, calls=%fused_computation.8 | convolution fusion | flops 2439512064 | bytes 11796584 | tf_op jit(solution)/shard_map/dot_general | solution.py:11
  (51 shorter events, 14.1 us)
Async XLA Ops:
  41.9 2.7 %copy-start.3 = (bf16[2048,1536]{1,0:T(8,128)(2,1)}, bf16[2048,1536]{1,0:T(8,128)(2,1)S(1)}, u32[]{:S(2)}) copy-start(bf16[2048,1536]{1,0:T(8,128)(2,1)S(1)} %convolution_convert_fusion) | copy-start | bytes 18874372
  59.2 9.3 %copy-start = (f32[128]{0:T(128)S(1)}, f32[128]{0:T(128)}, u32[]{:S(2)}) copy-start(f32[128]{0:T(128)} %param.8) | copy-start | bytes 1540
  59.2 9.3 %copy-start.10 = (s32[8]{0:T(128)S(1)}, s32[8]{0:T(128)}, u32[]{:S(2)}) copy-start(s32[8]{0:T(128)} %param.10) | copy-start | bytes 100
  61.8 14.3 %copy-start.9 = (f32[1536]{0:T(1024)S(1)}, f32[1536]{0:T(1024)}, u32[]{:S(2)}) copy-start(f32[1536]{0:T(1024)} %param.9) | copy-start | bytes 18436
  61.8 59.7 %all-to-all-start = ((bf16[16,48,1536]{2,0,1:T(8,128)(2,1)}), bf16[16,48,1536]{2,0,1:T(8,128)(2,1)S(1)}, u32[]{:S(2)}, u32[]{:S(2)}) async-start(bf16[16,48,1536]{2,0,1:T(8,128)(2,1)} %bitcast.79), calls=%async_computation | async-start | bytes 4718592 | tf_op jit(solution)/shard_map/all_to_all | solution.py:68
  121.6 1.4 copy-start.1
  124.3 7.5 %copy-start.2 = (bf16[16,16,3,1536]{3,1,0,2:T(8,128)(2,1)S(1)}, bf16[16,16,3,1536]{3,1,0,2:T(8,128)(2,1)}, u32[]{:S(2)}) copy-start(bf16[16,16,3,1536]{3,1,0,2:T(8,128)(2,1)} %copy-done.1) | copy-start | bytes 7077892
  124.3 41.3 %all-to-all-start.1 = ((bf16[16,32,1536]{2,0,1:T(8,128)(2,1)}), bf16[16,32,1536]{2,0,1:T(8,128)(2,1)}, u32[]{:S(2)}, u32[]{:S(2)}) async-start(bf16[16,32,1536]{2,0,1:T(8,128)(2,1)} %bitcast.86), calls=%async_computation.1 | async-start | bytes 3145728 | tf_op jit(solution)/shard_map/all_to_all | solution.py:68
  138.7 33.4 %copy-start.4 = (bf16[16,16,2,1536]{3,2,1,0:T(2,128)(2,1)S(1)}, bf16[16,16,2,1536]{3,2,1,0:T(2,128)(2,1)}, u32[]{:S(2)}) copy-start(bf16[16,16,2,1536]{3,2,1,0:T(2,128)(2,1)} %get-tuple-element.13) | copy-start | bytes 4718596
  167.1 41.2 %all-to-all-start.2 = ((bf16[16,32,1536]{2,0,1:T(8,128)(2,1)}), bf16[16,32,1536]{2,0,1:T(8,128)(2,1)}, u32[]{:S(2)}, u32[]{:S(2)}) async-start(bf16[16,32,1536]{2,0,1:T(8,128)(2,1)} %bitcast.85), calls=%async_computation.2 | async-start | bytes 3145728 | tf_op jit(solution)/shard_map/all_to_all | solution.py:68
  211.0 41.2 %all-to-all-start.3 = ((bf16[16,32,1536]{2,0,1:T(8,128)(2,1)}), bf16[16,32,1536]{2,0,1:T(8,128)(2,1)}, u32[]{:S(2)}, u32[]{:S(2)}) async-start(bf16[16,32,1536]{2,0,1:T(8,128)(2,1)} %bitcast.43), calls=%async_computation.3 | async-start | bytes 3145728 | tf_op jit(solution)/shard_map/all_to_all | solution.py:68
  215.9 39.0 %copy-start.5 = (bf16[256,2,1536]{2,0,1:T(8,128)(2,1)S(1)}, bf16[256,2,1536]{2,0,1:T(8,128)(2,1)}, u32[]{:S(2)}) copy-start(bf16[256,2,1536]{2,0,1:T(8,128)(2,1)} %slice.115) | copy-start | bytes 4718596
  253.7 1.2 copy-start.6
  254.9 9.7 %slice-start = ((s8[9437184]{0:T(1024)(128)(4,1)}), s8[4194304]{0:T(1024)(128)(4,1)S(1)}, s32[]{:S(2)}) async-start(s8[9437184]{0:T(1024)(128)(4,1)} %bitcast.76), calls=%async_computation.4 | async-start | bytes 8388608
  254.9 9.7 %slice-start.1 = ((s8[9437184]{0:T(1024)(128)(4,1)}), s8[4194304]{0:T(1024)(128)(4,1)S(1)}, s32[]{:S(2)}) async-start(s8[9437184]{0:T(1024)(128)(4,1)} %bitcast.76), calls=%async_computation.5 | async-start | bytes 8388608
  258.4 6.2 %slice-start.2 = ((s8[9437184]{0:T(1024)(128)(4,1)}), s8[1048576]{0:T(1024)(128)(4,1)S(1)}, s32[]{:S(2)}) async-start(s8[9437184]{0:T(1024)(128)(4,1)} %bitcast.76), calls=%async_computation.6 | async-start | bytes 2097152
  258.4 6.2 %copy-start.7 = (bf16[16,16,2,1536]{3,1,0,2:T(8,128)(2,1)S(1)}, bf16[16,16,2,1536]{3,1,0,2:T(8,128)(2,1)}, u32[]{:S(2)}) copy-start(bf16[16,16,2,1536]{3,1,0,2:T(8,128)(2,1)} %copy-done.6) | copy-start | bytes 4718596
  258.4 6.2 %copy-start.8 = (bf16[256,1,1536]{0,2,1:T(8,128)(2,1)S(1)}, bf16[256,1,1536]{0,2,1:T(8,128)(2,1)}, u32[]{:S(2)}) copy-start(bf16[256,1,1536]{0,2,1:T(8,128)(2,1)} %copy.15) | copy-start | bytes 2359300

commit v3 on v2

v3 whole, which is shorter than its diff:
```python
import jax
import jax.numpy as jnp
from jax import lax
from jax.sharding import PartitionSpec as P

VBLK = 192
CHUNKS = 4


def chunk_energies(factors, blocks, occ_rows, occ_cols, vir_chunk, vir_blocks, scale):
    coulomb = lax.dot_general(
        factors, blocks, (((0,), (0,)), ((), ())), preferred_element_type=jnp.float32
    )
    denom = (
        vir_chunk[None, :, None, None]
        + vir_blocks[None, None, :, :]
        - occ_rows[:, None, None, None]
        - occ_cols[None, None, :, None]
    )
    return jnp.sum(coulomb * coulomb / denom, axis=(1, 3))


def per_device(integrals, orbitals, occ_energy, vir_energy, owner, vblock):
    aux_here, occ_total, basis_count = integrals.shape
    nvir = orbitals.shape[1]
    step_count = owner.shape[0]
    groups = lax.psum(1, "occ")
    local_count = occ_total // groups
    chunks = CHUNKS
    while nvir % (chunks * 128):
        chunks -= 1
    span = nvir // chunks
    ride = step_count == local_count
    rows = integrals.reshape(aux_here, groups, local_count, basis_count)
    rows = jnp.transpose(rows, (1, 0, 2, 3))

    picked = jnp.take(integrals, owner, axis=1)
    picked = jnp.dot(
        picked.reshape(aux_here * step_count, basis_count), orbitals,
        preferred_element_type=jnp.float32,
    ).astype(jnp.bfloat16).reshape(aux_here, step_count, nvir)
    pieces = jnp.stack(
        [lax.dynamic_slice_in_dim(picked[:, s, :], vblock[s] * VBLK, VBLK, axis=1) for s in range(step_count)],
        axis=1,
    )

    me = lax.axis_index("occ")
    occ_here = lax.dynamic_slice(occ_energy, (me * local_count,), (local_count,))
    occ_cols = occ_energy[owner]
    vir_blocks = jnp.stack(
        [lax.dynamic_slice(vir_energy, (vblock[s] * VBLK,), (VBLK,)) for s in range(step_count)]
    )
    scale = 1.0 / (aux_here * groups * nvir * VBLK)

    if not ride:
        blocks = lax.all_gather(pieces, "occ", axis=0, tiled=True)
    parts = []
    sums = []
    factors = jnp.zeros((groups * aux_here, local_count, nvir), jnp.bfloat16)
    for c in range(chunks):
        cols = slice(c * span, (c + 1) * span)
        product = lax.dot_general(
            rows, orbitals[:, cols], (((3,), (0,)), ((), ())),
            preferred_element_type=jnp.float32,
        ).astype(jnp.bfloat16)
        if c == 0 and ride:
            extra = jnp.broadcast_to(pieces[None], (groups, aux_here, step_count, VBLK))
            product = jnp.concatenate([product, extra], axis=3)
        if c >= 1:
            held = (parts[-1],) + tuple(sums[-2:-1])
            product, _ = lax.optimization_barrier((product, held))
        got = lax.all_to_all(product, "occ", split_axis=0, concat_axis=0, tiled=True)
        got = got.reshape(groups * aux_here, local_count, got.shape[-1])
        if c == 0 and ride:
            blocks = got[:, :, span:]
            got = got[:, :, :span]
        parts.append(got)
        factors = lax.dynamic_update_slice(factors, got, (0, 0, c * span))
        sums.append(
            chunk_energies(lax.optimization_barrier(got), blocks, occ_here, occ_cols, vir_energy[cols], vir_blocks, scale)
        )
    total = sums[0]
    for extra_sum in sums[1:]:
        total = total + extra_sum
    energies = -total * scale
    return (factors, energies)


def solution(mesh):
    placed = (P(("mol", "occ"), None, None), P("mol", None), P("mol"), P("mol"), P("mol"), P("mol"))
    return jax.shard_map(
        per_device,
        mesh=mesh,
        in_specs=placed,
        out_specs=(P("mol", "occ", None), P(("mol", "occ"), None)),
        check_vma=False,
    )
```

time: 271 us -> 226 us (0.83)
  local copies, waits for them, and re-layouts: 49.6 us -> 19.2 us
  matrix products: 43 us -> 63.8 us
  waiting for transfers between devices: 124 us -> 106 us
  between operations: 21.5 us -> 5.95 us
    slice x10 -> x5, local copies, waits for them, and re-layouts: 29.8 us -> 4.73 us  [the longest x1 1.64 us: per_device(): vblock[s] * VBLK]
    dot_general x1 -> x5, matrix products: 17.3 us -> 39.3 us  [the longest x4 38.2 us: per_device(): lax.dot_general(rows, orbitals[:, cols], (((3,), (0,)), ((), ())), prefer...]
    all_to_all x4, waiting for transfers between devices: 124 us -> 106 us  [per_device(): lax.all_to_all(product, 'occ', split_axis=0, concat_axis=0, tiled=True)]
    unnamed x30 -> x19, local copies, waits for them, and re-layouts: 12.4 us -> 4.68 us
    all_to_all x4 -> x0, local copies, waits for them, and re-layouts: 5.87 us -> none  [per_device(): lax.all_to_all(payload, 'occ', split_axis=1, concat_axis=0, tiled=True)]
    dynamic_update_slice x0 -> x4, local copies, waits for them, and re-layouts: none -> 5.36 us  [per_device(): factors = lax.dynamic_update_slice(factors, got, (0, 0, c * span))]
    concatenate x3 -> x1, other arithmetic: 5.69 us -> 3.26 us  [per_device(): product = jnp.concatenate([product, extra], axis=3)]
  transfers between devices with their start and end apart: 4 -> 4, of which waited for: 4 -> 4; matrix products, arithmetic and copies ran while one was open for 14% -> 26% of each run, Pallas kernels for 0% -> 0%
where the time goes in v3:
time: 226 us; the launch traced here: 225 us
  waiting for transfers between devices  106 us (47%)
  matrix products  63.8 us (28%)
  starting transfers between devices  21.3 us (9%)
  local copies, waits for them, and re-layouts  19.2 us (8%)
  other arithmetic  9.57 us (4%)
  between operations  5.95 us (3%)
    all_to_all x4, waiting for transfers between devices, per_device(): lax.all_to_all(product, 'occ', split_axis=0, concat_axis=0, tiled=True)  106 us
    dot_general x4, matrix products, per_device(): lax.dot_general(rows, orbitals[:, cols], (((3,), (0,)), ((), ())), prefer...  38.2 us
    dot_general x4, matrix products, chunk_energies(): lax.dot_general(factors, blocks, (((0,), (0,)), ((), ())), preferred_elem...  24.6 us
    all_to_all x4, starting transfers between devices, per_device(): lax.all_to_all(product, 'occ', split_axis=0, concat_axis=0, tiled=True)  21.3 us
    dynamic_update_slice x4, local copies, waits for them, and re-layouts, per_device(): factors = lax.dynamic_update_slice(factors, got, (0, 0, c * span))  5.36 us
    unnamed x19, local copies, waits for them, and re-layouts  4.68 us
  transfers between devices with their start and end apart: 4, of which 4 were waited for; matrix products, arithmetic and copies ran while one was open for 26% of the time, Pallas kernels for 0%

profile of v3, /device:TPU:13, one launch (start us, length us, event | category | flops | bytes accessed | tf_op | source)
XLA Modules:
  0.0 225.4 jit_solution(5739785476335957690)
XLA Ops:
  0.6 1.6 fusion.51
  8.8 2.7 %gather_fusion = bf16[8,16,2048]{2,0,1:T(8,128)(2,1)S(1)} fusion(bf16[16,128,2048]{2,1,0:T(8,128)(2,1)} %param.6, s32[1024]{0:T(1024)S(1)} %pad_clamp_fusion), kind=kCustom, calls=%fused_computation | custom fusion | bytes 1048608 | tf_op jit(solution)/shard_map/jit(_take)/gather | solution.py:37
  11.5 9.6 %fusion.17 = bf16[16,16,8,384]{3,2,1,0:T(8,128)(2,1)} fusion(bf16[2048,1536]{1,0:T(8,128)(2,1)} %param.7, bf16[16,128,2048]{2,1,0:T(8,128)(2,1)} %param.6), kind=kOutput, calls=%fused_computation.25 | convolution fusion | flops 3222011904 | bytes 11534336 | tf_op jit(solution)/shard_map/dot_general | solution.py:62
  23.7 3.3 %pad_maximum_fusion = bf16[16,16,8,576]{3,2,1,0:T(8,128)(2,1)} fusion(bf16[16,16,8,192]{3,2,1,0:T(8,128)(2,1)S(1)} %broadcast_in_dim.23, bf16[16,16,8,384]{3,2,1,0:T(8,128)(2,1)} %fusion.17), kind=kLoop, calls=%fused_computation.22 | loop fusion | flops 4718592 | bytes 4718592 | tf_op jit(solution)/shard_map/concatenate | solution.py:68
  27.0 6.6 %all-to-all-start = ((bf16[16,16,8,576]{3,2,1,0:T(8,128)(2,1)}), bf16[16,16,8,576]{3,2,1,0:T(8,128)(2,1)S(1)}, u32[]{:S(2)}, u32[]{:S(2)}) async-start(bf16[16,16,8,576]{3,2,1,0:T(8,128)(2,1)} %pad_maximum_fusion), calls=%async_computation | async-start | bytes 5242880 | tf_op jit(solution)/shard_map/all_to_all | solution.py:72
  33.6 9.5 %fusion.20 = bf16[16,16,8,384]{3,2,1,0:T(8,128)(2,1)} fusion(bf16[2048,1536]{1,0:T(8,128)(2,1)} %param.7, bf16[16,128,2048]{2,1,0:T(8,128)(2,1)} %param.6), kind=kOutput, calls=%fused_computation.26 | convolution fusion | flops 3222011904 | bytes 11534336 | tf_op jit(solution)/shard_map/dot_general | solution.py:62
  43.1 9.4 %fusion.23 = bf16[16,16,8,384]{3,2,1,0:T(8,128)(2,1)} fusion(bf16[2048,1536]{1,0:T(8,128)(2,1)} %param.7, bf16[16,128,2048]{2,1,0:T(8,128)(2,1)} %param.6), kind=kOutput, calls=%fused_computation.27 | convolution fusion | flops 3222011904 | bytes 11534336 | tf_op jit(solution)/shard_map/dot_general | solution.py:62
  52.5 39.7 %all-to-all-done = bf16[16,16,8,576]{3,2,1,0:T(8,128)(2,1)S(1)} async-done(((bf16[16,16,8,576]{3,2,1,0:T(8,128)(2,1)}), bf16[16,16,8,576]{3,2,1,0:T(8,128)(2,1)S(1)}, u32[]{:S(2)}, u32[]{:S(2)}) %all-to-all-start) | async-done | bytes 2359328 | tf_op jit(solution)/shard_map/all_to_all | solution.py:72
  93.5 4.9 %all-to-all-start.1 = ((bf16[16,16,8,384]{3,2,1,0:T(8,128)(2,1)}), bf16[16,16,8,384]{3,2,1,0:T(8,128)(2,1)}, u32[]{:S(2)}, u32[]{:S(2)}) async-start(bf16[16,16,8,384]{3,2,1,0:T(8,128)(2,1)} %fusion.20), calls=%async_computation.1 | async-start | bytes 3145728 | tf_op jit(solution)/shard_map/all_to_all | solution.py:72
  99.3 4.4 %broadcast_add_fusion.1 = (f32[384,8,192]{0,2,1:T(8,128)}, f32[384,8,192]{0,2,1:T(8,128)}, f32[384,8,192]{0,2,1:T(8,128)}, f32[384,8,192]{0,2,1:T(8,128)}) fusion(f32[384]{0:T(512)S(1)} %get-tuple-element.20, f32[8,192]{1,0:T(8,128)S(1)} %stack.47, f32[384]{0:T(512)S(1)} %get-tuple-element.21, f32[384]{0:T(512)S(1)} %get-tuple-element.23, ...), kind=kLoop, calls=%fused_computation.42 | loop fusion | flops 2359296 | bytes 9449472 | tf_op jit(solution)/shard_map/add | solution.py:15
  104.7 1.9 copy.36
  106.7 6.8 %fusion = f32[8,8]{1,0:T(8,128)S(1)} fusion(f32[8]{0:T(128)S(1)} %gather_fusion.1, f32[8]{0:T(128)S(1)} %dynamic_slice.67, f32[384,8,192]{0,2,1:T(8,128)} %get-tuple-element.19, bf16[256,8,384,1]{2,1,0,3:T(8,128)(2,1)} %bitcast.99, bf16[256,8,192]{0,2,1:T(8,128)(2,1)S(1)} %copy.36), kind=kOutput, calls=%fused_computation.6 | convolution fusion | flops 2439512064 | bytes 4718912 | tf_op jit(solution)/shard_map/dot_general | solution.py:11
  113.5 21.3 %all-to-all-done.1 = bf16[16,16,8,384]{3,2,1,0:T(8,128)(2,1)} async-done(((bf16[16,16,8,384]{3,2,1,0:T(8,128)(2,1)}), bf16[16,16,8,384]{3,2,1,0:T(8,128)(2,1)}, u32[]{:S(2)}, u32[]{:S(2)}) %all-to-all-start.1) | async-done | bytes 1572896 | tf_op jit(solution)/shard_map/all_to_all | solution.py:72
  134.7 4.9 %all-to-all-start.2 = ((bf16[16,16,8,384]{3,2,1,0:T(8,128)(2,1)}), bf16[16,16,8,384]{3,2,1,0:T(8,128)(2,1)S(1)}, u32[]{:S(2)}, u32[]{:S(2)}) async-start(bf16[16,16,8,384]{3,2,1,0:T(8,128)(2,1)} %fusion.23), calls=%async_computation.2 | async-start | bytes 3145728 | tf_op jit(solution)/shard_map/all_to_all | solution.py:72
  139.7 9.6 %fusion.26 = bf16[16,16,8,384]{3,2,1,0:T(8,128)(2,1)} fusion(bf16[2048,1536]{1,0:T(8,128)(2,1)} %param.7, bf16[16,128,2048]{2,1,0:T(8,128)(2,1)} %param.6), kind=kOutput, calls=%fused_computation.28 | convolution fusion | flops 3222011904 | bytes 11534336 | tf_op jit(solution)/shard_map/dot_general | solution.py:62
  149.3 6.3 %fusion.1 = f32[8,8]{1,0:T(8,128)S(1)} fusion(f32[384,8,192]{0,2,1:T(8,128)S(1)} %copy-done.3, f32[8]{0:T(128)S(1)} %gather_fusion.1, f32[8]{0:T(128)S(1)} %dynamic_slice.67, bf16[256,8,384,1]{2,1,0,3:T(8,128)(2,1)} %bitcast.34, bf16[256,8,192]{0,2,1:T(8,128)(2,1)S(1)} %copy.36), kind=kOutput, calls=%fused_computation.7 | convolution fusion | flops 2439512064 | bytes 4718912 | tf_op jit(solution)/shard_map/dot_general | solution.py:11
  155.6 20.2 %all-to-all-done.2 = bf16[16,16,8,384]{3,2,1,0:T(8,128)(2,1)S(1)} async-done(((bf16[16,16,8,384]{3,2,1,0:T(8,128)(2,1)}), bf16[16,16,8,384]{3,2,1,0:T(8,128)(2,1)S(1)}, u32[]{:S(2)}, u32[]{:S(2)}) %all-to-all-start.2) | async-done | bytes 1572896 | tf_op jit(solution)/shard_map/all_to_all | solution.py:72
  175.8 4.9 %all-to-all-start.3 = ((bf16[16,16,8,384]{3,2,1,0:T(8,128)(2,1)}), bf16[16,16,8,384]{3,2,1,0:T(8,128)(2,1)S(1)}, u32[]{:S(2)}, u32[]{:S(2)}) async-start(bf16[16,16,8,384]{3,2,1,0:T(8,128)(2,1)} %fusion.26), calls=%async_computation.3 | async-start | bytes 3145728 | tf_op jit(solution)/shard_map/all_to_all | solution.py:72
  180.8 2.0 dynamic_update_slice.12
  182.8 1.7 constant_dynamic-update-slice_fusion.2
  184.9 2.7 %copy-done.1 = bf16[256,8,1536]{2,1,0:T(8,128)(2,1)} copy-done((bf16[256,8,1536]{2,1,0:T(8,128)(2,1)}, bf16[256,8,1536]{2,1,0:T(8,128)(2,1)S(1)}, u32[]{:S(2)}) %copy-start.1) | copy-done | bytes 6291480
  187.6 4.9 %fusion.2 = f32[8,8]{1,0:T(8,128)S(1)} fusion(f32[384,8,192]{0,2,1:T(8,128)S(1)} %copy-done.2, f32[8]{0:T(128)S(1)} %gather_fusion.1, f32[8]{0:T(128)S(1)} %dynamic_slice.67, bf16[256,8,384,1]{2,1,0,3:T(8,128)(2,1)S(1)} %bitcast.98, bf16[256,8,192]{0,2,1:T(8,128)(2,1)S(1)} %copy-done.5), kind=kOutput, calls=%fused_computation.8 | convolution fusion | flops 2439512064 | bytes 4718912 | tf_op jit(solution)/shard_map/dot_general | solution.py:11
  192.5 24.4 %all-to-all-done.3 = bf16[16,16,8,384]{3,2,1,0:T(8,128)(2,1)S(1)} async-done(((bf16[16,16,8,384]{3,2,1,0:T(8,128)(2,1)}), bf16[16,16,8,384]{3,2,1,0:T(8,128)(2,1)S(1)}, u32[]{:S(2)}, u32[]{:S(2)}) %all-to-all-start.3) | async-done | bytes 1572896 | tf_op jit(solution)/shard_map/all_to_all | solution.py:72
  218.2 6.6 %fusion.3 = f32[8,8]{1,0:T(8,128)S(1)} fusion(f32[384,8,192]{0,2,1:T(8,128)} %get-tuple-element.18, f32[8]{0:T(128)S(1)} %gather_fusion.1, f32[8]{0:T(128)S(1)} %dynamic_slice.67, bf16[256,8,384,1]{2,1,0,3:T(8,128)(2,1)S(1)} %bitcast.96, bf16[256,8,192]{0,2,1:T(8,128)(2,1)} %copy-done.4), kind=kOutput, calls=%fused_computation.9 | convolution fusion | flops 2439512064 | bytes 4718912 | tf_op jit(solution)/shard_map/dot_general | solution.py:11
  (41 shorter events, 9.4 us)
Async XLA Ops:
  8.8 12.3 %slice-start = ((s8[6291456]{0:T(1024)(128)(4,1)}), s8[2097152]{0:T(1024)(128)(4,1)S(1)}, s32[]{:S(2)}) async-start(s8[6291456]{0:T(1024)(128)(4,1)} %bitcast.93), calls=%async_computation.4 | async-start | bytes 4194304
  11.5 9.6 %slice-start.1 = ((s8[6291456]{0:T(1024)(128)(4,1)}), s8[4194304]{0:T(1024)(128)(4,1)S(1)}, s32[]{:S(2)}) async-start(s8[6291456]{0:T(1024)(128)(4,1)} %bitcast.93), calls=%async_computation.5 | async-start | bytes 8388608
  22.9 10.7 %copy-start.6 = (f32[1536]{0:T(1024)S(1)}, f32[1536]{0:T(1024)}, u32[]{:S(2)}) copy-start(f32[1536]{0:T(1024)} %param.9) | copy-start | bytes 18436
  27.0 65.2 %all-to-all-start = ((bf16[16,16,8,576]{3,2,1,0:T(8,128)(2,1)}), bf16[16,16,8,576]{3,2,1,0:T(8,128)(2,1)S(1)}, u32[]{:S(2)}, u32[]{:S(2)}) async-start(bf16[16,16,8,576]{3,2,1,0:T(8,128)(2,1)} %pad_maximum_fusion), calls=%async_computation | async-start | bytes 5242880 | tf_op jit(solution)/shard_map/all_to_all | solution.py:72
  52.5 46.0 %copy-start = (f32[128]{0:T(128)S(1)}, f32[128]{0:T(128)}, u32[]{:S(2)}) copy-start(f32[128]{0:T(128)} %param.8) | copy-start | bytes 1540
  93.5 41.2 %all-to-all-start.1 = ((bf16[16,16,8,384]{3,2,1,0:T(8,128)(2,1)}), bf16[16,16,8,384]{3,2,1,0:T(8,128)(2,1)}, u32[]{:S(2)}, u32[]{:S(2)}) async-start(bf16[16,16,8,384]{3,2,1,0:T(8,128)(2,1)} %fusion.20), calls=%async_computation.1 | async-start | bytes 3145728 | tf_op jit(solution)/shard_map/all_to_all | solution.py:72
  106.7 42.6 %copy-start.4 = (bf16[256,8,192]{0,2,1:T(8,128)(2,1)}, bf16[256,8,192]{0,2,1:T(8,128)(2,1)S(1)}, u32[]{:S(2)}) copy-start(bf16[256,8,192]{0,2,1:T(8,128)(2,1)S(1)} %copy.36) | copy-start | bytes 2359300
  134.7 41.1 %all-to-all-start.2 = ((bf16[16,16,8,384]{3,2,1,0:T(8,128)(2,1)}), bf16[16,16,8,384]{3,2,1,0:T(8,128)(2,1)S(1)}, u32[]{:S(2)}, u32[]{:S(2)}) async-start(bf16[16,16,8,384]{3,2,1,0:T(8,128)(2,1)} %fusion.23), calls=%async_computation.2 | async-start | bytes 3145728 | tf_op jit(solution)/shard_map/all_to_all | solution.py:72
  139.6 9.7 %copy-start.3 = (f32[384,8,192]{0,2,1:T(8,128)S(1)}, f32[384,8,192]{0,2,1:T(8,128)}, u32[]{:S(2)}) copy-start(f32[384,8,192]{0,2,1:T(8,128)} %get-tuple-element.17) | copy-start | bytes 7077892
  175.8 41.1 %all-to-all-start.3 = ((bf16[16,16,8,384]{3,2,1,0:T(8,128)(2,1)}), bf16[16,16,8,384]{3,2,1,0:T(8,128)(2,1)S(1)}, u32[]{:S(2)}, u32[]{:S(2)}) async-start(bf16[16,16,8,384]{3,2,1,0:T(8,128)(2,1)} %fusion.26), calls=%async_computation.3 | async-start | bytes 3145728 | tf_op jit(solution)/shard_map/all_to_all | solution.py:72
  180.7 6.8 %copy-start.2 = (f32[384,8,192]{0,2,1:T(8,128)S(1)}, f32[384,8,192]{0,2,1:T(8,128)}, u32[]{:S(2)}) copy-start(f32[384,8,192]{0,2,1:T(8,128)} %get-tuple-element.16) | copy-start | bytes 7077892
  180.7 6.8 %copy-start.5 = (bf16[256,8,192]{0,2,1:T(8,128)(2,1)S(1)}, bf16[256,8,192]{0,2,1:T(8,128)(2,1)}, u32[]{:S(2)}) copy-start(bf16[256,8,192]{0,2,1:T(8,128)(2,1)} %copy-done.4) | copy-start | bytes 2359300
  184.8 2.7 %copy-start.1 = (bf16[256,8,1536]{2,1,0:T(8,128)(2,1)}, bf16[256,8,1536]{2,1,0:T(8,128)(2,1)S(1)}, u32[]{:S(2)}) copy-start(bf16[256,8,1536]{2,1,0:T(8,128)(2,1)S(1)} %constant_dynamic-update-slice_fusion.1) | copy-start | bytes 18874372

commit v4 on v3

--- a/solution.py
+++ b/solution.py
@@ -4,7 +4,7 @@
 from jax.sharding import PartitionSpec as P
 
 VBLK = 192
-CHUNKS = 4
+TAIL_PART = 4
 
 
 def chunk_energies(factors, blocks, occ_rows, occ_cols, vir_chunk, vir_blocks, scale):
@@ -26,10 +26,12 @@
     step_count = owner.shape[0]
     groups = lax.psum(1, "occ")
     local_count = occ_total // groups
-    chunks = CHUNKS
-    while nvir % (chunks * 128):
-        chunks -= 1
-    span = nvir // chunks
+    if nvir % 128 == 0 and nvir >= 256:
+        tail = max(1, (nvir // 128) // TAIL_PART) * 128
+        bounds = [0, nvir - tail, nvir]
+    else:
+        bounds = [0, nvir]
+    chunks = len(bounds) - 1
     ride = step_count == local_count
     rows = integrals.reshape(aux_here, groups, local_count, basis_count)
     rows = jnp.transpose(rows, (1, 0, 2, 3))
@@ -56,9 +58,9 @@
         blocks = lax.all_gather(pieces, "occ", axis=0, tiled=True)
     parts = []
     sums = []
-    factors = jnp.zeros((groups * aux_here, local_count, nvir), jnp.bfloat16)
     for c in range(chunks):
-        cols = slice(c * span, (c + 1) * span)
+        cols = slice(bounds[c], bounds[c + 1])
+        span = bounds[c + 1] - bounds[c]
         product = lax.dot_general(
             rows, orbitals[:, cols], (((3,), (0,)), ((), ())),
             preferred_element_type=jnp.float32,
@@ -75,10 +77,18 @@
             blocks = got[:, :, span:]
             got = got[:, :, :span]
         parts.append(got)
-        factors = lax.dynamic_update_slice(factors, got, (0, 0, c * span))
+        if c == 0:
+            factors = jnp.pad(got, ((0, 0), (0, 0), (0, nvir - span)))
+        else:
+            factors = lax.dynamic_update_slice(factors, got, (0, 0, bounds[c]))
         sums.append(
-            chunk_energies(lax.optimization_barrier(got), blocks, occ_here, occ_cols, vir_energy[cols], vir_blocks, scale)
+            chunk_energies(
+                lax.optimization_barrier(got), blocks, occ_here, occ_cols,
+                vir_energy[cols], vir_blocks, scale,
+            )
         )
+        if c == 0:
+            factors, sums[0] = lax.optimization_barrier((factors, sums[0]))
     total = sums[0]
     for extra_sum in sums[1:]:
         total = total + extra_sum

time: 226 us -> 225 us (level)
  waiting for transfers between devices: 106 us -> 127 us
  matrix products: 63.8 us -> 48.4 us
  starting transfers between devices: 21.3 us -> 11.7 us
  other arithmetic: 9.57 us -> 12.5 us
    all_to_all x4 -> x2, waiting for transfers between devices: 106 us -> 127 us  [per_device(): lax.all_to_all(product, 'occ', split_axis=0, concat_axis=0, tiled=True)]
    dot_general x4 -> x2, matrix products: 38.2 us -> 25.8 us  [per_device(): lax.dot_general(rows, orbitals[:, cols], (((3,), (0,)), ((), ())), prefer...]
    all_to_all x4 -> x2, starting transfers between devices: 21.3 us -> 11.7 us  [per_device(): lax.all_to_all(product, 'occ', split_axis=0, concat_axis=0, tiled=True)]
    dynamic_update_slice x4 -> x1, local copies, waits for them, and re-layouts: 5.36 us -> 1.3 us  [per_device(): factors = lax.dynamic_update_slice(factors, got, (0, 0, bounds[c]))]
    slice x1, local copies, waits for them, and re-layouts: 1.35 us -> 4.88 us  [per_device(): got = got[:, :, :span]]
    pad x0 -> x1, local copies, waits for them, and re-layouts: none -> 3.19 us  [per_device(): factors = jnp.pad(got, ((0, 0), (0, 0), (0, nvir - span)))]
    unnamed x19 -> x15, local copies, waits for them, and re-layouts: 4.68 us -> 1.69 us
    dot_general x4 -> x2, matrix products: 24.6 us -> 21.6 us  [chunk_energies(): lax.dot_general(factors, blocks, (((0,), (0,)), ((), ())), preferred_elem...]
  transfers between devices with their start and end apart: 4 -> 2, of which waited for: 4 -> 2; matrix products, arithmetic and copies ran while one was open for 26% -> 16% of each run, Pallas kernels for 0% -> 0%
where the time goes in v4:
time: 225 us
  waiting for transfers between devices  127 us (56%)
  matrix products  48.4 us (22%)
  local copies, waits for them, and re-layouts  19.1 us (8%)
  other arithmetic  12.5 us (6%)
  starting transfers between devices  11.7 us (5%)
  between operations  5.93 us (3%)
    all_to_all x2, waiting for transfers between devices, per_device(): lax.all_to_all(product, 'occ', split_axis=0, concat_axis=0, tiled=True)  127 us
    dot_general x2, matrix products, per_device(): lax.dot_general(rows, orbitals[:, cols], (((3,), (0,)), ((), ())), prefer...  25.8 us
    dot_general x2, matrix products, chunk_energies(): lax.dot_general(factors, blocks, (((0,), (0,)), ((), ())), preferred_elem...  21.6 us
    all_to_all x2, starting transfers between devices, per_device(): lax.all_to_all(product, 'occ', split_axis=0, concat_axis=0, tiled=True)  11.7 us
    concatenate x1, other arithmetic, per_device(): product = jnp.concatenate([product, extra], axis=3)  5.53 us
    add x2, other arithmetic, chunk_energies(): vir_chunk[None, :, None, None] + vir_blocks[None, None, :, :]  5.08 us
    slice x1, local copies, waits for them, and re-layouts, per_device(): got = got[:, :, :span]  4.88 us
  transfers between devices with their start and end apart: 2, of which 2 were waited for; matrix products, arithmetic and copies ran while one was open for 16% of the time, Pallas kernels for 0%

profile of v4, /device:TPU:13, one launch (start us, length us, event | category | flops | bytes accessed | tf_op | source)
XLA Modules:
  0.0 224.5 jit_solution(12597923455849016050)
XLA Ops:
  0.6 1.6 fusion.28
  3.6 0.7 compare_select_fusion
  4.2 0.7 compare_and_fusion
  8.8 2.7 %gather_fusion = bf16[8,16,2048]{2,0,1:T(8,128)(2,1)S(1)} fusion(bf16[16,128,2048]{2,1,0:T(8,128)(2,1)} %param.6, s32[1024]{0:T(1024)S(1)} %pad_clamp_fusion), kind=kCustom, calls=%fused_computation | custom fusion | bytes 1048608 | tf_op jit(solution)/shard_map/jit(_take)/gather | solution.py:39
  11.5 16.3 %fusion.8 = bf16[16,16,8,1152]{3,2,1,0:T(8,128)(2,1)} fusion(bf16[2048,1536]{1,0:T(8,128)(2,1)} %param.7, bf16[16,128,2048]{2,1,0:T(8,128)(2,1)} %param.6), kind=kOutput, calls=%fused_computation.13 | convolution fusion | flops 9666035712 | bytes 17825792 | tf_op jit(solution)/shard_map/dot_general | solution.py:64
  27.8 1.1 fusion.14
  28.9 0.7 fusion.26
  30.4 5.5 %pad_maximum_fusion = bf16[16,16,8,1344]{3,2,1,0:T(8,128)(2,1)} fusion(bf16[16,16,8,192]{3,2,1,0:T(8,128)(2,1)S(1)} %broadcast_in_dim.36, bf16[16,16,8,1152]{3,2,1,0:T(8,128)(2,1)} %fusion.8), kind=kLoop, calls=%fused_computation.12 | loop fusion | flops 11010048 | bytes 11010048 | tf_op jit(solution)/shard_map/concatenate | solution.py:70
  36.0 6.7 %all-to-all-start = ((bf16[16,16,8,1344]{3,2,1,0:T(8,128)(2,1)}), bf16[16,16,8,1344]{3,2,1,0:T(8,128)(2,1)}, u32[]{:S(2)}, u32[]{:S(2)}) async-start(bf16[16,16,8,1344]{3,2,1,0:T(8,128)(2,1)} %pad_maximum_fusion), calls=%async_computation | async-start | bytes 11534336 | tf_op jit(solution)/shard_map/all_to_all | solution.py:74
  42.7 0.6 gather_fusion.1
  43.6 1.7 broadcast_add_fusion.1
  45.2 3.4 %broadcast_add_fusion = f32[1152,8,192]{0,2,1:T(8,128)} fusion(f32[8,192]{1,0:T(8,128)S(1)} %stack.47, f32[1152]{0:T(1024)S(1)} %bitcast.67), kind=kLoop, calls=%fused_computation.17 | loop fusion | flops 1769472 | bytes 7088640 | tf_op jit(solution)/shard_map/add | solution.py:15
  48.6 9.4 %fusion.15 = bf16[16,16,8,384]{3,2,1,0:T(8,128)(2,1)} fusion(bf16[2048,1536]{1,0:T(8,128)(2,1)} %param.7, bf16[16,128,2048]{2,1,0:T(8,128)(2,1)} %param.6), kind=kOutput, calls=%fused_computation.20 | convolution fusion | flops 3222011904 | bytes 11534336 | tf_op jit(solution)/shard_map/dot_general | solution.py:64
  58.1 110.8 %all-to-all-done = bf16[16,16,8,1344]{3,2,1,0:T(8,128)(2,1)} async-done(((bf16[16,16,8,1344]{3,2,1,0:T(8,128)(2,1)}), bf16[16,16,8,1344]{3,2,1,0:T(8,128)(2,1)}, u32[]{:S(2)}, u32[]{:S(2)}) %all-to-all-start) | async-done | bytes 5505056 | tf_op jit(solution)/shard_map/all_to_all | solution.py:74
  168.8 4.9 %slice.108 = bf16[256,8,1152]{2,1,0:T(8,128)(2,1)} slice(bf16[256,8,1344]{2,1,0:T(8,128)(2,1)} %bitcast.15), slice={[0:256], [0:8], [0:1152]} | slice | bytes 9437184 | tf_op jit(solution)/shard_map/slice | solution.py:78
  173.7 1.3 slice.109
  175.0 5.1 %all-to-all-start.1 = ((bf16[16,16,8,384]{3,2,1,0:T(8,128)(2,1)}), bf16[16,16,8,384]{3,2,1,0:T(8,128)(2,1)S(1)}, u32[]{:S(2)}, u32[]{:S(2)}) async-start(bf16[16,16,8,384]{3,2,1,0:T(8,128)(2,1)} %fusion.15), calls=%async_computation.1 | async-start | bytes 3145728 | tf_op jit(solution)/shard_map/all_to_all | solution.py:74
  180.1 1.7 copy.24
  181.7 15.3 %fusion = f32[8,8]{1,0:T(8,128)S(1)} fusion(f32[8]{0:T(128)S(1)} %gather_fusion.1, f32[8]{0:T(128)S(1)} %dynamic_slice.67, f32[1152,8,192]{0,2,1:T(8,128)} %broadcast_add_fusion, bf16[256,8,1152,1]{2,1,0,3:T(8,128)(2,1)} %bitcast.60, bf16[256,8,192]{0,2,1:T(8,128)(2,1)} %copy.24), kind=kOutput, calls=%fused_computation.3 | convolution fusion | flops 7318536192 | bytes 12583232 | tf_op jit(solution)/shard_map/dot_general | solution.py:11
  197.0 3.2 %pad.4 = bf16[256,8,1536]{2,1,0:T(8,128)(2,1)} pad(bf16[256,8,1152]{2,1,0:T(8,128)(2,1)S(1)} %bitcast.62, bf16[]{:T(256)} %constant.48.clone.1), padding=0_0x0_0x0_384 | pad | bytes 11010050 | tf_op jit(solution)/shard_map/jit(_pad)/pad | solution.py:81
  200.2 16.0 %all-to-all-done.1 = bf16[16,16,8,384]{3,2,1,0:T(8,128)(2,1)S(1)} async-done(((bf16[16,16,8,384]{3,2,1,0:T(8,128)(2,1)}), bf16[16,16,8,384]{3,2,1,0:T(8,128)(2,1)S(1)}, u32[]{:S(2)}, u32[]{:S(2)}) %all-to-all-start.1) | async-done | bytes 1572896 | tf_op jit(solution)/shard_map/all_to_all | solution.py:74
  216.3 1.3 constant_dynamic-update-slice_fusion
  217.6 6.3 %fusion.1 = f32[8,8]{1,0:T(8,128)S(1)} fusion(f32[8]{0:T(128)S(1)} %gather_fusion.1, f32[8]{0:T(128)S(1)} %dynamic_slice.67, f32[384,8,192]{0,2,1:T(8,128)} %broadcast_add_fusion.1, bf16[256,8,384,1]{2,1,0,3:T(8,128)(2,1)S(1)} %bitcast.66, bf16[256,8,192]{0,2,1:T(8,128)(2,1)S(1)} %copy-done.1), kind=kOutput, calls=%fused_computation.5 | convolution fusion | flops 2439512064 | bytes 4718912 | tf_op jit(solution)/shard_map/dot_general | solution.py:11
  223.9 0.6 negate_multiply_fusion
  (29 shorter events, 1.1 us)
Async XLA Ops:
  8.8 19.0 %slice-start.2 = ((s8[6291456]{0:T(1024)(128)(4,1)}), s8[2097152]{0:T(1024)(128)(4,1)S(1)}, s32[]{:S(2)}) async-start(s8[6291456]{0:T(1024)(128)(4,1)} %bitcast.63), calls=%async_computation.4 | async-start | bytes 4194304
  11.5 16.3 %slice-start.3 = ((s8[6291456]{0:T(1024)(128)(4,1)}), s8[4194304]{0:T(1024)(128)(4,1)S(1)}, s32[]{:S(2)}) async-start(s8[6291456]{0:T(1024)(128)(4,1)} %bitcast.63), calls=%async_computation.5 | async-start | bytes 8388608
  36.0 6.7 %copy-start.2 = (f32[1536]{0:T(1024)S(1)}, f32[1536]{0:T(1024)}, u32[]{:S(2)}) copy-start(f32[1536]{0:T(1024)} %param.9) | copy-start | bytes 18436
  36.0 6.7 %copy-start = (f32[128]{0:T(128)S(1)}, f32[128]{0:T(128)}, u32[]{:S(2)}) copy-start(f32[128]{0:T(128)} %param.8) | copy-start | bytes 1540
  36.0 132.9 %all-to-all-start = ((bf16[16,16,8,1344]{3,2,1,0:T(8,128)(2,1)}), bf16[16,16,8,1344]{3,2,1,0:T(8,128)(2,1)}, u32[]{:S(2)}, u32[]{:S(2)}) async-start(bf16[16,16,8,1344]{3,2,1,0:T(8,128)(2,1)} %pad_maximum_fusion), calls=%async_computation | async-start | bytes 11534336 | tf_op jit(solution)/shard_map/all_to_all | solution.py:74
  175.0 22.0 %slice-start = ((s8[4718592]{0:T(1024)(128)(4,1)}), s8[524288]{0:T(1024)(128)(4,1)S(1)}, s32[]{:S(2)}) async-start(s8[4718592]{0:T(1024)(128)(4,1)} %bitcast.61), calls=%async_computation.2 | async-start | bytes 1048576
  175.0 41.2 %all-to-all-start.1 = ((bf16[16,16,8,384]{3,2,1,0:T(8,128)(2,1)}), bf16[16,16,8,384]{3,2,1,0:T(8,128)(2,1)S(1)}, u32[]{:S(2)}, u32[]{:S(2)}) async-start(bf16[16,16,8,384]{3,2,1,0:T(8,128)(2,1)} %fusion.15), calls=%async_computation.1 | async-start | bytes 3145728 | tf_op jit(solution)/shard_map/all_to_all | solution.py:74
  181.7 15.3 %slice-start.1 = ((s8[4718592]{0:T(1024)(128)(4,1)}), s8[4194304]{0:T(1024)(128)(4,1)S(1)}, s32[]{:S(2)}) async-start(s8[4718592]{0:T(1024)(128)(4,1)} %bitcast.61), calls=%async_computation.3 | async-start | bytes 8388608
  197.0 20.5 %copy-start.1 = (bf16[256,8,192]{0,2,1:T(8,128)(2,1)S(1)}, bf16[256,8,192]{0,2,1:T(8,128)(2,1)}, u32[]{:S(2)}) copy-start(bf16[256,8,192]{0,2,1:T(8,128)(2,1)} %copy.24) | copy-start | bytes 2359300

commit v5 on v4

--- a/solution.py
+++ b/solution.py
@@ -4,7 +4,7 @@
 from jax.sharding import PartitionSpec as P
 
 VBLK = 192
-TAIL_PART = 4
+TAIL_PART = 0
 
 
 def chunk_energies(factors, blocks, occ_rows, occ_cols, vir_chunk, vir_blocks, scale):
@@ -26,7 +26,7 @@
     step_count = owner.shape[0]
     groups = lax.psum(1, "occ")
     local_count = occ_total // groups
-    if nvir % 128 == 0 and nvir >= 256:
+    if TAIL_PART and nvir % 128 == 0 and nvir >= 256:
         tail = max(1, (nvir // 128) // TAIL_PART) * 128
         bounds = [0, nvir - tail, nvir]
     else:

time: 225 us -> 241 us (1.071)
  waiting for transfers between devices: 127 us -> 155 us
  starting transfers between devices: 11.7 us -> 6.69 us
  local copies, waits for them, and re-layouts: 19.1 us -> 14.9 us
  matrix products: 48.4 us -> 45.8 us
    all_to_all x2 -> x1, waiting for transfers between devices: 127 us -> 155 us  [per_device(): lax.all_to_all(product, 'occ', split_axis=0, concat_axis=0, tiled=True)]
    dot_general x2 -> x1, matrix products: 25.8 us -> 19 us  [per_device(): lax.dot_general(rows, orbitals[:, cols], (((3,), (0,)), ((), ())), prefer...]
    all_to_all x2 -> x1, starting transfers between devices: 11.7 us -> 6.69 us  [per_device(): lax.all_to_all(product, 'occ', split_axis=0, concat_axis=0, tiled=True)]
    dot_general x2 -> x1, matrix products: 21.6 us -> 25.7 us  [chunk_energies(): lax.dot_general(factors, blocks, (((0,), (0,)), ((), ())), preferred_elem...]
    pad x1 -> x0, local copies, waits for them, and re-layouts: 3.19 us -> none  [per_device(): factors = jnp.pad(got, ((0, 0), (0, 0), (0, nvir - span)))]
    add x2 -> x1, other arithmetic: 5.08 us -> 4.33 us  [chunk_energies(): vir_chunk[None, :, None, None] + vir_blocks[None, None, :, :]]
  transfers between devices with their start and end apart: 2 -> 1, of which waited for: 2 -> 1; matrix products, arithmetic and copies ran while one was open for 16% -> 2% of each run, Pallas kernels for 0% -> 0%
where the time goes in v5:
time: 241 us
  waiting for transfers between devices  155 us (64%)
  matrix products  45.8 us (19%)
  local copies, waits for them, and re-layouts  14.9 us (6%)
  other arithmetic  12.7 us (5%)
  starting transfers between devices  6.69 us (3%)
  between operations  5.81 us (2%)
    all_to_all x1, waiting for transfers between devices, per_device(): lax.all_to_all(product, 'occ', split_axis=0, concat_axis=0, tiled=True)  155 us
    dot_general x1, matrix products, chunk_energies(): lax.dot_general(factors, blocks, (((0,), (0,)), ((), ())), preferred_elem...  25.7 us
    dot_general x1, matrix products, per_device(): lax.dot_general(rows, orbitals[:, cols], (((3,), (0,)), ((), ())), prefer...  19 us
    all_to_all x1, starting transfers between devices, per_device(): lax.all_to_all(product, 'occ', split_axis=0, concat_axis=0, tiled=True)  6.69 us
    concatenate x1, other arithmetic, per_device(): product = jnp.concatenate([product, extra], axis=3)  6.42 us
    slice x1, local copies, waits for them, and re-layouts, per_device(): got = got[:, :, :span]  5.89 us
  transfers between devices with their start and end apart: 1, of which 1 were waited for; matrix products, arithmetic and copies ran while one was open for 2% of the time, Pallas kernels for 0%

profile of v5, /device:TPU:13, one launch (start us, length us, event | category | flops | bytes accessed | tf_op | source)
XLA Modules:
  0.0 240.6 jit_solution(6072845948992709421)
XLA Ops:
  0.6 0.7 compare_and_fusion
  1.3 0.7 compare_select_fusion
  2.0 1.6 fusion.18
  8.7 2.7 %gather_fusion = bf16[8,16,2048]{2,0,1:T(8,128)(2,1)S(1)} fusion(bf16[16,128,2048]{2,1,0:T(8,128)(2,1)} %param.6, s32[1024]{0:T(1024)S(1)} %pad_clamp_fusion), kind=kCustom, calls=%fused_computation | custom fusion | bytes 1048608 | tf_op jit(solution)/shard_map/jit(_take)/gather | solution.py:39
  11.4 19.0 %fusion.6 = bf16[16,16,8,1536]{3,2,1,0:T(8,128)(2,1)} fusion(bf16[2048,1536]{1,0:T(8,128)(2,1)} %param.7, bf16[16,128,2048]{2,1,0:T(8,128)(2,1)} %param.6), kind=kOutput, calls=%fused_computation.10 | convolution fusion | flops 12888047616 | bytes 20971520 | tf_op jit(solution)/shard_map/dot_general | solution.py:64
  30.4 1.1 fusion.11
  31.5 0.7 fusion.16
  32.2 0.1 constant_dynamic-slice_fusion
  32.4 0.1 constant_dynamic-slice_fusion.2
  32.5 0.1 constant_dynamic-slice_fusion.4
  32.6 0.1 constant_dynamic-slice_fusion.6
  32.7 0.2 stack.38
  32.9 0.1 broadcast_in_dim.32
  33.0 6.4 %pad_maximum_fusion = bf16[16,16,8,1728]{3,2,1,0:T(8,128)(2,1)} fusion(bf16[16,16,8,192]{3,2,1,0:T(8,128)(2,1)S(1)} %broadcast_in_dim.32, bf16[16,16,8,1536]{3,2,1,0:T(8,128)(2,1)} %fusion.6), kind=kLoop, calls=%fused_computation.7 | loop fusion | flops 14155776 | bytes 14155776 | tf_op jit(solution)/shard_map/concatenate | solution.py:70
  39.5 6.7 %all-to-all-start = ((bf16[16,16,8,1728]{3,2,1,0:T(8,128)(2,1)}), bf16[16,16,8,1728]{3,2,1,0:T(8,128)(2,1)}, u32[]{:S(2)}, u32[]{:S(2)}) async-start(bf16[16,16,8,1728]{3,2,1,0:T(8,128)(2,1)} %pad_maximum_fusion), calls=%async_computation | async-start | bytes 14680064 | tf_op jit(solution)/shard_map/all_to_all | solution.py:74
  46.2 0.6 gather_fusion.1
  46.9 0.1 fusion.17
  47.0 4.3 %broadcast_add_fusion = f32[1536,8,192]{0,2,1:T(8,128)} fusion(f32[8,192]{1,0:T(8,128)S(1)} %stack.47, f32[1536]{0:T(1024)S(1)} %copy-done.1), kind=kLoop, calls=%fused_computation.11 | loop fusion | flops 2359296 | bytes 9449472 | tf_op jit(solution)/shard_map/add | solution.py:15
  51.4 154.7 %all-to-all-done = bf16[16,16,8,1728]{3,2,1,0:T(8,128)(2,1)} async-done(((bf16[16,16,8,1728]{3,2,1,0:T(8,128)(2,1)}), bf16[16,16,8,1728]{3,2,1,0:T(8,128)(2,1)}, u32[]{:S(2)}, u32[]{:S(2)}) %all-to-all-start) | async-done | bytes 7077920 | tf_op jit(solution)/shard_map/all_to_all | solution.py:74
  206.0 1.3 slice.93
  207.4 5.9 %slice.92 = bf16[256,8,1536]{2,1,0:T(8,128)(2,1)} slice(bf16[256,8,1728]{2,1,0:T(8,128)(2,1)} %bitcast.15), slice={[0:256], [0:8], [0:1536]} | slice | bytes 12582912 | tf_op jit(solution)/shard_map/slice | solution.py:78
  213.3 1.0 copy.18
  214.3 25.7 %fusion = f32[8,8]{1,0:T(8,128)S(1)} fusion(f32[8]{0:T(128)S(1)} %gather_fusion.1, f32[8]{0:T(128)S(1)} %dynamic_slice.67, f32[1536,8,192]{0,2,1:T(8,128)} %broadcast_add_fusion, bf16[256,8,1536,1]{2,1,0,3:T(8,128)(2,1)} %bitcast.47, bf16[256,8,192]{0,2,1:T(8,128)(2,1)S(1)} %copy.18), kind=kOutput, calls=%fused_computation.3 | convolution fusion | flops 9758048256 | bytes 16515392 | tf_op jit(solution)/shard_map/dot_general | solution.py:11
  240.0 0.6 negate_multiply_fusion
  (14 shorter events, 0.2 us)
Async XLA Ops:
  8.7 21.7 %slice-start = ((s8[6291456]{0:T(1024)(128)(4,1)}), s8[2097152]{0:T(1024)(128)(4,1)S(1)}, s32[]{:S(2)}) async-start(s8[6291456]{0:T(1024)(128)(4,1)} %bitcast.45), calls=%async_computation.1 | async-start | bytes 4194304
  11.4 19.0 %slice-start.1 = ((s8[6291456]{0:T(1024)(128)(4,1)}), s8[4194304]{0:T(1024)(128)(4,1)S(1)}, s32[]{:S(2)}) async-start(s8[6291456]{0:T(1024)(128)(4,1)} %bitcast.45), calls=%async_computation.2 | async-start | bytes 8388608
  39.5 6.7 %copy-start = (f32[128]{0:T(128)S(1)}, f32[128]{0:T(128)}, u32[]{:S(2)}) copy-start(f32[128]{0:T(128)} %param.8) | copy-start | bytes 1540
  39.5 7.4 %copy-start.1 = (f32[1536]{0:T(1024)S(1)}, f32[1536]{0:T(1024)}, u32[]{:S(2)}) copy-start(f32[1536]{0:T(1024)} %param.9) | copy-start | bytes 18436
  39.5 166.6 %all-to-all-start = ((bf16[16,16,8,1728]{3,2,1,0:T(8,128)(2,1)}), bf16[16,16,8,1728]{3,2,1,0:T(8,128)(2,1)}, u32[]{:S(2)}, u32[]{:S(2)}) async-start(bf16[16,16,8,1728]{3,2,1,0:T(8,128)(2,1)} %pad_maximum_fusion), calls=%async_computation | async-start | bytes 14680064 | tf_op jit(solution)/shard_map/all_to_all | solution.py:74

commit v6 on v4

--- a/solution.py
+++ b/solution.py
@@ -57,6 +57,7 @@
     if not ride:
         blocks = lax.all_gather(pieces, "occ", axis=0, tiled=True)
     parts = []
+    raw = []
     sums = []
     for c in range(chunks):
         cols = slice(bounds[c], bounds[c + 1])
@@ -69,9 +70,10 @@
             extra = jnp.broadcast_to(pieces[None], (groups, aux_here, step_count, VBLK))
             product = jnp.concatenate([product, extra], axis=3)
         if c >= 1:
-            held = (parts[-1],) + tuple(sums[-2:-1])
+            held = (raw[-1],) + tuple(sums[-2:-1])
             product, _ = lax.optimization_barrier((product, held))
         got = lax.all_to_all(product, "occ", split_axis=0, concat_axis=0, tiled=True)
+        raw.append(got)
         got = got.reshape(groups * aux_here, local_count, got.shape[-1])
         if c == 0 and ride:
             blocks = got[:, :, span:]
@@ -81,11 +83,16 @@
             factors = jnp.pad(got, ((0, 0), (0, 0), (0, nvir - span)))
         else:
             factors = lax.dynamic_update_slice(factors, got, (0, 0, bounds[c]))
+        if c == 0 and ride:
+            whole = raw[-1].reshape(groups * aux_here, local_count, span + VBLK)
+            vir_here = jnp.concatenate(
+                [vir_energy[cols], jnp.full((VBLK,), jnp.inf, vir_energy.dtype)]
+            )
+        else:
+            whole = lax.optimization_barrier(got)
+            vir_here = vir_energy[cols]
         sums.append(
-            chunk_energies(
-                lax.optimization_barrier(got), blocks, occ_here, occ_cols,
-                vir_energy[cols], vir_blocks, scale,
-            )
+            chunk_energies(whole, blocks, occ_here, occ_cols, vir_here, vir_blocks, scale)
         )
         if c == 0:
             factors, sums[0] = lax.optimization_barrier((factors, sums[0]))

time: 225 us -> 221 us (0.982)
  waiting for transfers between devices: 127 us -> 119 us
  matrix products: 48.4 us -> 54.6 us
  local copies, waits for them, and re-layouts: 19.1 us -> 16.2 us
    all_to_all x2, waiting for transfers between devices: 127 us -> 119 us  [per_device(): lax.all_to_all(product, 'occ', split_axis=0, concat_axis=0, tiled=True)]
    dot_general x2, matrix products: 21.6 us -> 27.7 us  [chunk_energies(): lax.dot_general(factors, blocks, (((0,), (0,)), ((), ())), preferred_elem...]
  transfers between devices with their start and end apart: 2 -> 2, of which waited for: 2 -> 2; matrix products, arithmetic and copies ran while one was open for 16% -> 20% of each run, Pallas kernels for 0% -> 0%
where the time goes in v6:
time: 221 us; the launch traced here: 220 us
  waiting for transfers between devices  119 us (54%)
  matrix products  54.6 us (25%)
  local copies, waits for them, and re-layouts  16.2 us (7%)
  other arithmetic  13.1 us (6%)
  starting transfers between devices  11.6 us (5%)
  between operations  5.79 us (3%)
    all_to_all x2, waiting for transfers between devices, per_device(): lax.all_to_all(product, 'occ', split_axis=0, concat_axis=0, tiled=True)  119 us
    dot_general x2, matrix products, chunk_energies(): lax.dot_general(factors, blocks, (((0,), (0,)), ((), ())), preferred_elem...  27.7 us
    dot_general x2, matrix products, per_device(): lax.dot_general(rows, orbitals[:, cols], (((3,), (0,)), ((), ())), prefer...  25.8 us
    all_to_all x2, starting transfers between devices, per_device(): lax.all_to_all(product, 'occ', split_axis=0, concat_axis=0, tiled=True)  11.6 us
    add x2, other arithmetic, chunk_energies(): vir_chunk[None, :, None, None] + vir_blocks[None, None, :, :]  5.63 us
    concatenate x1, other arithmetic, per_device(): product = jnp.concatenate([product, extra], axis=3)  5.53 us
  transfers between devices with their start and end apart: 2, of which 2 were waited for; matrix products, arithmetic and copies ran while one was open for 20% of the time, Pallas kernels for 0%

profile of v6, /device:TPU:13, one launch (start us, length us, event | category | flops | bytes accessed | tf_op | source)
XLA Modules:
  0.0 220.4 jit_solution(11376395698575550028)
XLA Ops:
  0.6 1.6 fusion.28
  3.5 0.7 compare_select_fusion
  4.1 0.7 compare_and_fusion
  8.7 2.7 %gather_fusion = bf16[8,16,2048]{2,0,1:T(8,128)(2,1)S(1)} fusion(bf16[16,128,2048]{2,1,0:T(8,128)(2,1)} %param.6, s32[1024]{0:T(1024)S(1)} %pad_clamp_fusion), kind=kCustom, calls=%fused_computation | custom fusion | bytes 1048608 | tf_op jit(solution)/shard_map/jit(_take)/gather | solution.py:39
  11.4 16.3 %fusion.9 = bf16[16,16,8,1152]{3,2,1,0:T(8,128)(2,1)} fusion(bf16[2048,1536]{1,0:T(8,128)(2,1)} %param.7, bf16[16,128,2048]{2,1,0:T(8,128)(2,1)} %param.6), kind=kOutput, calls=%fused_computation.14 | convolution fusion | flops 9666035712 | bytes 17825792 | tf_op jit(solution)/shard_map/dot_general | solution.py:65
  27.7 1.1 fusion.14
  28.7 0.7 fusion.26
  30.3 5.5 %pad_maximum_fusion = bf16[16,16,8,1344]{3,2,1,0:T(8,128)(2,1)} fusion(bf16[16,16,8,192]{3,2,1,0:T(8,128)(2,1)S(1)} %broadcast_in_dim.37, bf16[16,16,8,1152]{3,2,1,0:T(8,128)(2,1)} %fusion.9), kind=kLoop, calls=%fused_computation.12 | loop fusion | flops 11010048 | bytes 11010048 | tf_op jit(solution)/shard_map/concatenate | solution.py:71
  35.8 6.7 %all-to-all-start = ((bf16[16,16,8,1344]{3,2,1,0:T(8,128)(2,1)}), bf16[16,16,8,1344]{3,2,1,0:T(8,128)(2,1)}, u32[]{:S(2)}, u32[]{:S(2)}) async-start(bf16[16,16,8,1344]{3,2,1,0:T(8,128)(2,1)} %pad_maximum_fusion), calls=%async_computation | async-start | bytes 11534336 | tf_op jit(solution)/shard_map/all_to_all | solution.py:75
  42.5 0.6 gather_fusion.1
  43.4 1.6 broadcast_add_fusion.1
  45.1 4.0 %broadcast_add_fusion = f32[1344,8,192]{0,2,1:T(8,128)} fusion(f32[8,192]{1,0:T(8,128)S(1)} %stack.47, f32[1344]{0:T(1024)S(1)} %slice_select_fusion), kind=kLoop, calls=%fused_computation.17 | loop fusion | flops 2064384 | bytes 8269056 | tf_op jit(solution)/shard_map/add | solution.py:15
  49.0 9.5 %fusion.15 = bf16[16,16,8,384]{3,2,1,0:T(8,128)(2,1)} fusion(bf16[2048,1536]{1,0:T(8,128)(2,1)} %param.7, bf16[16,128,2048]{2,1,0:T(8,128)(2,1)} %param.6), kind=kOutput, calls=%fused_computation.20 | convolution fusion | flops 3222011904 | bytes 11534336 | tf_op jit(solution)/shard_map/dot_general | solution.py:65
  58.5 110.2 %all-to-all-done = bf16[16,16,8,1344]{3,2,1,0:T(8,128)(2,1)} async-done(((bf16[16,16,8,1344]{3,2,1,0:T(8,128)(2,1)}), bf16[16,16,8,1344]{3,2,1,0:T(8,128)(2,1)}, u32[]{:S(2)}, u32[]{:S(2)}) %all-to-all-start) | async-done | bytes 5505056 | tf_op jit(solution)/shard_map/all_to_all | solution.py:75
  168.7 1.3 slice.110
  170.0 1.0 copy.24
  171.0 4.9 %all-to-all-start.1 = ((bf16[16,16,8,384]{3,2,1,0:T(8,128)(2,1)}), bf16[16,16,8,384]{3,2,1,0:T(8,128)(2,1)S(1)}, u32[]{:S(2)}, u32[]{:S(2)}) async-start(bf16[16,16,8,384]{3,2,1,0:T(8,128)(2,1)} %fusion.15), calls=%async_computation.1 | async-start | bytes 3145728 | tf_op jit(solution)/shard_map/all_to_all | solution.py:75
  175.9 21.4 %fusion = f32[8,8]{1,0:T(8,128)S(1)} fusion(f32[8]{0:T(128)S(1)} %gather_fusion.1, f32[8]{0:T(128)S(1)} %dynamic_slice.67, f32[1344,8,192]{0,2,1:T(8,128)} %broadcast_add_fusion, bf16[256,8,1344,1]{2,1,0,3:T(8,128)(2,1)} %bitcast.16, bf16[256,8,192]{0,2,1:T(8,128)(2,1)S(1)} %copy.24), kind=kOutput, calls=%fused_computation.3 | convolution fusion | flops 8538292224 | bytes 14549312 | tf_op jit(solution)/shard_map/dot_general | solution.py:11
  197.3 2.7 %slice.109 = bf16[256,8,1152]{2,1,0:T(8,128)(2,1)S(1)} slice(bf16[256,8,1344]{2,1,0:T(8,128)(2,1)} %bitcast.15), slice={[0:256], [0:8], [0:1152]} | slice | bytes 9437184 | tf_op jit(solution)/shard_map/slice | solution.py:80
  200.0 3.2 %pad.5 = bf16[256,8,1536]{2,1,0:T(8,128)(2,1)} pad(bf16[256,8,1152]{2,1,0:T(8,128)(2,1)S(1)} %slice.109, bf16[]{:T(256)} %constant.50.clone.1), padding=0_0x0_0x0_384 | pad | bytes 11010050 | tf_op jit(solution)/shard_map/jit(_pad)/pad | solution.py:83
  203.2 8.9 %all-to-all-done.1 = bf16[16,16,8,384]{3,2,1,0:T(8,128)(2,1)S(1)} async-done(((bf16[16,16,8,384]{3,2,1,0:T(8,128)(2,1)}), bf16[16,16,8,384]{3,2,1,0:T(8,128)(2,1)S(1)}, u32[]{:S(2)}, u32[]{:S(2)}) %all-to-all-start.1) | async-done | bytes 1572896 | tf_op jit(solution)/shard_map/all_to_all | solution.py:75
  212.1 1.3 constant_dynamic-update-slice_fusion
  213.4 6.3 %fusion.1 = f32[8,8]{1,0:T(8,128)S(1)} fusion(f32[8]{0:T(128)S(1)} %gather_fusion.1, f32[8]{0:T(128)S(1)} %dynamic_slice.67, f32[384,8,192]{0,2,1:T(8,128)} %broadcast_add_fusion.1, bf16[256,8,384,1]{2,1,0,3:T(8,128)(2,1)S(1)} %bitcast.63, bf16[256,8,192]{0,2,1:T(8,128)(2,1)S(1)} %copy.24), kind=kOutput, calls=%fused_computation.5 | convolution fusion | flops 2439512064 | bytes 4718912 | tf_op jit(solution)/shard_map/dot_general | solution.py:11
  219.8 0.6 negate_multiply_fusion
  (25 shorter events, 1.1 us)
Async XLA Ops:
  8.7 19.0 %slice-start = ((s8[6291456]{0:T(1024)(128)(4,1)}), s8[2097152]{0:T(1024)(128)(4,1)S(1)}, s32[]{:S(2)}) async-start(s8[6291456]{0:T(1024)(128)(4,1)} %bitcast.60), calls=%async_computation.2 | async-start | bytes 4194304
  11.3 16.3 %slice-start.1 = ((s8[6291456]{0:T(1024)(128)(4,1)}), s8[4194304]{0:T(1024)(128)(4,1)S(1)}, s32[]{:S(2)}) async-start(s8[6291456]{0:T(1024)(128)(4,1)} %bitcast.60), calls=%async_computation.3 | async-start | bytes 8388608
  35.8 6.7 %copy-start = (f32[128]{0:T(128)S(1)}, f32[128]{0:T(128)}, u32[]{:S(2)}) copy-start(f32[128]{0:T(128)} %param.8) | copy-start | bytes 1540
  35.8 7.4 %copy-start.1 = (f32[1536]{0:T(1024)S(1)}, f32[1536]{0:T(1024)}, u32[]{:S(2)}) copy-start(f32[1536]{0:T(1024)} %param.9) | copy-start | bytes 18436
  35.8 7.6 %copy-start.2 = (pred[1344]{0:T(1024)(128)(4,1)S(1)}, pred[1344]{0:T(1024)(128)(4,1)}, u32[]{:S(2)}) copy-start(pred[1344]{0:T(1024)(128)(4,1)} %constant.51.clone.1) | copy-start | bytes 4036
  35.8 132.9 %all-to-all-start = ((bf16[16,16,8,1344]{3,2,1,0:T(8,128)(2,1)}), bf16[16,16,8,1344]{3,2,1,0:T(8,128)(2,1)}, u32[]{:S(2)}, u32[]{:S(2)}) async-start(bf16[16,16,8,1344]{3,2,1,0:T(8,128)(2,1)} %pad_maximum_fusion), calls=%async_computation | async-start | bytes 11534336 | tf_op jit(solution)/shard_map/all_to_all | solution.py:75
  171.0 41.1 %all-to-all-start.1 = ((bf16[16,16,8,384]{3,2,1,0:T(8,128)(2,1)}), bf16[16,16,8,384]{3,2,1,0:T(8,128)(2,1)S(1)}, u32[]{:S(2)}, u32[]{:S(2)}) async-start(bf16[16,16,8,384]{3,2,1,0:T(8,128)(2,1)} %fusion.15), calls=%async_computation.1 | async-start | bytes 3145728 | tf_op jit(solution)/shard_map/all_to_all | solution.py:75

commit v7 on v6

--- a/solution.py
+++ b/solution.py
@@ -4,7 +4,7 @@
 from jax.sharding import PartitionSpec as P
 
 VBLK = 192
-TAIL_PART = 4
+EDGE_PART = 4
 
 
 def chunk_energies(factors, blocks, occ_rows, occ_cols, vir_chunk, vir_blocks, scale):
@@ -26,9 +26,10 @@
     step_count = owner.shape[0]
     groups = lax.psum(1, "occ")
     local_count = occ_total // groups
-    if nvir % 128 == 0 and nvir >= 256:
-        tail = max(1, (nvir // 128) // TAIL_PART) * 128
-        bounds = [0, nvir - tail, nvir]
+    tiles = nvir // 128 if nvir % 128 == 0 else 0
+    edge = tiles // EDGE_PART
+    if edge >= 1 and tiles - 2 * edge >= 1:
+        bounds = [0, edge * 128, nvir - edge * 128, nvir]
     else:
         bounds = [0, nvir]
     chunks = len(bounds) - 1
@@ -36,7 +37,15 @@
     rows = integrals.reshape(aux_here, groups, local_count, basis_count)
     rows = jnp.transpose(rows, (1, 0, 2, 3))
 
-    picked = jnp.take(integrals, owner, axis=1)
+    def chunk_product(c):
+        return lax.dot_general(
+            rows, orbitals[:, bounds[c]:bounds[c + 1]], (((3,), (0,)), ((), ())),
+            preferred_element_type=jnp.float32,
+        ).astype(jnp.bfloat16)
+
+    first_product = chunk_product(0)
+    first_product, late = lax.optimization_barrier((first_product, owner))
+    picked = jnp.take(integrals, late, axis=1)
     picked = jnp.dot(
         picked.reshape(aux_here * step_count, basis_count), orbitals,
         preferred_element_type=jnp.float32,
@@ -62,10 +71,7 @@
     for c in range(chunks):
         cols = slice(bounds[c], bounds[c + 1])
         span = bounds[c + 1] - bounds[c]
-        product = lax.dot_general(
-            rows, orbitals[:, cols], (((3,), (0,)), ((), ())),
-            preferred_element_type=jnp.float32,
-        ).astype(jnp.bfloat16)
+        product = first_product if c == 0 else chunk_product(c)
         if c == 0 and ride:
             extra = jnp.broadcast_to(pieces[None], (groups, aux_here, step_count, VBLK))
             product = jnp.concatenate([product, extra], axis=3)

time: 221 us -> 218 us (0.986)
  waiting for transfers between devices: 119 us -> 106 us
  local copies, waits for them, and re-layouts: 16.2 us -> 22.2 us
  starting transfers between devices: 11.6 us -> 16.4 us
  other arithmetic: 13.1 us -> 8.91 us
  matrix products: 54.6 us -> 58.1 us
    all_to_all x2 -> x3, waiting for transfers between devices: 119 us -> 106 us  [per_device(): lax.all_to_all(product, 'occ', split_axis=0, concat_axis=0, tiled=True)]
    all_to_all x2 -> x3, starting transfers between devices: 11.6 us -> 16.4 us  [per_device(): lax.all_to_all(product, 'occ', split_axis=0, concat_axis=0, tiled=True)]
    concatenate x1, other arithmetic: 5.53 us -> 1.85 us  [per_device(): product = jnp.concatenate([product, extra], axis=3)]
    unnamed x11 -> x23, local copies, waits for them, and re-layouts: 1.03 us -> 4.37 us
    dot_general x2 -> x3, matrix products: 25.8 us -> 29.1 us  [chunk_product(): lax.dot_general(rows, orbitals[:, bounds[c]:bounds[c + 1]], (((3,), (0,))...]
    dynamic_update_slice x1 -> x2, local copies, waits for them, and re-layouts: 1.3 us -> 4.58 us  [per_device(): factors = lax.dynamic_update_slice(factors, got, (0, 0, bounds[c]))]
    dot_general x1, matrix products: 1.05 us -> 3.84 us  [per_device(): jnp.dot(picked.reshape(aux_here * step_count, basis_count), orbitals, pre...]
    dot_general x2 -> x3, matrix products: 27.7 us -> 25.2 us  [chunk_energies(): lax.dot_general(factors, blocks, (((0,), (0,)), ((), ())), preferred_elem...]
  transfers between devices with their start and end apart: 2 -> 3, of which waited for: 2 -> 3; matrix products, arithmetic and copies ran while one was open for 20% -> 27% of each run, Pallas kernels for 0% -> 0%
where the time goes in v7:
time: 218 us
  waiting for transfers between devices  106 us (49%)
  matrix products  58.1 us (27%)
  local copies, waits for them, and re-layouts  22.2 us (10%)
  starting transfers between devices  16.4 us (8%)
  other arithmetic  8.91 us (4%)
  between operations  5.85 us (3%)
    all_to_all x3, waiting for transfers between devices, per_device(): lax.all_to_all(product, 'occ', split_axis=0, concat_axis=0, tiled=True)  106 us
    dot_general x3, matrix products, chunk_product(): lax.dot_general(rows, orbitals[:, bounds[c]:bounds[c + 1]], (((3,), (0,))...  29.1 us
    dot_general x3, matrix products, chunk_energies(): lax.dot_general(factors, blocks, (((0,), (0,)), ((), ())), preferred_elem...  25.2 us
    all_to_all x3, starting transfers between devices, per_device(): lax.all_to_all(product, 'occ', split_axis=0, concat_axis=0, tiled=True)  16.4 us
    add x3, other arithmetic, chunk_energies(): vir_chunk[None, :, None, None] + vir_blocks[None, None, :, :]  6.43 us
    pad x1, local copies, waits for them, and re-layouts, per_device(): factors = jnp.pad(got, ((0, 0), (0, 0), (0, nvir - span)))  4.81 us
    dynamic_update_slice x2, local copies, waits for them, and re-layouts, per_device(): factors = lax.dynamic_update_slice(factors, got, (0, 0, bounds[c]))  4.58 us
    unnamed x23, local copies, waits for them, and re-layouts  4.37 us
  transfers between devices with their start and end apart: 3, of which 3 were waited for; matrix products, arithmetic and copies ran while one was open for 27% of the time, Pallas kernels for 0%

profile of v7, /device:TPU:13, one launch (start us, length us, event | category | flops | bytes accessed | tf_op | source)
XLA Modules:
  0.0 217.7 jit_solution(9734034968702282449)
XLA Ops:
  0.6 8.3 %fusion.22 = bf16[16,16,8,384]{3,2,1,0:T(8,128)(2,1)S(1)} fusion(bf16[2048,1536]{1,0:T(8,128)(2,1)} %param.7, bf16[16,128,2048]{2,1,0:T(8,128)(2,1)} %param.6), kind=kOutput, calls=%fused_computation.27 | convolution fusion | flops 3222011904 | bytes 11534336 | tf_op jit(solution)/shard_map/dot_general | solution.py:41
  14.6 2.6 %gather_fusion = bf16[8,16,2048]{2,0,1:T(8,128)(2,1)S(1)} fusion(bf16[16,128,2048]{2,1,0:T(8,128)(2,1)} %param.6, s32[1024]{0:T(1024)S(1)} %pad_clamp_fusion.1), kind=kCustom, calls=%fused_computation | custom fusion | bytes 1048608 | tf_op jit(solution)/shard_map/jit(_take)/gather | solution.py:48
  17.4 3.8 %fusion.16 = bf16[16,8,1536]{2,1,0:T(8,128)(2,1)S(1)} fusion(bf16[2048,1536]{1,0:T(8,128)(2,1)} %param.7, bf16[8,16,2048]{2,0,1:T(8,128)(2,1)S(1)} %gather_fusion, pred[128]{0:T(512)(128)(4,1)S(1)} %broadcast_in_dim.21), kind=kOutput, calls=%fused_computation.24 | convolution fusion | flops 805765120 | bytes 7209088 | tf_op jit(solution)/shard_map/dot_general | solution.py:49
  23.1 1.9 pad_maximum_fusion
  25.0 6.6 %all-to-all-start = ((bf16[16,16,8,576]{3,2,1,0:T(8,128)(2,1)}), bf16[16,16,8,576]{3,2,1,0:T(8,128)(2,1)S(1)}, u32[]{:S(2)}, u32[]{:S(2)}) async-start(bf16[16,16,8,576]{3,2,1,0:T(8,128)(2,1)} %pad_maximum_fusion), calls=%async_computation | async-start | bytes 5242880 | tf_op jit(solution)/shard_map/all_to_all | solution.py:81
  31.7 11.2 %fusion.17 = bf16[16,16,8,768]{3,2,1,0:T(8,128)(2,1)} fusion(bf16[2048,1536]{1,0:T(8,128)(2,1)} %param.7, bf16[16,128,2048]{2,1,0:T(8,128)(2,1)} %param.6), kind=kOutput, calls=%fused_computation.25 | convolution fusion | flops 6444023808 | bytes 14680064 | tf_op jit(solution)/shard_map/dot_general | solution.py:41
  42.8 47.4 %all-to-all-done = bf16[16,16,8,576]{3,2,1,0:T(8,128)(2,1)S(1)} async-done(((bf16[16,16,8,576]{3,2,1,0:T(8,128)(2,1)}), bf16[16,16,8,576]{3,2,1,0:T(8,128)(2,1)S(1)}, u32[]{:S(2)}, u32[]{:S(2)}) %all-to-all-start) | async-done | bytes 2359328 | tf_op jit(solution)/shard_map/all_to_all | solution.py:81
  90.2 1.5 copy-done.1
  91.7 4.9 %all-to-all-start.1 = ((bf16[16,16,8,768]{3,2,1,0:T(8,128)(2,1)}), bf16[16,16,8,768]{3,2,1,0:T(8,128)(2,1)S(1)}, u32[]{:S(2)}, u32[]{:S(2)}) async-start(bf16[16,16,8,768]{3,2,1,0:T(8,128)(2,1)} %fusion.17), calls=%async_computation.1 | async-start | bytes 6291456 | tf_op jit(solution)/shard_map/all_to_all | solution.py:81
  97.4 1.6 broadcast_add_fusion.2
  99.1 2.3 %broadcast_add_fusion.1 = f32[576,8,192]{0,2,1:T(8,128)} fusion(f32[8,192]{1,0:T(8,128)S(1)} %stack.47, f32[576]{0:T(1024)S(1)} %slice_select_fusion), kind=kLoop, calls=%fused_computation.26 | loop fusion | flops 884736 | bytes 3547392 | tf_op jit(solution)/shard_map/add | solution.py:15
  101.4 2.5 %broadcast_add_fusion = f32[768,8,192]{0,2,1:T(8,128)} fusion(f32[8,192]{1,0:T(8,128)S(1)} %stack.47, f32[768]{0:T(1024)S(1)} %slice.103), kind=kLoop, calls=%fused_computation.23 | loop fusion | flops 1179648 | bytes 4727808 | tf_op jit(solution)/shard_map/add | solution.py:15
  103.9 9.6 %fusion.25 = bf16[16,16,8,384]{3,2,1,0:T(8,128)(2,1)} fusion(bf16[2048,1536]{1,0:T(8,128)(2,1)} %param.7, bf16[16,128,2048]{2,1,0:T(8,128)(2,1)} %param.6), kind=kOutput, calls=%fused_computation.28 | convolution fusion | flops 3222011904 | bytes 11534336 | tf_op jit(solution)/shard_map/dot_general | solution.py:41
  114.5 1.3 slice.117
  115.8 2.6 %copy.30 = bf16[256,8,192]{0,2,1:T(8,128)(2,1)} copy(bf16[256,8,192]{2,1,0:T(8,128)(2,1)} %slice.118) | data formatting | bytes 1572864
  118.5 4.8 %pad.5 = bf16[256,8,1536]{2,1,0:T(8,128)(2,1)} pad(bf16[256,8,384]{2,1,0:T(8,128)(2,1)} %slice.117, bf16[]{:T(256)} %constant.51.clone.1), padding=0_0x0_0x0_1152 | pad | bytes 7864322 | tf_op jit(solution)/shard_map/jit(_pad)/pad | solution.py:89
  123.4 8.3 %fusion.1 = f32[8,8]{1,0:T(8,128)S(1)} fusion(f32[8]{0:T(128)S(1)} %gather_fusion.1, f32[8]{0:T(128)S(1)} %dynamic_slice.67, f32[576,8,192]{0,2,1:T(8,128)S(1)} %copy-done.4, bf16[256,8,576,1]{2,1,0,3:T(8,128)(2,1)S(1)} %bitcast.82, bf16[256,8,192]{0,2,1:T(8,128)(2,1)S(1)} %copy-done.5), kind=kOutput, calls=%fused_computation.5 | convolution fusion | flops 3659268096 | bytes 6684992 | tf_op jit(solution)/shard_map/dot_general | solution.py:11
  131.8 34.8 %all-to-all-done.1 = bf16[16,16,8,768]{3,2,1,0:T(8,128)(2,1)S(1)} async-done(((bf16[16,16,8,768]{3,2,1,0:T(8,128)(2,1)}), bf16[16,16,8,768]{3,2,1,0:T(8,128)(2,1)S(1)}, u32[]{:S(2)}, u32[]{:S(2)}) %all-to-all-start.1) | async-done | bytes 3145760 | tf_op jit(solution)/shard_map/all_to_all | solution.py:81
  166.5 4.9 %all-to-all-start.2 = ((bf16[16,16,8,384]{3,2,1,0:T(8,128)(2,1)}), bf16[16,16,8,384]{3,2,1,0:T(8,128)(2,1)}, u32[]{:S(2)}, u32[]{:S(2)}) async-start(bf16[16,16,8,384]{3,2,1,0:T(8,128)(2,1)} %fusion.25), calls=%async_computation.2 | async-start | bytes 3145728 | tf_op jit(solution)/shard_map/all_to_all | solution.py:81
  171.5 1.9 constant_dynamic-update-slice_fusion.1
  173.3 10.3 %fusion = f32[8,8]{1,0:T(8,128)S(1)} fusion(f32[8]{0:T(128)S(1)} %gather_fusion.1, f32[8]{0:T(128)S(1)} %dynamic_slice.67, f32[768,8,192]{0,2,1:T(8,128)} %broadcast_add_fusion, bf16[256,8,768,1]{2,1,0,3:T(8,128)(2,1)S(1)} %bitcast.79, bf16[256,8,192]{0,2,1:T(8,128)(2,1)S(1)} %copy-done.6), kind=kOutput, calls=%fused_computation.3 | convolution fusion | flops 4879024128 | bytes 8651072 | tf_op jit(solution)/shard_map/dot_general | solution.py:11
  183.6 24.1 %all-to-all-done.2 = bf16[16,16,8,384]{3,2,1,0:T(8,128)(2,1)} async-done(((bf16[16,16,8,384]{3,2,1,0:T(8,128)(2,1)}), bf16[16,16,8,384]{3,2,1,0:T(8,128)(2,1)}, u32[]{:S(2)}, u32[]{:S(2)}) %all-to-all-start.2) | async-done | bytes 1572896 | tf_op jit(solution)/shard_map/all_to_all | solution.py:81
  207.7 2.7 %constant_dynamic-update-slice_fusion = bf16[256,8,1536]{2,1,0:T(8,128)(2,1)} fusion(bf16[256,8,1536]{2,1,0:T(8,128)(2,1)} %constant_dynamic-update-slice_fusion.1, bf16[256,8,384]{2,1,0:T(8,128)(2,1)} %bitcast.31), kind=kLoop, calls=%fused_computation.47 | loop fusion | bytes 3145728 | tf_op jit(solution)/shard_map/dynamic_update_slice | solution.py:91
  210.4 6.6 %fusion.2 = f32[8,8]{1,0:T(8,128)S(1)} fusion(f32[8]{0:T(128)S(1)} %gather_fusion.1, f32[8]{0:T(128)S(1)} %dynamic_slice.67, f32[384,8,192]{0,2,1:T(8,128)} %broadcast_add_fusion.2, bf16[256,8,384,1]{2,1,0,3:T(8,128)(2,1)} %bitcast.33, bf16[256,8,192]{0,2,1:T(8,128)(2,1)} %copy.30), kind=kOutput, calls=%fused_computation.7 | convolution fusion | flops 2439512064 | bytes 4718912 | tf_op jit(solution)/shard_map/dot_general | solution.py:11
  (48 shorter events, 5.3 us)
Async XLA Ops:
  0.6 8.3 %copy-start.10 = (s32[8]{0:T(128)S(1)}, s32[8]{0:T(128)}, u32[]{:S(2)}) copy-start(s32[8]{0:T(128)} %param.10) | copy-start | bytes 100
  0.6 8.4 %copy-start.8 = (s32[8]{0:T(128)S(1)}, s32[8]{0:T(128)}, u32[]{:S(2)}) copy-start(s32[8]{0:T(128)} %param.11) | copy-start | bytes 100
  21.9 9.6 %copy-start.7 = (f32[1536]{0:T(1024)S(1)}, f32[1536]{0:T(1024)}, u32[]{:S(2)}) copy-start(f32[1536]{0:T(1024)} %param.9) | copy-start | bytes 18436
  22.0 9.7 %copy-start.9 = (pred[576]{0:T(1024)(128)(4,1)S(1)}, pred[576]{0:T(1024)(128)(4,1)}, u32[]{:S(2)}) copy-start(pred[576]{0:T(1024)(128)(4,1)} %constant.52.clone.1) | copy-start | bytes 1732
  25.0 65.2 %all-to-all-start = ((bf16[16,16,8,576]{3,2,1,0:T(8,128)(2,1)}), bf16[16,16,8,576]{3,2,1,0:T(8,128)(2,1)S(1)}, u32[]{:S(2)}, u32[]{:S(2)}) async-start(bf16[16,16,8,576]{3,2,1,0:T(8,128)(2,1)} %pad_maximum_fusion), calls=%async_computation | async-start | bytes 5242880 | tf_op jit(solution)/shard_map/all_to_all | solution.py:81
  42.8 53.9 %copy-start = (f32[128]{0:T(128)S(1)}, f32[128]{0:T(128)}, u32[]{:S(2)}) copy-start(f32[128]{0:T(128)} %param.8) | copy-start | bytes 1540
  90.2 1.6 copy-start.1
  91.7 74.8 %all-to-all-start.1 = ((bf16[16,16,8,768]{3,2,1,0:T(8,128)(2,1)}), bf16[16,16,8,768]{3,2,1,0:T(8,128)(2,1)S(1)}, u32[]{:S(2)}, u32[]{:S(2)}) async-start(bf16[16,16,8,768]{3,2,1,0:T(8,128)(2,1)} %fusion.17), calls=%async_computation.1 | async-start | bytes 6291456 | tf_op jit(solution)/shard_map/all_to_all | solution.py:81
  103.9 9.6 %copy-start.2 = (bf16[16,16,8,576]{3,2,1,0:T(8,128)(2,1)S(1)}, bf16[16,16,8,576]{3,2,1,0:T(8,128)(2,1)}, u32[]{:S(2)}) copy-start(bf16[16,16,8,576]{3,2,1,0:T(8,128)(2,1)} %copy-done.1) | copy-start | bytes 7077892
  118.5 4.8 %copy-start.3 = (bf16[16,16,8,576]{3,2,1,0:T(8,128)(2,1)S(1)}, bf16[16,16,8,576]{3,2,1,0:T(8,128)(2,1)}, u32[]{:S(2)}) copy-start(bf16[16,16,8,576]{3,2,1,0:T(8,128)(2,1)} %copy-done.1) | copy-start | bytes 7077892
  118.5 4.8 %copy-start.4 = (f32[576,8,192]{0,2,1:T(8,128)S(1)}, f32[576,8,192]{0,2,1:T(8,128)}, u32[]{:S(2)}) copy-start(f32[576,8,192]{0,2,1:T(8,128)} %broadcast_add_fusion.1) | copy-start | bytes 10616836
  118.5 5.0 %copy-start.5 = (bf16[256,8,192]{0,2,1:T(8,128)(2,1)S(1)}, bf16[256,8,192]{0,2,1:T(8,128)(2,1)}, u32[]{:S(2)}) copy-start(bf16[256,8,192]{0,2,1:T(8,128)(2,1)} %copy.30) | copy-start | bytes 2359300
  166.5 41.2 %all-to-all-start.2 = ((bf16[16,16,8,384]{3,2,1,0:T(8,128)(2,1)}), bf16[16,16,8,384]{3,2,1,0:T(8,128)(2,1)}, u32[]{:S(2)}, u32[]{:S(2)}) async-start(bf16[16,16,8,384]{3,2,1,0:T(8,128)(2,1)} %fusion.25), calls=%async_computation.2 | async-start | bytes 3145728 | tf_op jit(solution)/shard_map/all_to_all | solution.py:81
  171.4 1.9 copy-start.6

commit v8 on v7

--- a/solution.py
+++ b/solution.py
@@ -45,7 +45,10 @@
 
     first_product = chunk_product(0)
     first_product, late = lax.optimization_barrier((first_product, owner))
-    picked = jnp.take(integrals, late, axis=1)
+    picked = jnp.concatenate(
+        [lax.dynamic_slice_in_dim(integrals, late[s], 1, axis=1) for s in range(step_count)],
+        axis=1,
+    )
     picked = jnp.dot(
         picked.reshape(aux_here * step_count, basis_count), orbitals,
         preferred_element_type=jnp.float32,

time: 218 us -> 236 us (1.083)
  between operations: 5.85 us -> 21.2 us
  local copies, waits for them, and re-layouts: 22.2 us -> 24.7 us
    dynamic_slice x0 -> x1, local copies, waits for them, and re-layouts: none -> 3.31 us  [per_device(): lax.dynamic_slice_in_dim(integrals, late[s], 1, axis=1)]
    gather x1 -> x0, local copies, waits for them, and re-layouts: 2.62 us -> none  [per_device(): picked = jnp.take(integrals, late, axis=1)]
  transfers between devices with their start and end apart: 3 -> 3, of which waited for: 3 -> 3; matrix products, arithmetic and copies ran while one was open for 27% -> 25% of each run, Pallas kernels for 0% -> 0%
where the time goes in v8:
time: 236 us; the launch traced here: 235 us
  waiting for transfers between devices  106 us (45%)
  matrix products  58.1 us (25%)
  local copies, waits for them, and re-layouts  24.7 us (10%)
  between operations  21.2 us (9%)
  starting transfers between devices  16.4 us (7%)
  other arithmetic  8.9 us (4%)
    all_to_all x3, waiting for transfers between devices, per_device(): lax.all_to_all(product, 'occ', split_axis=0, concat_axis=0, tiled=True)  106 us
    dot_general x3, matrix products, chunk_product(): lax.dot_general(rows, orbitals[:, bounds[c]:bounds[c + 1]], (((3,), (0,))...  29.1 us
    dot_general x3, matrix products, chunk_energies(): lax.dot_general(factors, blocks, (((0,), (0,)), ((), ())), preferred_elem...  25.2 us
    all_to_all x3, starting transfers between devices, per_device(): lax.all_to_all(product, 'occ', split_axis=0, concat_axis=0, tiled=True)  16.4 us
    add x3, other arithmetic, chunk_energies(): vir_chunk[None, :, None, None] + vir_blocks[None, None, :, :]  6.43 us
    pad x1, local copies, waits for them, and re-layouts, per_device(): factors = jnp.pad(got, ((0, 0), (0, 0), (0, nvir - span)))  4.81 us
  transfers between devices with their start and end apart: 3, of which 3 were waited for; matrix products, arithmetic and copies ran while one was open for 25% of the time, Pallas kernels for 0%

profile of v8, /device:TPU:13, one launch (start us, length us, event | category | flops | bytes accessed | tf_op | source)
XLA Modules:
  0.0 235.5 jit_solution(2848230317621926692)
XLA Ops:
  0.6 8.3 %fusion.22 = bf16[16,16,8,384]{3,2,1,0:T(8,128)(2,1)S(1)} fusion(bf16[2048,1536]{1,0:T(8,128)(2,1)} %param.7, bf16[16,128,2048]{2,1,0:T(8,128)(2,1)} %param.6), kind=kOutput, calls=%fused_computation.26 | convolution fusion | flops 3222011904 | bytes 11534336 | tf_op jit(solution)/shard_map/dot_general | solution.py:41
  30.7 3.3 %constant_dynamic-slice_fusion.8 = (bf16[16,1,2048]{2,1,0:T(2,128)(2,1)S(1)}, bf16[16,1,2048]{2,1,0:T(2,128)(2,1)S(1)}, bf16[16,1,2048]{2,1,0:T(2,128)(2,1)S(1)}...) fusion(bf16[16,128,2048]{2,1,0:T(8,128)(2,1)} %param.6, ...), kind=kLoop, calls=%fused_computation.48 | loop fusion | bytes 1048608 | tf_op jit(solution)/shard_map/dynamic_slice | solution.py:49
  34.0 1.6 concatenate.9
  35.6 3.8 %fusion.16 = bf16[16,8,1536]{2,1,0:T(8,128)(2,1)S(1)} fusion(bf16[2048,1536]{1,0:T(8,128)(2,1)} %param.7, bf16[16,8,2048]{2,1,0:T(8,128)(2,1)S(1)} %concatenate.9), kind=kOutput, calls=%fused_computation.23 | convolution fusion | flops 805502976 | bytes 7208960 | tf_op jit(solution)/shard_map/dot_general | solution.py:52
  40.9 1.9 pad_maximum_fusion
  42.8 6.6 %all-to-all-start = ((bf16[16,16,8,576]{3,2,1,0:T(8,128)(2,1)}), bf16[16,16,8,576]{3,2,1,0:T(8,128)(2,1)S(1)}, u32[]{:S(2)}, u32[]{:S(2)}) async-start(bf16[16,16,8,576]{3,2,1,0:T(8,128)(2,1)} %pad_maximum_fusion), calls=%async_computation | async-start | bytes 5242880 | tf_op jit(solution)/shard_map/all_to_all | solution.py:84
  49.5 11.2 %fusion.17 = bf16[16,16,8,768]{3,2,1,0:T(8,128)(2,1)} fusion(bf16[2048,1536]{1,0:T(8,128)(2,1)} %param.7, bf16[16,128,2048]{2,1,0:T(8,128)(2,1)} %param.6), kind=kOutput, calls=%fused_computation.24 | convolution fusion | flops 6444023808 | bytes 14680064 | tf_op jit(solution)/shard_map/dot_general | solution.py:41
  60.7 47.3 %all-to-all-done = bf16[16,16,8,576]{3,2,1,0:T(8,128)(2,1)S(1)} async-done(((bf16[16,16,8,576]{3,2,1,0:T(8,128)(2,1)}), bf16[16,16,8,576]{3,2,1,0:T(8,128)(2,1)S(1)}, u32[]{:S(2)}, u32[]{:S(2)}) %all-to-all-start) | async-done | bytes 2359328 | tf_op jit(solution)/shard_map/all_to_all | solution.py:84
  108.0 1.5 copy-done.1
  109.6 4.9 %all-to-all-start.1 = ((bf16[16,16,8,768]{3,2,1,0:T(8,128)(2,1)}), bf16[16,16,8,768]{3,2,1,0:T(8,128)(2,1)S(1)}, u32[]{:S(2)}, u32[]{:S(2)}) async-start(bf16[16,16,8,768]{3,2,1,0:T(8,128)(2,1)} %fusion.17), calls=%async_computation.1 | async-start | bytes 6291456 | tf_op jit(solution)/shard_map/all_to_all | solution.py:84
  115.3 1.7 broadcast_add_fusion.2
  116.9 2.3 broadcast_add_fusion.1
  119.2 2.5 %broadcast_add_fusion = f32[768,8,192]{0,2,1:T(8,128)} fusion(f32[8,192]{1,0:T(8,128)S(1)} %stack.47, f32[768]{0:T(1024)S(1)} %slice.135), kind=kLoop, calls=%fused_computation.22 | loop fusion | flops 1179648 | bytes 4727808 | tf_op jit(solution)/shard_map/add | solution.py:15
  121.7 9.6 %fusion.25 = bf16[16,16,8,384]{3,2,1,0:T(8,128)(2,1)} fusion(bf16[2048,1536]{1,0:T(8,128)(2,1)} %param.7, bf16[16,128,2048]{2,1,0:T(8,128)(2,1)} %param.6), kind=kOutput, calls=%fused_computation.27 | convolution fusion | flops 3222011904 | bytes 11534336 | tf_op jit(solution)/shard_map/dot_general | solution.py:41
  133.6 2.6 %copy.30 = bf16[256,8,192]{0,2,1:T(8,128)(2,1)} copy(bf16[256,8,192]{2,1,0:T(8,128)(2,1)} %slice.148) | data formatting | bytes 1572864
  136.3 4.8 %pad.5 = bf16[256,8,1536]{2,1,0:T(8,128)(2,1)} pad(bf16[256,8,384]{2,1,0:T(8,128)(2,1)} %slice.147, bf16[]{:T(256)} %constant.37.clone.1), padding=0_0x0_0x0_1152 | pad | bytes 7864322 | tf_op jit(solution)/shard_map/jit(_pad)/pad | solution.py:92
  141.3 8.3 %fusion.1 = f32[8,8]{1,0:T(8,128)S(1)} fusion(f32[8]{0:T(128)S(1)} %gather_fusion, f32[8]{0:T(128)S(1)} %dynamic_slice.99, f32[576,8,192]{0,2,1:T(8,128)S(1)} %copy-done.4, bf16[256,8,576,1]{2,1,0,3:T(8,128)(2,1)S(1)} %bitcast.88, bf16[256,8,192]{0,2,1:T(8,128)(2,1)S(1)} %copy-done.5), kind=kOutput, calls=%fused_computation.4 | convolution fusion | flops 3659268096 | bytes 6684992 | tf_op jit(solution)/shard_map/dot_general | solution.py:11
  149.6 34.8 %all-to-all-done.1 = bf16[16,16,8,768]{3,2,1,0:T(8,128)(2,1)S(1)} async-done(((bf16[16,16,8,768]{3,2,1,0:T(8,128)(2,1)}), bf16[16,16,8,768]{3,2,1,0:T(8,128)(2,1)S(1)}, u32[]{:S(2)}, u32[]{:S(2)}) %all-to-all-start.1) | async-done | bytes 3145760 | tf_op jit(solution)/shard_map/all_to_all | solution.py:84
  184.4 4.9 %all-to-all-start.2 = ((bf16[16,16,8,384]{3,2,1,0:T(8,128)(2,1)}), bf16[16,16,8,384]{3,2,1,0:T(8,128)(2,1)}, u32[]{:S(2)}, u32[]{:S(2)}) async-start(bf16[16,16,8,384]{3,2,1,0:T(8,128)(2,1)} %fusion.25), calls=%async_computation.2 | async-start | bytes 3145728 | tf_op jit(solution)/shard_map/all_to_all | solution.py:84
  189.3 1.9 constant_dynamic-update-slice_fusion.1
  191.1 10.3 %fusion = f32[8,8]{1,0:T(8,128)S(1)} fusion(f32[8]{0:T(128)S(1)} %gather_fusion, f32[8]{0:T(128)S(1)} %dynamic_slice.99, f32[768,8,192]{0,2,1:T(8,128)} %broadcast_add_fusion, bf16[256,8,768,1]{2,1,0,3:T(8,128)(2,1)S(1)} %bitcast.85, bf16[256,8,192]{0,2,1:T(8,128)(2,1)S(1)} %copy-done.6), kind=kOutput, calls=%fused_computation.2 | convolution fusion | flops 4879024128 | bytes 8651072 | tf_op jit(solution)/shard_map/dot_general | solution.py:11
  201.4 24.1 %all-to-all-done.2 = bf16[16,16,8,384]{3,2,1,0:T(8,128)(2,1)} async-done(((bf16[16,16,8,384]{3,2,1,0:T(8,128)(2,1)}), bf16[16,16,8,384]{3,2,1,0:T(8,128)(2,1)}, u32[]{:S(2)}, u32[]{:S(2)}) %all-to-all-start.2) | async-done | bytes 1572896 | tf_op jit(solution)/shard_map/all_to_all | solution.py:84
  225.6 2.7 %constant_dynamic-update-slice_fusion = bf16[256,8,1536]{2,1,0:T(8,128)(2,1)} fusion(bf16[256,8,1536]{2,1,0:T(8,128)(2,1)} %constant_dynamic-update-slice_fusion.1, bf16[256,8,384]{2,1,0:T(8,128)(2,1)} %bitcast.38), kind=kLoop, calls=%fused_computation.38 | loop fusion | bytes 3145728 | tf_op jit(solution)/shard_map/dynamic_update_slice | solution.py:94
  228.3 6.6 %fusion.2 = f32[8,8]{1,0:T(8,128)S(1)} fusion(f32[8]{0:T(128)S(1)} %gather_fusion, f32[8]{0:T(128)S(1)} %dynamic_slice.99, f32[384,8,192]{0,2,1:T(8,128)} %broadcast_add_fusion.2, bf16[256,8,384,1]{2,1,0,3:T(8,128)(2,1)} %bitcast.40, bf16[256,8,192]{0,2,1:T(8,128)(2,1)} %copy.30), kind=kOutput, calls=%fused_computation.6 | convolution fusion | flops 2439512064 | bytes 4718912 | tf_op jit(solution)/shard_map/dot_general | solution.py:11
  (42 shorter events, 6.9 us)
Async XLA Ops:
  0.6 8.3 %copy-start.9 = (s32[8]{0:T(128)S(1)}, s32[8]{0:T(128)}, u32[]{:S(2)}) copy-start(s32[8]{0:T(128)} %param.10) | copy-start | bytes 100
  0.6 19.1 %copy-start.8 = (s32[8]{0:T(128)S(1)}, s32[8]{0:T(128)}, u32[]{:S(2)}) copy-start(s32[8]{0:T(128)} %param.11) | copy-start | bytes 100
  40.1 9.3 %copy-start.7 = (f32[1536]{0:T(1024)S(1)}, f32[1536]{0:T(1024)}, u32[]{:S(2)}) copy-start(f32[1536]{0:T(1024)} %param.9) | copy-start | bytes 18436
  40.1 9.4 %copy-start.10 = (pred[576]{0:T(1024)(128)(4,1)S(1)}, pred[576]{0:T(1024)(128)(4,1)}, u32[]{:S(2)}) copy-start(pred[576]{0:T(1024)(128)(4,1)} %constant.38.clone.1) | copy-start | bytes 1732
  42.8 65.2 %all-to-all-start = ((bf16[16,16,8,576]{3,2,1,0:T(8,128)(2,1)}), bf16[16,16,8,576]{3,2,1,0:T(8,128)(2,1)S(1)}, u32[]{:S(2)}, u32[]{:S(2)}) async-start(bf16[16,16,8,576]{3,2,1,0:T(8,128)(2,1)} %pad_maximum_fusion), calls=%async_computation | async-start | bytes 5242880 | tf_op jit(solution)/shard_map/all_to_all | solution.py:84
  60.7 53.8 %copy-start = (f32[128]{0:T(128)S(1)}, f32[128]{0:T(128)}, u32[]{:S(2)}) copy-start(f32[128]{0:T(128)} %param.8) | copy-start | bytes 1540
  108.0 1.5 copy-start.1
  109.6 74.8 %all-to-all-start.1 = ((bf16[16,16,8,768]{3,2,1,0:T(8,128)(2,1)}), bf16[16,16,8,768]{3,2,1,0:T(8,128)(2,1)S(1)}, u32[]{:S(2)}, u32[]{:S(2)}) async-start(bf16[16,16,8,768]{3,2,1,0:T(8,128)(2,1)} %fusion.17), calls=%async_computation.1 | async-start | bytes 6291456 | tf_op jit(solution)/shard_map/all_to_all | solution.py:84
  121.7 9.6 %copy-start.2 = (bf16[16,16,8,576]{3,2,1,0:T(8,128)(2,1)S(1)}, bf16[16,16,8,576]{3,2,1,0:T(8,128)(2,1)}, u32[]{:S(2)}) copy-start(bf16[16,16,8,576]{3,2,1,0:T(8,128)(2,1)} %copy-done.1) | copy-start | bytes 7077892
  136.3 4.8 %copy-start.3 = (bf16[16,16,8,576]{3,2,1,0:T(8,128)(2,1)S(1)}, bf16[16,16,8,576]{3,2,1,0:T(8,128)(2,1)}, u32[]{:S(2)}) copy-start(bf16[16,16,8,576]{3,2,1,0:T(8,128)(2,1)} %copy-done.1) | copy-start | bytes 7077892
  136.3 4.8 %copy-start.4 = (f32[576,8,192]{0,2,1:T(8,128)S(1)}, f32[576,8,192]{0,2,1:T(8,128)}, u32[]{:S(2)}) copy-start(f32[576,8,192]{0,2,1:T(8,128)} %broadcast_add_fusion.1) | copy-start | bytes 10616836
  136.3 5.0 %copy-start.5 = (bf16[256,8,192]{0,2,1:T(8,128)(2,1)S(1)}, bf16[256,8,192]{0,2,1:T(8,128)(2,1)}, u32[]{:S(2)}) copy-start(bf16[256,8,192]{0,2,1:T(8,128)(2,1)} %copy.30) | copy-start | bytes 2359300
  184.4 41.2 %all-to-all-start.2 = ((bf16[16,16,8,384]{3,2,1,0:T(8,128)(2,1)}), bf16[16,16,8,384]{3,2,1,0:T(8,128)(2,1)}, u32[]{:S(2)}, u32[]{:S(2)}) async-start(bf16[16,16,8,384]{3,2,1,0:T(8,128)(2,1)} %fusion.25), calls=%async_computation.2 | async-start | bytes 3145728 | tf_op jit(solution)/shard_map/all_to_all | solution.py:84
  189.3 1.9 copy-start.6

commit v9 on v7

--- a/solution.py
+++ b/solution.py
@@ -63,33 +63,34 @@
     )
     scale = 1.0 / (aux_here * groups * nvir * VBLK)
 
+    carrier = min(1, chunks - 1) if ride else -1
     if not ride:
         blocks = lax.all_gather(pieces, "occ", axis=0, tiled=True)
-    parts = []
     raw = []
     sums = []
+    made_at = {}
+    pending = []
     for c in range(chunks):
         cols = slice(bounds[c], bounds[c + 1])
         span = bounds[c + 1] - bounds[c]
         product = first_product if c == 0 else chunk_product(c)
-        if c == 0 and ride:
+        if c == carrier:
             extra = jnp.broadcast_to(pieces[None], (groups, aux_here, step_count, VBLK))
             product = jnp.concatenate([product, extra], axis=3)
         if c >= 1:
-            held = (raw[-1],) + tuple(sums[-2:-1])
+            held = (raw[-1],) + tuple(made_at.get(c - 2, ()))
             product, _ = lax.optimization_barrier((product, held))
         got = lax.all_to_all(product, "occ", split_axis=0, concat_axis=0, tiled=True)
         raw.append(got)
         got = got.reshape(groups * aux_here, local_count, got.shape[-1])
-        if c == 0 and ride:
+        if c == carrier:
             blocks = got[:, :, span:]
             got = got[:, :, :span]
-        parts.append(got)
         if c == 0:
             factors = jnp.pad(got, ((0, 0), (0, 0), (0, nvir - span)))
         else:
             factors = lax.dynamic_update_slice(factors, got, (0, 0, bounds[c]))
-        if c == 0 and ride:
+        if c == carrier:
             whole = raw[-1].reshape(groups * aux_here, local_count, span + VBLK)
             vir_here = jnp.concatenate(
                 [vir_energy[cols], jnp.full((VBLK,), jnp.inf, vir_energy.dtype)]
@@ -97,11 +98,17 @@
         else:
             whole = lax.optimization_barrier(got)
             vir_here = vir_energy[cols]
-        sums.append(
-            chunk_energies(whole, blocks, occ_here, occ_cols, vir_here, vir_blocks, scale)
-        )
-        if c == 0:
-            factors, sums[0] = lax.optimization_barrier((factors, sums[0]))
+        pending.append((whole, vir_here))
+        if c >= carrier:
+            made = [
+                chunk_energies(view, blocks, occ_here, occ_cols, vir_k, vir_blocks, scale)
+                for view, vir_k in pending
+            ]
+            pending = []
+            if c < chunks - 1:
+                factors, made[0] = lax.optimization_barrier((factors, made[0]))
+            made_at[c] = made
+            sums.extend(made)
     total = sums[0]
     for extra_sum in sums[1:]:
         total = total + extra_sum

time: 218 us -> 200 us (0.917)
  waiting for transfers between devices: 106 us -> 90.3 us
  local copies, waits for them, and re-layouts: 22.2 us -> 19.3 us
    all_to_all x3, waiting for transfers between devices: 106 us -> 90.3 us  [per_device(): lax.all_to_all(product, 'occ', split_axis=0, concat_axis=0, tiled=True)]
    unnamed x23 -> x13, local copies, waits for them, and re-layouts: 4.37 us -> 2.64 us
    add x3 -> x2, other arithmetic: 6.43 us -> 5.65 us  [chunk_energies(): vir_chunk[None, :, None, None] + vir_blocks[None, None, :, :]]
  transfers between devices with their start and end apart: 3 -> 3, of which waited for: 3 -> 3; matrix products, arithmetic and copies ran while one was open for 27% -> 35% of each run, Pallas kernels for 0% -> 0%
where the time goes in v9:
time: 200 us
  waiting for transfers between devices  90.3 us (45%)
  matrix products  58.9 us (29%)
  local copies, waits for them, and re-layouts  19.3 us (10%)
  starting transfers between devices  16.4 us (8%)
  other arithmetic  8.97 us (4%)
  between operations  5.88 us (3%)
    all_to_all x3, waiting for transfers between devices, per_device(): lax.all_to_all(product, 'occ', split_axis=0, concat_axis=0, tiled=True)  90.3 us
    dot_general x3, matrix products, chunk_product(): lax.dot_general(rows, orbitals[:, bounds[c]:bounds[c + 1]], (((3,), (0,))...  28.9 us
    dot_general x3, matrix products, chunk_energies(): lax.dot_general(factors, blocks, (((0,), (0,)), ((), ())), preferred_elem...  26.1 us
    all_to_all x3, starting transfers between devices, per_device(): lax.all_to_all(product, 'occ', split_axis=0, concat_axis=0, tiled=True)  16.4 us
    add x2, other arithmetic, chunk_energies(): vir_chunk[None, :, None, None] + vir_blocks[None, None, :, :]  5.65 us
    dynamic_update_slice x2, local copies, waits for them, and re-layouts, per_device(): factors = lax.dynamic_update_slice(factors, got, (0, 0, bounds[c]))  5.21 us
  transfers between devices with their start and end apart: 3, of which 3 were waited for; matrix products, arithmetic and copies ran while one was open for 35% of the time, Pallas kernels for 0%

profile of v9, /device:TPU:13, one launch (start us, length us, event | category | flops | bytes accessed | tf_op | source)
XLA Modules:
  0.0 199.8 jit_solution(10401303738093176105)
XLA Ops:
  0.6 9.4 %fusion.21 = bf16[16,16,8,384]{3,2,1,0:T(8,128)(2,1)} fusion(bf16[2048,1536]{1,0:T(8,128)(2,1)} %param.7, bf16[16,128,2048]{2,1,0:T(8,128)(2,1)} %param.6), kind=kOutput, calls=%fused_computation.26 | convolution fusion | flops 3222011904 | bytes 11534336 | tf_op jit(solution)/shard_map/dot_general | solution.py:41
  10.1 6.6 %all-to-all-start = ((bf16[16,16,8,384]{3,2,1,0:T(8,128)(2,1)}), bf16[16,16,8,384]{3,2,1,0:T(8,128)(2,1)S(1)}, u32[]{:S(2)}, u32[]{:S(2)}) async-start(bf16[16,16,8,384]{3,2,1,0:T(8,128)(2,1)} %fusion.21), calls=%async_computation | async-start | bytes 3145728 | tf_op jit(solution)/shard_map/all_to_all | solution.py:83
  16.7 0.7 fusion.42
  22.5 2.6 %gather_fusion = bf16[8,16,2048]{2,0,1:T(8,128)(2,1)S(1)} fusion(bf16[16,128,2048]{2,1,0:T(8,128)(2,1)} %param.6, s32[1024]{0:T(1024)S(1)} %pad_clamp_fusion.1), kind=kCustom, calls=%fused_computation | custom fusion | bytes 1048608 | tf_op jit(solution)/shard_map/jit(_take)/gather | solution.py:48
  25.2 3.8 %fusion.15 = bf16[16,8,1536]{2,1,0:T(8,128)(2,1)S(1)} fusion(bf16[2048,1536]{1,0:T(8,128)(2,1)} %param.7, bf16[8,16,2048]{2,0,1:T(8,128)(2,1)S(1)} %gather_fusion, pred[128]{0:T(512)(128)(4,1)S(1)} %broadcast_in_dim.21), kind=kOutput, calls=%fused_computation.24 | convolution fusion | flops 805765120 | bytes 7209088 | tf_op jit(solution)/shard_map/dot_general | solution.py:49
  29.0 0.7 fusion.39
  30.7 10.0 %fusion.16 = bf16[16,16,8,768]{3,2,1,0:T(8,128)(2,1)S(1)} fusion(bf16[2048,1536]{1,0:T(8,128)(2,1)} %param.7, bf16[16,128,2048]{2,1,0:T(8,128)(2,1)} %param.6), kind=kOutput, calls=%fused_computation.25 | convolution fusion | flops 6444023808 | bytes 14680064 | tf_op jit(solution)/shard_map/dot_general | solution.py:41
  40.9 2.7 %pad_maximum_fusion = bf16[16,16,8,960]{3,2,1,0:T(8,128)(2,1)} fusion(bf16[16,16,8,192]{3,2,1,0:T(8,128)(2,1)S(1)} %broadcast_in_dim.43, bf16[16,16,8,768]{3,2,1,0:T(8,128)(2,1)S(1)} %fusion.16), kind=kLoop, calls=%fused_computation.17 | loop fusion | flops 7864320 | bytes 7864320 | tf_op jit(solution)/shard_map/concatenate | solution.py:79
  43.6 9.2 %all-to-all-done = bf16[16,16,8,384]{3,2,1,0:T(8,128)(2,1)S(1)} async-done(((bf16[16,16,8,384]{3,2,1,0:T(8,128)(2,1)}), bf16[16,16,8,384]{3,2,1,0:T(8,128)(2,1)S(1)}, u32[]{:S(2)}, u32[]{:S(2)}) %all-to-all-start) | async-done | bytes 1572896 | tf_op jit(solution)/shard_map/all_to_all | solution.py:83
  52.8 4.9 %all-to-all-start.1 = ((bf16[16,16,8,960]{3,2,1,0:T(8,128)(2,1)}), bf16[16,16,8,960]{3,2,1,0:T(8,128)(2,1)}, u32[]{:S(2)}, u32[]{:S(2)}) async-start(bf16[16,16,8,960]{3,2,1,0:T(8,128)(2,1)} %pad_maximum_fusion), calls=%async_computation.1 | async-start | bytes 8388608 | tf_op jit(solution)/shard_map/all_to_all | solution.py:83
  58.7 2.5 %broadcast_add_fusion.1 = (f32[384,8,192]{0,2,1:T(8,128)}, f32[384,8,192]{0,2,1:T(8,128)}) fusion(f32[384]{0:T(512)S(1)} %get-tuple-element.24, f32[8,192]{1,0:T(8,128)S(1)} %stack.47, f32[384]{0:T(512)S(1)} %get-tuple-element.25), kind=kLoop, calls=%fused_computation.34 | loop fusion | flops 1179648 | bytes 4727808 | tf_op jit(solution)/shard_map/add | solution.py:15
  61.2 3.1 %broadcast_add_fusion = f32[960,8,192]{0,2,1:T(8,128)} fusion(f32[8,192]{1,0:T(8,128)S(1)} %stack.47, f32[960]{0:T(1024)S(1)} %concatenate.7), kind=kLoop, calls=%fused_computation.21 | loop fusion | flops 1474560 | bytes 5908224 | tf_op jit(solution)/shard_map/add | solution.py:15
  64.3 9.4 %fusion.24 = bf16[16,16,8,384]{3,2,1,0:T(8,128)(2,1)} fusion(bf16[2048,1536]{1,0:T(8,128)(2,1)} %param.7, bf16[16,128,2048]{2,1,0:T(8,128)(2,1)} %param.6), kind=kOutput, calls=%fused_computation.27 | convolution fusion | flops 3222011904 | bytes 11534336 | tf_op jit(solution)/shard_map/dot_general | solution.py:41
  73.8 3.2 %pad.5 = bf16[256,8,1536]{2,1,0:T(8,128)(2,1)} pad(bf16[256,8,384]{2,1,0:T(8,128)(2,1)S(1)} %bitcast.80, bf16[]{:T(256)} %constant.44.clone.1), padding=0_0x0_0x0_1152 | pad | bytes 7864322 | tf_op jit(solution)/shard_map/jit(_pad)/pad | solution.py:90
  76.9 73.3 %all-to-all-done.1 = bf16[16,16,8,960]{3,2,1,0:T(8,128)(2,1)} async-done(((bf16[16,16,8,960]{3,2,1,0:T(8,128)(2,1)}), bf16[16,16,8,960]{3,2,1,0:T(8,128)(2,1)}, u32[]{:S(2)}, u32[]{:S(2)}) %all-to-all-start.1) | async-done | bytes 3932192 | tf_op jit(solution)/shard_map/all_to_all | solution.py:83
  150.2 4.9 %all-to-all-start.2 = ((bf16[16,16,8,384]{3,2,1,0:T(8,128)(2,1)}), bf16[16,16,8,384]{3,2,1,0:T(8,128)(2,1)S(1)}, u32[]{:S(2)}, u32[]{:S(2)}) async-start(bf16[16,16,8,384]{3,2,1,0:T(8,128)(2,1)} %fusion.24), calls=%async_computation.2 | async-start | bytes 3145728 | tf_op jit(solution)/shard_map/all_to_all | solution.py:83
  155.1 2.3 %slice.117 = bf16[256,8,192]{2,1,0:T(8,128)(2,1)} slice(bf16[256,8,960]{2,1,0:T(8,128)(2,1)} %bitcast.18), slice={[0:256], [0:8], [768:960]} | slice | bytes 1572864 | tf_op jit(solution)/shard_map/slice | solution.py:87
  157.4 2.6 %copy.30 = bf16[256,8,192]{0,2,1:T(8,128)(2,1)} copy(bf16[256,8,192]{2,1,0:T(8,128)(2,1)} %slice.117) | data formatting | bytes 1572864
  160.0 14.8 %fusion = f32[8,8]{1,0:T(8,128)S(1)} fusion(f32[8]{0:T(128)S(1)} %gather_fusion.1, f32[8]{0:T(128)S(1)} %dynamic_slice.67, f32[960,8,192]{0,2,1:T(8,128)} %broadcast_add_fusion, bf16[256,8,960,1]{2,1,0,3:T(8,128)(2,1)} %bitcast.32, bf16[256,8,192]{0,2,1:T(8,128)(2,1)} %copy.30), kind=kOutput, calls=%fused_computation.3 | convolution fusion | flops 6098780160 | bytes 10617152 | tf_op jit(solution)/shard_map/dot_general | solution.py:11
  174.9 3.9 %slice_dynamic-update-slice_fusion = bf16[256,8,1536]{2,1,0:T(8,128)(2,1)} fusion(bf16[256,8,1536]{2,1,0:T(8,128)(2,1)} %pad.5, bf16[256,8,960]{2,1,0:T(8,128)(2,1)} %bitcast.18), kind=kLoop, calls=%fused_computation.19 | loop fusion | bytes 6291456 | tf_op jit(solution)/shard_map/dynamic_update_slice | solution.py:92
  178.8 4.7 %fusion.1 = f32[8,8]{1,0:T(8,128)S(1)} fusion(f32[8]{0:T(128)S(1)} %gather_fusion.1, f32[8]{0:T(128)S(1)} %dynamic_slice.67, f32[384,8,192]{0,2,1:T(8,128)S(1)} %copy-done.1, bf16[256,8,384,1]{2,1,0,3:T(8,128)(2,1)S(1)} %bitcast.81, bf16[256,8,192]{0,2,1:T(8,128)(2,1)S(1)} %copy-done.2), kind=kOutput, calls=%fused_computation.6 | convolution fusion | flops 2439512064 | bytes 4718912 | tf_op jit(solution)/shard_map/dot_general | solution.py:11
  183.5 7.8 %all-to-all-done.2 = bf16[16,16,8,384]{3,2,1,0:T(8,128)(2,1)S(1)} async-done(((bf16[16,16,8,384]{3,2,1,0:T(8,128)(2,1)}), bf16[16,16,8,384]{3,2,1,0:T(8,128)(2,1)S(1)}, u32[]{:S(2)}, u32[]{:S(2)}) %all-to-all-start.2) | async-done | bytes 1572896 | tf_op jit(solution)/shard_map/all_to_all | solution.py:83
  191.3 1.3 constant_dynamic-update-slice_fusion
  192.6 6.6 %fusion.2 = f32[8,8]{1,0:T(8,128)S(1)} fusion(f32[384,8,192]{0,2,1:T(8,128)} %get-tuple-element.22, f32[8]{0:T(128)S(1)} %gather_fusion.1, f32[8]{0:T(128)S(1)} %dynamic_slice.67, bf16[256,8,384,1]{2,1,0,3:T(8,128)(2,1)S(1)} %bitcast.79, bf16[256,8,192]{0,2,1:T(8,128)(2,1)} %copy.30), kind=kOutput, calls=%fused_computation.7 | convolution fusion | flops 2439512064 | bytes 4718912 | tf_op jit(solution)/shard_map/dot_general | solution.py:11
  (36 shorter events, 2.7 us)
Async XLA Ops:
  0.6 21.7 %copy-start.5 = (s32[8]{0:T(128)S(1)}, s32[8]{0:T(128)}, u32[]{:S(2)}) copy-start(s32[8]{0:T(128)} %param.10) | copy-start | bytes 100
  0.6 16.0 %copy-start.4 = (s32[8]{0:T(128)S(1)}, s32[8]{0:T(128)}, u32[]{:S(2)}) copy-start(s32[8]{0:T(128)} %param.11) | copy-start | bytes 100
  10.1 42.7 %all-to-all-start = ((bf16[16,16,8,384]{3,2,1,0:T(8,128)(2,1)}), bf16[16,16,8,384]{3,2,1,0:T(8,128)(2,1)S(1)}, u32[]{:S(2)}, u32[]{:S(2)}) async-start(bf16[16,16,8,384]{3,2,1,0:T(8,128)(2,1)} %fusion.21), calls=%async_computation | async-start | bytes 3145728 | tf_op jit(solution)/shard_map/all_to_all | solution.py:83
  43.6 14.1 %copy-start.3 = (f32[1536]{0:T(1024)S(1)}, f32[1536]{0:T(1024)}, u32[]{:S(2)}) copy-start(f32[1536]{0:T(1024)} %param.9) | copy-start | bytes 18436
  43.6 14.2 %copy-start = (f32[128]{0:T(128)S(1)}, f32[128]{0:T(128)}, u32[]{:S(2)}) copy-start(f32[128]{0:T(128)} %param.8) | copy-start | bytes 1540
  52.8 97.4 %all-to-all-start.1 = ((bf16[16,16,8,960]{3,2,1,0:T(8,128)(2,1)}), bf16[16,16,8,960]{3,2,1,0:T(8,128)(2,1)}, u32[]{:S(2)}, u32[]{:S(2)}) async-start(bf16[16,16,8,960]{3,2,1,0:T(8,128)(2,1)} %pad_maximum_fusion), calls=%async_computation.1 | async-start | bytes 8388608 | tf_op jit(solution)/shard_map/all_to_all | solution.py:83
  150.2 41.1 %all-to-all-start.2 = ((bf16[16,16,8,384]{3,2,1,0:T(8,128)(2,1)}), bf16[16,16,8,384]{3,2,1,0:T(8,128)(2,1)S(1)}, u32[]{:S(2)}, u32[]{:S(2)}) async-start(bf16[16,16,8,384]{3,2,1,0:T(8,128)(2,1)} %fusion.24), calls=%async_computation.2 | async-start | bytes 3145728 | tf_op jit(solution)/shard_map/all_to_all | solution.py:83
  174.9 3.9 %copy-start.1 = (f32[384,8,192]{0,2,1:T(8,128)S(1)}, f32[384,8,192]{0,2,1:T(8,128)}, u32[]{:S(2)}) copy-start(f32[384,8,192]{0,2,1:T(8,128)} %get-tuple-element.23) | copy-start | bytes 7077892
  174.9 3.9 %copy-start.2 = (bf16[256,8,192]{0,2,1:T(8,128)(2,1)S(1)}, bf16[256,8,192]{0,2,1:T(8,128)(2,1)}, u32[]{:S(2)}) copy-start(bf16[256,8,192]{0,2,1:T(8,128)(2,1)} %copy.30) | copy-start | bytes 2359300

commit v10 on v9

--- a/solution.py
+++ b/solution.py
@@ -4,7 +4,7 @@
 from jax.sharding import PartitionSpec as P
 
 VBLK = 192
-EDGE_PART = 4
+EDGE_PART = 6
 
 
 def chunk_energies(factors, blocks, occ_rows, occ_cols, vir_chunk, vir_blocks, scale):

time: 200 us -> 208 us (1.040)
  waiting for transfers between devices: 90.3 us -> 98.4 us
    all_to_all x3, waiting for transfers between devices: 90.3 us -> 98.4 us  [per_device(): lax.all_to_all(product, 'occ', split_axis=0, concat_axis=0, tiled=True)]
    dot_general x3, matrix products: 28.9 us -> 26.4 us  [chunk_product(): lax.dot_general(rows, orbitals[:, bounds[c]:bounds[c + 1]], (((3,), (0,))...]
  transfers between devices with their start and end apart: 3 -> 3, of which waited for: 3 -> 1; matrix products, arithmetic and copies ran while one was open for 35% -> 34% of each run, Pallas kernels for 0% -> 0%
where the time goes in v10:
time: 208 us; the launch traced here: 207 us
  waiting for transfers between devices  98.4 us (47%)
  matrix products  58.3 us (28%)
  starting transfers between devices  17.6 us (8%)
  local copies, waits for them, and re-layouts  17.3 us (8%)
  other arithmetic  9.14 us (4%)
  between operations  5.95 us (3%)
    all_to_all x3, waiting for transfers between devices, per_device(): lax.all_to_all(product, 'occ', split_axis=0, concat_axis=0, tiled=True)  98.4 us
    dot_general x3, matrix products, chunk_energies(): lax.dot_general(factors, blocks, (((0,), (0,)), ((), ())), preferred_elem...  28 us
    dot_general x3, matrix products, chunk_product(): lax.dot_general(rows, orbitals[:, bounds[c]:bounds[c + 1]], (((3,), (0,))...  26.4 us
    all_to_all x3, starting transfers between devices, per_device(): lax.all_to_all(product, 'occ', split_axis=0, concat_axis=0, tiled=True)  17.6 us
    dynamic_update_slice x2, local copies, waits for them, and re-layouts, per_device(): factors = lax.dynamic_update_slice(factors, got, (0, 0, bounds[c]))  5.8 us
    add x2, other arithmetic, chunk_energies(): vir_chunk[None, :, None, None] + vir_blocks[None, None, :, :]  5.55 us
  transfers between devices with their start and end apart: 3, of which 1 were waited for; matrix products, arithmetic and copies ran while one was open for 34% of the time, Pallas kernels for 0%

profile of v10, /device:TPU:13, one launch (start us, length us, event | category | flops | bytes accessed | tf_op | source)
XLA Modules:
  0.0 206.6 jit_solution(136988580192996077)
XLA Ops:
  0.6 6.9 %fusion.21 = bf16[16,16,8,256]{3,2,1,0:T(8,128)(2,1)} fusion(bf16[2048,1536]{1,0:T(8,128)(2,1)} %param.7, bf16[16,128,2048]{2,1,0:T(8,128)(2,1)} %param.6), kind=kOutput, calls=%fused_computation.26 | convolution fusion | flops 2148007936 | bytes 10485760 | tf_op jit(solution)/shard_map/dot_general | solution.py:41
  7.6 6.6 %all-to-all-start = ((bf16[16,16,8,256]{3,2,1,0:T(8,128)(2,1)}), bf16[16,16,8,256]{3,2,1,0:T(8,128)(2,1)S(1)}, u32[]{:S(2)}, u32[]{:S(2)}) async-start(bf16[16,16,8,256]{3,2,1,0:T(8,128)(2,1)} %fusion.21), calls=%async_computation | async-start | bytes 2097152 | tf_op jit(solution)/shard_map/all_to_all | solution.py:83
  14.2 0.7 fusion.42
  19.9 2.6 %gather_fusion = bf16[8,16,2048]{2,0,1:T(8,128)(2,1)S(1)} fusion(bf16[16,128,2048]{2,1,0:T(8,128)(2,1)} %param.6, s32[1024]{0:T(1024)S(1)} %pad_clamp_fusion.1), kind=kCustom, calls=%fused_computation | custom fusion | bytes 1048608 | tf_op jit(solution)/shard_map/jit(_take)/gather | solution.py:48
  22.6 3.8 %fusion.20 = bf16[16,8,1536]{2,1,0:T(8,128)(2,1)S(1)} fusion(bf16[2048,1536]{1,0:T(8,128)(2,1)} %param.7, bf16[8,16,2048]{2,0,1:T(8,128)(2,1)S(1)} %gather_fusion, pred[128]{0:T(512)(128)(4,1)S(1)} %broadcast_in_dim.21), kind=kOutput, calls=%fused_computation.25 | convolution fusion | flops 805765120 | bytes 7209088 | tf_op jit(solution)/shard_map/dot_general | solution.py:49
  26.5 0.7 fusion.39
  28.3 12.5 %fusion.15 = bf16[16,16,8,1024]{3,2,1,0:T(8,128)(2,1)S(1)} fusion(bf16[2048,1536]{1,0:T(8,128)(2,1)} %param.7, bf16[16,128,2048]{2,1,0:T(8,128)(2,1)} %param.6), kind=kOutput, calls=%fused_computation.23 | convolution fusion | flops 8592031744 | bytes 16777216 | tf_op jit(solution)/shard_map/dot_general | solution.py:41
  40.9 3.0 %pad_maximum_fusion = bf16[16,16,8,1216]{3,2,1,0:T(8,128)(2,1)} fusion(bf16[16,16,8,192]{3,2,1,0:T(8,128)(2,1)S(1)} %broadcast_in_dim.43, bf16[16,16,8,1024]{3,2,1,0:T(8,128)(2,1)S(1)} %fusion.15), kind=kLoop, calls=%fused_computation.17 | loop fusion | flops 9961472 | bytes 9961472 | tf_op jit(solution)/shard_map/concatenate | solution.py:79
  43.9 6.1 %all-to-all-start.1 = ((bf16[16,16,8,1216]{3,2,1,0:T(8,128)(2,1)}), bf16[16,16,8,1216]{3,2,1,0:T(8,128)(2,1)}, u32[]{:S(2)}, u32[]{:S(2)}) async-start(bf16[16,16,8,1216]{3,2,1,0:T(8,128)(2,1)} %pad_maximum_fusion), calls=%async_computation.1 | async-start | bytes 10485760 | tf_op jit(solution)/shard_map/all_to_all | solution.py:83
  50.1 0.6 gather_fusion.1
  50.9 1.9 broadcast_add_fusion.1
  52.8 3.6 %broadcast_add_fusion = f32[1216,8,192]{0,2,1:T(8,128)} fusion(f32[8,192]{1,0:T(8,128)S(1)} %stack.47, f32[1216]{0:T(1024)S(1)} %concatenate.7), kind=kLoop, calls=%fused_computation.22 | loop fusion | flops 1867776 | bytes 7482112 | tf_op jit(solution)/shard_map/add | solution.py:15
  56.5 7.0 %fusion.24 = bf16[16,16,8,256]{3,2,1,0:T(8,128)(2,1)} fusion(bf16[2048,1536]{1,0:T(8,128)(2,1)} %param.7, bf16[16,128,2048]{2,1,0:T(8,128)(2,1)} %param.6), kind=kOutput, calls=%fused_computation.27 | convolution fusion | flops 2148007936 | bytes 10485760 | tf_op jit(solution)/shard_map/dot_general | solution.py:41
  63.4 3.1 %pad.5 = bf16[256,8,1536]{2,1,0:T(8,128)(2,1)} pad(bf16[256,8,256]{2,1,0:T(8,128)(2,1)S(1)} %bitcast.80, bf16[]{:T(256)} %constant.44.clone.1), padding=0_0x0_0x0_1280 | pad | bytes 7340034 | tf_op jit(solution)/shard_map/jit(_pad)/pad | solution.py:90
  66.6 98.4 %all-to-all-done.1 = bf16[16,16,8,1216]{3,2,1,0:T(8,128)(2,1)} async-done(((bf16[16,16,8,1216]{3,2,1,0:T(8,128)(2,1)}), bf16[16,16,8,1216]{3,2,1,0:T(8,128)(2,1)}, u32[]{:S(2)}, u32[]{:S(2)}) %all-to-all-start.1) | async-done | bytes 4980768 | tf_op jit(solution)/shard_map/all_to_all | solution.py:83
  164.9 1.3 slice.117
  166.2 1.0 copy.30
  167.2 4.9 %all-to-all-start.2 = ((bf16[16,16,8,256]{3,2,1,0:T(8,128)(2,1)}), bf16[16,16,8,256]{3,2,1,0:T(8,128)(2,1)S(1)}, u32[]{:S(2)}, u32[]{:S(2)}) async-start(bf16[16,16,8,256]{3,2,1,0:T(8,128)(2,1)} %fusion.24), calls=%async_computation.2 | async-start | bytes 2097152 | tf_op jit(solution)/shard_map/all_to_all | solution.py:83
  172.2 20.4 %fusion = f32[8,8]{1,0:T(8,128)S(1)} fusion(f32[8]{0:T(128)S(1)} %gather_fusion.1, f32[8]{0:T(128)S(1)} %dynamic_slice.67, f32[1216,8,192]{0,2,1:T(8,128)} %broadcast_add_fusion, bf16[256,8,1216,1]{2,1,0,3:T(8,128)(2,1)} %bitcast.32, bf16[256,8,192]{0,2,1:T(8,128)(2,1)S(1)} %copy.30), kind=kOutput, calls=%fused_computation.3 | convolution fusion | flops 7725121536 | bytes 13238592 | tf_op jit(solution)/shard_map/dot_general | solution.py:11
  192.6 4.8 %slice_dynamic-update-slice_fusion = bf16[256,8,1536]{2,1,0:T(8,128)(2,1)} fusion(bf16[256,8,1536]{2,1,0:T(8,128)(2,1)} %pad.5, bf16[256,8,1216]{2,1,0:T(8,128)(2,1)} %bitcast.18), kind=kLoop, calls=%fused_computation.19 | loop fusion | bytes 8388608 | tf_op jit(solution)/shard_map/dynamic_update_slice | solution.py:92
  197.4 3.3 %fusion.1 = f32[8,8]{1,0:T(8,128)S(1)} fusion(f32[8]{0:T(128)S(1)} %gather_fusion.1, f32[8]{0:T(128)S(1)} %dynamic_slice.67, f32[256,8,192]{0,2,1:T(8,128)S(1)} %copy-done.1, bf16[256,8,256,1]{2,1,0,3:T(8,128)(2,1)S(1)} %bitcast.81, bf16[256,8,192]{0,2,1:T(8,128)(2,1)S(1)} %copy.30), kind=kOutput, calls=%fused_computation.6 | convolution fusion | flops 1626341376 | bytes 3408192 | tf_op jit(solution)/shard_map/dot_general | solution.py:11
  200.7 1.0 constant_dynamic-update-slice_fusion
  201.7 4.3 %fusion.2 = f32[8,8]{1,0:T(8,128)S(1)} fusion(f32[256,8,192]{0,2,1:T(8,128)} %get-tuple-element.22, f32[8]{0:T(128)S(1)} %gather_fusion.1, f32[8]{0:T(128)S(1)} %dynamic_slice.67, bf16[256,8,256,1]{2,1,0,3:T(8,128)(2,1)S(1)} %bitcast.79, bf16[256,8,192]{0,2,1:T(8,128)(2,1)S(1)} %copy.30), kind=kOutput, calls=%fused_computation.7 | convolution fusion | flops 1626341376 | bytes 3408192 | tf_op jit(solution)/shard_map/dot_general | solution.py:11
  206.0 0.6 negate_multiply_fusion
  (34 shorter events, 1.4 us)
Async XLA Ops:
  0.6 13.5 %copy-start.4 = (s32[8]{0:T(128)S(1)}, s32[8]{0:T(128)}, u32[]{:S(2)}) copy-start(s32[8]{0:T(128)} %param.10) | copy-start | bytes 100
  0.6 13.5 %copy-start.2 = (s32[8]{0:T(128)S(1)}, s32[8]{0:T(128)}, u32[]{:S(2)}) copy-start(s32[8]{0:T(128)} %param.11) | copy-start | bytes 100
  7.6 36.3 %all-to-all-start = ((bf16[16,16,8,256]{3,2,1,0:T(8,128)(2,1)}), bf16[16,16,8,256]{3,2,1,0:T(8,128)(2,1)S(1)}, u32[]{:S(2)}, u32[]{:S(2)}) async-start(bf16[16,16,8,256]{3,2,1,0:T(8,128)(2,1)} %fusion.21), calls=%async_computation | async-start | bytes 2097152 | tf_op jit(solution)/shard_map/all_to_all | solution.py:83
  43.8 6.2 %copy-start.3 = (f32[1536]{0:T(1024)S(1)}, f32[1536]{0:T(1024)}, u32[]{:S(2)}) copy-start(f32[1536]{0:T(1024)} %param.9) | copy-start | bytes 18436
  43.8 6.2 %copy-start = (f32[128]{0:T(128)S(1)}, f32[128]{0:T(128)}, u32[]{:S(2)}) copy-start(f32[128]{0:T(128)} %param.8) | copy-start | bytes 1540
  43.9 121.1 %all-to-all-start.1 = ((bf16[16,16,8,1216]{3,2,1,0:T(8,128)(2,1)}), bf16[16,16,8,1216]{3,2,1,0:T(8,128)(2,1)}, u32[]{:S(2)}, u32[]{:S(2)}) async-start(bf16[16,16,8,1216]{3,2,1,0:T(8,128)(2,1)} %pad_maximum_fusion), calls=%async_computation.1 | async-start | bytes 10485760 | tf_op jit(solution)/shard_map/all_to_all | solution.py:83
  167.2 33.4 %all-to-all-start.2 = ((bf16[16,16,8,256]{3,2,1,0:T(8,128)(2,1)}), bf16[16,16,8,256]{3,2,1,0:T(8,128)(2,1)S(1)}, u32[]{:S(2)}, u32[]{:S(2)}) async-start(bf16[16,16,8,256]{3,2,1,0:T(8,128)(2,1)} %fusion.24), calls=%async_computation.2 | async-start | bytes 2097152 | tf_op jit(solution)/shard_map/all_to_all | solution.py:83
  192.6 4.8 %copy-start.1 = (f32[256,8,192]{0,2,1:T(8,128)S(1)}, f32[256,8,192]{0,2,1:T(8,128)}, u32[]{:S(2)}) copy-start(f32[256,8,192]{0,2,1:T(8,128)} %get-tuple-element.23) | copy-start | bytes 4718596

commit v11 on v9

--- a/solution.py
+++ b/solution.py
@@ -11,12 +11,9 @@
     coulomb = lax.dot_general(
         factors, blocks, (((0,), (0,)), ((), ())), preferred_element_type=jnp.float32
     )
-    denom = (
-        vir_chunk[None, :, None, None]
-        + vir_blocks[None, None, :, :]
-        - occ_rows[:, None, None, None]
-        - occ_cols[None, None, :, None]
-    )
+    rows_part = vir_chunk[None, :] - occ_rows[:, None]
+    cols_part = vir_blocks - occ_cols[:, None]
+    denom = rows_part[:, :, None, None] + cols_part[None, None, :, :]
     return jnp.sum(coulomb * coulomb / denom, axis=(1, 3))
 
 

time: 200 us -> 198 us (0.990)
  other arithmetic: 8.97 us -> 3.46 us
  waiting for transfers between devices: 90.3 us -> 94.2 us
    add x2 -> x0, other arithmetic: 5.65 us -> none  [chunk_energies(): vir_chunk[None, :, None, None] + vir_blocks[None, None, :, :]]
    all_to_all x3, waiting for transfers between devices: 90.3 us -> 94.2 us  [per_device(): lax.all_to_all(product, 'occ', split_axis=0, concat_axis=0, tiled=True)]
  transfers between devices with their start and end apart: 3 -> 3, of which waited for: 3 -> 3; matrix products, arithmetic and copies ran while one was open for 35% -> 33% of each run, Pallas kernels for 0% -> 0%
where the time goes in v11:
time: 198 us; the launch traced here: 197 us
  waiting for transfers between devices  94.2 us (48%)
  matrix products  58.1 us (29%)
  local copies, waits for them, and re-layouts  19.3 us (10%)
  starting transfers between devices  16.4 us (8%)
  between operations  5.89 us (3%)
  other arithmetic  3.46 us (2%)
    all_to_all x3, waiting for transfers between devices, per_device(): lax.all_to_all(product, 'occ', split_axis=0, concat_axis=0, tiled=True)  94.2 us
    dot_general x3, matrix products, chunk_product(): lax.dot_general(rows, orbitals[:, bounds[c]:bounds[c + 1]], (((3,), (0,))...  29 us
    dot_general x3, matrix products, chunk_energies(): lax.dot_general(factors, blocks, (((0,), (0,)), ((), ())), preferred_elem...  25.3 us
    all_to_all x3, starting transfers between devices, per_device(): lax.all_to_all(product, 'occ', split_axis=0, concat_axis=0, tiled=True)  16.4 us
    dynamic_update_slice x2, local copies, waits for them, and re-layouts, per_device(): factors = lax.dynamic_update_slice(factors, got, (0, 0, bounds[c]))  5.13 us
  transfers between devices with their start and end apart: 3, of which 3 were waited for; matrix products, arithmetic and copies ran while one was open for 33% of the time, Pallas kernels for 0%

profile of v11, /device:TPU:13, one launch (start us, length us, event | category | flops | bytes accessed | tf_op | source)
XLA Modules:
  0.0 197.3 jit_solution(8760700567116603394)
XLA Ops:
  0.6 9.4 %fusion.21 = bf16[16,16,8,384]{3,2,1,0:T(8,128)(2,1)} fusion(bf16[2048,1536]{1,0:T(8,128)(2,1)} %param.7, bf16[16,128,2048]{2,1,0:T(8,128)(2,1)} %param.6), kind=kOutput, calls=%fused_computation.25 | convolution fusion | flops 3222011904 | bytes 11534336 | tf_op jit(solution)/shard_map/dot_general | solution.py:38
  10.1 6.6 %all-to-all-start = ((bf16[16,16,8,384]{3,2,1,0:T(8,128)(2,1)}), bf16[16,16,8,384]{3,2,1,0:T(8,128)(2,1)S(1)}, u32[]{:S(2)}, u32[]{:S(2)}) async-start(bf16[16,16,8,384]{3,2,1,0:T(8,128)(2,1)} %fusion.21), calls=%async_computation | async-start | bytes 3145728 | tf_op jit(solution)/shard_map/all_to_all | solution.py:80
  16.7 0.7 fusion.42
  22.5 2.6 %gather_fusion = bf16[8,16,2048]{2,0,1:T(8,128)(2,1)S(1)} fusion(bf16[16,128,2048]{2,1,0:T(8,128)(2,1)} %param.6, s32[1024]{0:T(1024)S(1)} %pad_clamp_fusion.1), kind=kCustom, calls=%fused_computation | custom fusion | bytes 1048608 | tf_op jit(solution)/shard_map/jit(_take)/gather | solution.py:45
  25.2 3.8 %fusion.15 = bf16[16,8,1536]{2,1,0:T(8,128)(2,1)S(1)} fusion(bf16[2048,1536]{1,0:T(8,128)(2,1)} %param.7, bf16[8,16,2048]{2,0,1:T(8,128)(2,1)S(1)} %gather_fusion, pred[128]{0:T(512)(128)(4,1)S(1)} %broadcast_in_dim.21), kind=kOutput, calls=%fused_computation.23 | convolution fusion | flops 805765120 | bytes 7209088 | tf_op jit(solution)/shard_map/dot_general | solution.py:46
  29.0 0.7 fusion.39
  30.7 10.0 %fusion.16 = bf16[16,16,8,768]{3,2,1,0:T(8,128)(2,1)S(1)} fusion(bf16[2048,1536]{1,0:T(8,128)(2,1)} %param.7, bf16[16,128,2048]{2,1,0:T(8,128)(2,1)} %param.6), kind=kOutput, calls=%fused_computation.24 | convolution fusion | flops 6444023808 | bytes 14680064 | tf_op jit(solution)/shard_map/dot_general | solution.py:38
  40.9 2.6 %pad_maximum_fusion = bf16[16,16,8,960]{3,2,1,0:T(8,128)(2,1)} fusion(bf16[16,16,8,192]{3,2,1,0:T(8,128)(2,1)S(1)} %broadcast_in_dim.25, bf16[16,16,8,768]{3,2,1,0:T(8,128)(2,1)S(1)} %fusion.16), kind=kLoop, calls=%fused_computation.17 | loop fusion | flops 7864320 | bytes 7864320 | tf_op jit(solution)/shard_map/concatenate | solution.py:76
  43.5 9.3 %all-to-all-done = bf16[16,16,8,384]{3,2,1,0:T(8,128)(2,1)S(1)} async-done(((bf16[16,16,8,384]{3,2,1,0:T(8,128)(2,1)}), bf16[16,16,8,384]{3,2,1,0:T(8,128)(2,1)S(1)}, u32[]{:S(2)}, u32[]{:S(2)}) %all-to-all-start) | async-done | bytes 1572896 | tf_op jit(solution)/shard_map/all_to_all | solution.py:80
  52.8 4.9 %all-to-all-start.1 = ((bf16[16,16,8,960]{3,2,1,0:T(8,128)(2,1)}), bf16[16,16,8,960]{3,2,1,0:T(8,128)(2,1)}, u32[]{:S(2)}, u32[]{:S(2)}) async-start(bf16[16,16,8,960]{3,2,1,0:T(8,128)(2,1)} %pad_maximum_fusion), calls=%async_computation.1 | async-start | bytes 8388608 | tf_op jit(solution)/shard_map/all_to_all | solution.py:80
  57.9 0.6 gather_fusion.1
  58.9 9.5 %fusion.24 = bf16[16,16,8,384]{3,2,1,0:T(8,128)(2,1)} fusion(bf16[2048,1536]{1,0:T(8,128)(2,1)} %param.7, bf16[16,128,2048]{2,1,0:T(8,128)(2,1)} %param.6), kind=kOutput, calls=%fused_computation.26 | convolution fusion | flops 3222011904 | bytes 11534336 | tf_op jit(solution)/shard_map/dot_general | solution.py:38
  68.4 3.2 %pad.5 = bf16[256,8,1536]{2,1,0:T(8,128)(2,1)} pad(bf16[256,8,384]{2,1,0:T(8,128)(2,1)S(1)} %bitcast.80, bf16[]{:T(256)} %constant.44.clone.1), padding=0_0x0_0x0_1152 | pad | bytes 7864322 | tf_op jit(solution)/shard_map/jit(_pad)/pad | solution.py:87
  71.5 78.7 %all-to-all-done.1 = bf16[16,16,8,960]{3,2,1,0:T(8,128)(2,1)} async-done(((bf16[16,16,8,960]{3,2,1,0:T(8,128)(2,1)}), bf16[16,16,8,960]{3,2,1,0:T(8,128)(2,1)}, u32[]{:S(2)}, u32[]{:S(2)}) %all-to-all-start.1) | async-done | bytes 3932192 | tf_op jit(solution)/shard_map/all_to_all | solution.py:80
  150.2 4.9 %all-to-all-start.2 = ((bf16[16,16,8,384]{3,2,1,0:T(8,128)(2,1)}), bf16[16,16,8,384]{3,2,1,0:T(8,128)(2,1)S(1)}, u32[]{:S(2)}, u32[]{:S(2)}) async-start(bf16[16,16,8,384]{3,2,1,0:T(8,128)(2,1)} %fusion.24), calls=%async_computation.2 | async-start | bytes 3145728 | tf_op jit(solution)/shard_map/all_to_all | solution.py:80
  155.1 2.3 %slice.117 = bf16[256,8,192]{2,1,0:T(8,128)(2,1)} slice(bf16[256,8,960]{2,1,0:T(8,128)(2,1)} %bitcast.18), slice={[0:256], [0:8], [768:960]} | slice | bytes 1572864 | tf_op jit(solution)/shard_map/slice | solution.py:84
  157.4 2.7 %copy.30 = bf16[256,8,192]{0,2,1:T(8,128)(2,1)} copy(bf16[256,8,192]{2,1,0:T(8,128)(2,1)} %slice.117) | data formatting | bytes 1572864
  160.0 3.8 %slice_dynamic-update-slice_fusion = bf16[256,8,1536]{2,1,0:T(8,128)(2,1)} fusion(bf16[256,8,1536]{2,1,0:T(8,128)(2,1)} %pad.5, bf16[256,8,960]{2,1,0:T(8,128)(2,1)} %bitcast.18), kind=kLoop, calls=%fused_computation.19 | loop fusion | bytes 6291456 | tf_op jit(solution)/shard_map/dynamic_update_slice | solution.py:89
  163.9 4.1 %fusion.1 = f32[8,8]{1,0:T(8,128)S(1)} fusion(f32[8,192]{1,0:T(8,128)S(1)} %broadcast_subtract_fusion.3, f32[8,384]{1,0:T(8,128)S(1)} %get-tuple-element.33, bf16[256,8,384,1]{2,1,0,3:T(8,128)(2,1)S(1)} %bitcast.81, bf16[256,8,192]{0,2,1:T(8,128)(2,1)S(1)} %copy-done.1), kind=kOutput, calls=%fused_computation.6 | convolution fusion | flops 2434793472 | bytes 2377984 | tf_op jit(solution)/shard_map/dot_general | solution.py:11
  168.0 17.1 %fusion = f32[8,8]{1,0:T(8,128)S(1)} fusion(f32[8,192]{1,0:T(8,128)S(1)} %broadcast_subtract_fusion.3, f32[8,960]{1,0:T(8,128)S(1)} %broadcast_subtract_fusion, bf16[256,8,960,1]{2,1,0,3:T(8,128)(2,1)} %bitcast.32, bf16[256,8,192]{0,2,1:T(8,128)(2,1)S(1)} %copy-done.1), kind=kOutput, calls=%fused_computation.3 | convolution fusion | flops 6086983680 | bytes 4755712 | tf_op jit(solution)/shard_map/dot_general | solution.py:11
  185.1 6.2 %all-to-all-done.2 = bf16[16,16,8,384]{3,2,1,0:T(8,128)(2,1)S(1)} async-done(((bf16[16,16,8,384]{3,2,1,0:T(8,128)(2,1)}), bf16[16,16,8,384]{3,2,1,0:T(8,128)(2,1)S(1)}, u32[]{:S(2)}, u32[]{:S(2)}) %all-to-all-start.2) | async-done | bytes 1572896 | tf_op jit(solution)/shard_map/all_to_all | solution.py:80
  191.3 1.3 constant_dynamic-update-slice_fusion
  192.6 4.1 %fusion.2 = f32[8,8]{1,0:T(8,128)S(1)} fusion(f32[8,384]{1,0:T(8,128)S(1)} %get-tuple-element.32, f32[8,192]{1,0:T(8,128)S(1)} %broadcast_subtract_fusion.3, bf16[256,8,384,1]{2,1,0,3:T(8,128)(2,1)S(1)} %bitcast.79, bf16[256,8,192]{0,2,1:T(8,128)(2,1)S(1)} %copy-done.2), kind=kOutput, calls=%fused_computation.7 | convolution fusion | flops 2434793472 | bytes 2377984 | tf_op jit(solution)/shard_map/dot_general | solution.py:11
  196.7 0.6 negate_multiply_fusion
  (37 shorter events, 1.7 us)
Async XLA Ops:
  0.6 21.7 %copy-start.5 = (s32[8]{0:T(128)S(1)}, s32[8]{0:T(128)}, u32[]{:S(2)}) copy-start(s32[8]{0:T(128)} %param.10) | copy-start | bytes 100
  0.6 16.0 %copy-start.4 = (s32[8]{0:T(128)S(1)}, s32[8]{0:T(128)}, u32[]{:S(2)}) copy-start(s32[8]{0:T(128)} %param.11) | copy-start | bytes 100
  10.1 42.7 %all-to-all-start = ((bf16[16,16,8,384]{3,2,1,0:T(8,128)(2,1)}), bf16[16,16,8,384]{3,2,1,0:T(8,128)(2,1)S(1)}, u32[]{:S(2)}, u32[]{:S(2)}) async-start(bf16[16,16,8,384]{3,2,1,0:T(8,128)(2,1)} %fusion.21), calls=%async_computation | async-start | bytes 3145728 | tf_op jit(solution)/shard_map/all_to_all | solution.py:80
  43.5 14.2 %copy-start.3 = (f32[1536]{0:T(1024)S(1)}, f32[1536]{0:T(1024)}, u32[]{:S(2)}) copy-start(f32[1536]{0:T(1024)} %param.9) | copy-start | bytes 18436
  43.5 14.2 %copy-start = (f32[128]{0:T(128)S(1)}, f32[128]{0:T(128)}, u32[]{:S(2)}) copy-start(f32[128]{0:T(128)} %param.8) | copy-start | bytes 1540
  52.8 97.4 %all-to-all-start.1 = ((bf16[16,16,8,960]{3,2,1,0:T(8,128)(2,1)}), bf16[16,16,8,960]{3,2,1,0:T(8,128)(2,1)}, u32[]{:S(2)}, u32[]{:S(2)}) async-start(bf16[16,16,8,960]{3,2,1,0:T(8,128)(2,1)} %pad_maximum_fusion), calls=%async_computation.1 | async-start | bytes 8388608 | tf_op jit(solution)/shard_map/all_to_all | solution.py:80
  150.2 41.1 %all-to-all-start.2 = ((bf16[16,16,8,384]{3,2,1,0:T(8,128)(2,1)}), bf16[16,16,8,384]{3,2,1,0:T(8,128)(2,1)S(1)}, u32[]{:S(2)}, u32[]{:S(2)}) async-start(bf16[16,16,8,384]{3,2,1,0:T(8,128)(2,1)} %fusion.24), calls=%async_computation.2 | async-start | bytes 3145728 | tf_op jit(solution)/shard_map/all_to_all | solution.py:80
  160.0 3.8 %copy-start.1 = (bf16[256,8,192]{0,2,1:T(8,128)(2,1)S(1)}, bf16[256,8,192]{0,2,1:T(8,128)(2,1)}, u32[]{:S(2)}) copy-start(bf16[256,8,192]{0,2,1:T(8,128)(2,1)} %copy.30) | copy-start | bytes 2359300
  168.0 24.6 %copy-start.2 = (bf16[256,8,192]{0,2,1:T(8,128)(2,1)S(1)}, bf16[256,8,192]{0,2,1:T(8,128)(2,1)}, u32[]{:S(2)}) copy-start(bf16[256,8,192]{0,2,1:T(8,128)(2,1)} %copy.30) | copy-start | bytes 2359300

commit v12 on v11

--- a/solution.py
+++ b/solution.py
@@ -5,6 +5,7 @@
 
 VBLK = 192
 EDGE_PART = 4
+LEAD_PART = 6
 
 
 def chunk_energies(factors, blocks, occ_rows, occ_cols, vir_chunk, vir_blocks, scale):
@@ -25,8 +26,9 @@
     local_count = occ_total // groups
     tiles = nvir // 128 if nvir % 128 == 0 else 0
     edge = tiles // EDGE_PART
-    if edge >= 1 and tiles - 2 * edge >= 1:
-        bounds = [0, edge * 128, nvir - edge * 128, nvir]
+    lead = tiles // LEAD_PART
+    if edge >= 1 and lead >= 1 and tiles - edge - lead >= 1:
+        bounds = [0, lead * 128, nvir - edge * 128, nvir]
     else:
         bounds = [0, nvir]
     chunks = len(bounds) - 1

time: 198 us -> 201 us (1.015)
  waiting for transfers between devices: 94.2 us -> 100 us
  matrix products: 58.1 us -> 54.7 us
    all_to_all x3, waiting for transfers between devices: 94.2 us -> 100 us  [per_device(): lax.all_to_all(product, 'occ', split_axis=0, concat_axis=0, tiled=True)]
    dot_general x3, matrix products: 25.3 us -> 22.1 us  [chunk_energies(): lax.dot_general(factors, blocks, (((0,), (0,)), ((), ())), preferred_elem...]
  transfers between devices with their start and end apart: 3 -> 3, of which waited for: 3 -> 2; matrix products, arithmetic and copies ran while one was open for 33% -> 30% of each run, Pallas kernels for 0% -> 0%
where the time goes in v12:
time: 201 us; the launch traced here: 200 us
  waiting for transfers between devices  100 us (50%)
  matrix products  54.7 us (27%)
  local copies, waits for them, and re-layouts  18.2 us (9%)
  starting transfers between devices  17.6 us (9%)
  between operations  5.92 us (3%)
  other arithmetic  3.64 us (2%)
    all_to_all x3, waiting for transfers between devices, per_device(): lax.all_to_all(product, 'occ', split_axis=0, concat_axis=0, tiled=True)  100 us
    dot_general x3, matrix products, chunk_product(): lax.dot_general(rows, orbitals[:, bounds[c]:bounds[c + 1]], (((3,), (0,))...  28.7 us
    dot_general x3, matrix products, chunk_energies(): lax.dot_general(factors, blocks, (((0,), (0,)), ((), ())), preferred_elem...  22.1 us
    all_to_all x3, starting transfers between devices, per_device(): lax.all_to_all(product, 'occ', split_axis=0, concat_axis=0, tiled=True)  17.6 us
  transfers between devices with their start and end apart: 3, of which 2 were waited for; matrix products, arithmetic and copies ran while one was open for 30% of the time, Pallas kernels for 0%

profile of v12, /device:TPU:13, one launch (start us, length us, event | category | flops | bytes accessed | tf_op | source)
XLA Modules:
  0.0 200.4 jit_solution(16720711098783035175)
XLA Ops:
  0.6 6.9 %fusion.27 = bf16[16,16,8,256]{3,2,1,0:T(8,128)(2,1)} fusion(bf16[2048,1536]{1,0:T(8,128)(2,1)} %param.7, bf16[16,128,2048]{2,1,0:T(8,128)(2,1)} %param.6), kind=kOutput, calls=%fused_computation.29 | convolution fusion | flops 2148007936 | bytes 10485760 | tf_op jit(solution)/shard_map/dot_general | solution.py:40
  7.6 6.6 %all-to-all-start = ((bf16[16,16,8,256]{3,2,1,0:T(8,128)(2,1)}), bf16[16,16,8,256]{3,2,1,0:T(8,128)(2,1)S(1)}, u32[]{:S(2)}, u32[]{:S(2)}) async-start(bf16[16,16,8,256]{3,2,1,0:T(8,128)(2,1)} %fusion.27), calls=%async_computation | async-start | bytes 2097152 | tf_op jit(solution)/shard_map/all_to_all | solution.py:82
  14.1 0.7 fusion.41
  20.0 2.6 %gather_fusion = bf16[8,16,2048]{2,0,1:T(8,128)(2,1)S(1)} fusion(bf16[16,128,2048]{2,1,0:T(8,128)(2,1)} %param.6, s32[1024]{0:T(1024)S(1)} %pad_clamp_fusion.1), kind=kCustom, calls=%fused_computation | custom fusion | bytes 1048608 | tf_op jit(solution)/shard_map/jit(_take)/gather | solution.py:47
  22.6 3.8 %fusion.20 = bf16[16,8,1536]{2,1,0:T(8,128)(2,1)S(1)} fusion(bf16[2048,1536]{1,0:T(8,128)(2,1)} %param.7, bf16[8,16,2048]{2,0,1:T(8,128)(2,1)S(1)} %gather_fusion, pred[128]{0:T(512)(128)(4,1)S(1)} %broadcast_in_dim.21), kind=kOutput, calls=%fused_computation.24 | convolution fusion | flops 805765120 | bytes 7209088 | tf_op jit(solution)/shard_map/dot_general | solution.py:48
  26.4 0.7 fusion.39
  28.2 12.3 %fusion.15 = bf16[16,16,8,896]{3,2,1,0:T(8,128)(2,1)S(1)} fusion(bf16[2048,1536]{1,0:T(8,128)(2,1)} %param.7, bf16[16,128,2048]{2,1,0:T(8,128)(2,1)} %param.6), kind=kOutput, calls=%fused_computation.22 | convolution fusion | flops 7518027776 | bytes 15728640 | tf_op jit(solution)/shard_map/dot_general | solution.py:40
  40.7 2.7 %pad_maximum_fusion = bf16[16,16,8,1088]{3,2,1,0:T(8,128)(2,1)} fusion(bf16[16,16,8,192]{3,2,1,0:T(8,128)(2,1)S(1)} %broadcast_in_dim.25, bf16[16,16,8,896]{3,2,1,0:T(8,128)(2,1)S(1)} %fusion.15), kind=kLoop, calls=%fused_computation.17 | loop fusion | flops 8912896 | bytes 8912896 | tf_op jit(solution)/shard_map/concatenate | solution.py:78
  43.4 6.2 %all-to-all-start.1 = ((bf16[16,16,8,1088]{3,2,1,0:T(8,128)(2,1)}), bf16[16,16,8,1088]{3,2,1,0:T(8,128)(2,1)}, u32[]{:S(2)}, u32[]{:S(2)}) async-start(bf16[16,16,8,1088]{3,2,1,0:T(8,128)(2,1)} %pad_maximum_fusion), calls=%async_computation.1 | async-start | bytes 9437184 | tf_op jit(solution)/shard_map/all_to_all | solution.py:82
  49.7 0.6 gather_fusion.1
  50.8 9.4 %fusion.21 = bf16[16,16,8,384]{3,2,1,0:T(8,128)(2,1)} fusion(bf16[2048,1536]{1,0:T(8,128)(2,1)} %param.7, bf16[16,128,2048]{2,1,0:T(8,128)(2,1)} %param.6), kind=kOutput, calls=%fused_computation.25 | convolution fusion | flops 3222011904 | bytes 11534336 | tf_op jit(solution)/shard_map/dot_general | solution.py:40
  60.2 3.1 %pad.5 = bf16[256,8,1536]{2,1,0:T(8,128)(2,1)} pad(bf16[256,8,256]{2,1,0:T(8,128)(2,1)S(1)} %bitcast.80, bf16[]{:T(256)} %constant.44.clone.1), padding=0_0x0_0x0_1280 | pad | bytes 7340034 | tf_op jit(solution)/shard_map/jit(_pad)/pad | solution.py:89
  63.3 89.9 %all-to-all-done.1 = bf16[16,16,8,1088]{3,2,1,0:T(8,128)(2,1)} async-done(((bf16[16,16,8,1088]{3,2,1,0:T(8,128)(2,1)}), bf16[16,16,8,1088]{3,2,1,0:T(8,128)(2,1)}, u32[]{:S(2)}, u32[]{:S(2)}) %all-to-all-start.1) | async-done | bytes 4456480 | tf_op jit(solution)/shard_map/all_to_all | solution.py:82
  153.3 4.9 %all-to-all-start.2 = ((bf16[16,16,8,384]{3,2,1,0:T(8,128)(2,1)}), bf16[16,16,8,384]{3,2,1,0:T(8,128)(2,1)S(1)}, u32[]{:S(2)}, u32[]{:S(2)}) async-start(bf16[16,16,8,384]{3,2,1,0:T(8,128)(2,1)} %fusion.21), calls=%async_computation.2 | async-start | bytes 3145728 | tf_op jit(solution)/shard_map/all_to_all | solution.py:82
  158.2 1.3 slice.117
  159.5 1.0 copy.30
  160.5 15.0 %fusion = f32[8,8]{1,0:T(8,128)S(1)} fusion(f32[8,192]{1,0:T(8,128)S(1)} %broadcast_subtract_fusion.2, f32[8,1088]{1,0:T(8,128)S(1)} %broadcast_subtract_fusion, bf16[256,8,1088,1]{2,1,0,3:T(8,128)(2,1)} %bitcast.32, bf16[256,8,192]{0,2,1:T(8,128)(2,1)S(1)} %copy.30), kind=kOutput, calls=%fused_computation.3 | convolution fusion | flops 6898581504 | bytes 5284096 | tf_op jit(solution)/shard_map/dot_general | solution.py:12
  175.5 2.7 %slice_dynamic-update-slice_fusion = bf16[256,8,1536]{2,1,0:T(8,128)(2,1)S(1)} fusion(bf16[256,8,1536]{2,1,0:T(8,128)(2,1)S(1)} %copy-done.1, bf16[256,8,1088]{2,1,0:T(8,128)(2,1)} %bitcast.18), kind=kLoop, calls=%fused_computation.19 | loop fusion | bytes 7340032 | tf_op jit(solution)/shard_map/dynamic_update_slice | solution.py:91
  178.3 2.7 %copy-done.2 = bf16[256,8,1536]{2,1,0:T(8,128)(2,1)} copy-done((bf16[256,8,1536]{2,1,0:T(8,128)(2,1)}, bf16[256,8,1536]{2,1,0:T(8,128)(2,1)S(1)}, u32[]{:S(2)}) %copy-start.2) | copy-done | bytes 6291480
  181.0 3.0 %fusion.2 = f32[8,8]{1,0:T(8,128)S(1)} fusion(f32[8,192]{1,0:T(8,128)S(1)} %broadcast_subtract_fusion.2, f32[8,256]{1,0:T(8,128)S(1)} %broadcast_subtract_fusion.3, bf16[256,8,256,1]{2,1,0,3:T(8,128)(2,1)S(1)} %bitcast.81, bf16[256,8,192]{0,2,1:T(8,128)(2,1)S(1)} %copy.30), kind=kOutput, calls=%fused_computation.7 | convolution fusion | flops 1623195648 | bytes 1849600 | tf_op jit(solution)/shard_map/dot_general | solution.py:12
  184.0 10.4 %all-to-all-done.2 = bf16[16,16,8,384]{3,2,1,0:T(8,128)(2,1)S(1)} async-done(((bf16[16,16,8,384]{3,2,1,0:T(8,128)(2,1)}), bf16[16,16,8,384]{3,2,1,0:T(8,128)(2,1)S(1)}, u32[]{:S(2)}, u32[]{:S(2)}) %all-to-all-start.2) | async-done | bytes 1572896 | tf_op jit(solution)/shard_map/all_to_all | solution.py:82
  194.4 1.3 constant_dynamic-update-slice_fusion
  195.7 4.1 %fusion.1 = f32[8,8]{1,0:T(8,128)S(1)} fusion(f32[8,192]{1,0:T(8,128)S(1)} %broadcast_subtract_fusion.2, f32[8,384]{1,0:T(8,128)S(1)} %broadcast_subtract_fusion.1, bf16[256,8,384,1]{2,1,0,3:T(8,128)(2,1)S(1)} %bitcast.79, bf16[256,8,192]{0,2,1:T(8,128)(2,1)S(1)} %copy.30), kind=kOutput, calls=%fused_computation.5 | convolution fusion | flops 2434793472 | bytes 2377984 | tf_op jit(solution)/shard_map/dot_general | solution.py:12
  199.8 0.6 negate_multiply_fusion
  (44 shorter events, 1.8 us)
Async XLA Ops:
  0.6 19.2 %copy-start.7 = (s32[8]{0:T(128)S(1)}, s32[8]{0:T(128)}, u32[]{:S(2)}) copy-start(s32[8]{0:T(128)} %param.10) | copy-start | bytes 100
  0.6 13.5 %copy-start.5 = (s32[8]{0:T(128)S(1)}, s32[8]{0:T(128)}, u32[]{:S(2)}) copy-start(s32[8]{0:T(128)} %param.11) | copy-start | bytes 100
  7.6 35.8 %all-to-all-start = ((bf16[16,16,8,256]{3,2,1,0:T(8,128)(2,1)}), bf16[16,16,8,256]{3,2,1,0:T(8,128)(2,1)S(1)}, u32[]{:S(2)}, u32[]{:S(2)}) async-start(bf16[16,16,8,256]{3,2,1,0:T(8,128)(2,1)} %fusion.27), calls=%async_computation | async-start | bytes 2097152 | tf_op jit(solution)/shard_map/all_to_all | solution.py:82
  43.4 6.2 %copy-start.6 = (f32[1536]{0:T(1024)S(1)}, f32[1536]{0:T(1024)}, u32[]{:S(2)}) copy-start(f32[1536]{0:T(1024)} %param.9) | copy-start | bytes 18436
  43.4 6.2 %copy-start = (f32[128]{0:T(128)S(1)}, f32[128]{0:T(128)}, u32[]{:S(2)}) copy-start(f32[128]{0:T(128)} %param.8) | copy-start | bytes 1540
  43.4 7.1 %slice-start = ((f32[1536]{0:T(1024)}), f32[256]{0:T(256)S(1)}, s32[]{:S(2)}) async-start(f32[1536]{0:T(1024)} %param.9), calls=%async_computation.3 | async-start | bytes 2048 | tf_op jit(solution)/shard_map/slice | solution.py:99
  43.4 16.8 %copy-start.3 = (bf16[16,16,8,256]{3,2,1,0:T(8,128)(2,1)}, bf16[16,16,8,256]{3,2,1,0:T(8,128)(2,1)S(1)}, u32[]{:S(2)}) copy-start(bf16[16,16,8,256]{3,2,1,0:T(8,128)(2,1)S(1)} %all-to-all-done) | copy-start | bytes 3145732
  43.4 109.9 %all-to-all-start.1 = ((bf16[16,16,8,1088]{3,2,1,0:T(8,128)(2,1)}), bf16[16,16,8,1088]{3,2,1,0:T(8,128)(2,1)}, u32[]{:S(2)}, u32[]{:S(2)}) async-start(bf16[16,16,8,1088]{3,2,1,0:T(8,128)(2,1)} %pad_maximum_fusion), calls=%async_computation.1 | async-start | bytes 9437184 | tf_op jit(solution)/shard_map/all_to_all | solution.py:82
  153.3 41.1 %all-to-all-start.2 = ((bf16[16,16,8,384]{3,2,1,0:T(8,128)(2,1)}), bf16[16,16,8,384]{3,2,1,0:T(8,128)(2,1)S(1)}, u32[]{:S(2)}, u32[]{:S(2)}) async-start(bf16[16,16,8,384]{3,2,1,0:T(8,128)(2,1)} %fusion.21), calls=%async_computation.2 | async-start | bytes 3145728 | tf_op jit(solution)/shard_map/all_to_all | solution.py:82
  160.5 15.0 %copy-start.1 = (bf16[256,8,1536]{2,1,0:T(8,128)(2,1)S(1)}, bf16[256,8,1536]{2,1,0:T(8,128)(2,1)}, u32[]{:S(2)}) copy-start(bf16[256,8,1536]{2,1,0:T(8,128)(2,1)} %pad.5) | copy-start | bytes 18874372
  175.5 5.4 %copy-start.4 = (bf16[16,16,8,256]{3,2,1,0:T(8,128)(2,1)S(1)}, bf16[16,16,8,256]{3,2,1,0:T(8,128)(2,1)}, u32[]{:S(2)}) copy-start(bf16[16,16,8,256]{3,2,1,0:T(8,128)(2,1)} %copy-done.3) | copy-start | bytes 3145732
  178.3 2.7 %copy-start.2 = (bf16[256,8,1536]{2,1,0:T(8,128)(2,1)}, bf16[256,8,1536]{2,1,0:T(8,128)(2,1)S(1)}, u32[]{:S(2)}) copy-start(bf16[256,8,1536]{2,1,0:T(8,128)(2,1)S(1)} %slice_dynamic-update-slice_fusion) | copy-start | bytes 18874372

commit v13 on v12

--- a/solution.py
+++ b/solution.py
@@ -4,8 +4,8 @@
 from jax.sharding import PartitionSpec as P
 
 VBLK = 192
-EDGE_PART = 4
-LEAD_PART = 6
+EDGE_PART = 6
+LEAD_PART = 4
 
 
 def chunk_energies(factors, blocks, occ_rows, occ_cols, vir_chunk, vir_blocks, scale):

time: 201 us -> 200 us (level)
    unnamed x17 -> x9, local copies, waits for them, and re-layouts: 3.74 us -> 1.02 us
    dynamic_update_slice x2, local copies, waits for them, and re-layouts: 4.01 us -> 6.44 us  [per_device(): factors = lax.dynamic_update_slice(factors, got, (0, 0, bounds[c]))]
  transfers between devices with their start and end apart: 3 -> 3, of which waited for: 2 -> 2; matrix products, arithmetic and copies ran while one was open for 30% -> 31% of each run, Pallas kernels for 0% -> 0%
where the time goes in v13:
time: 200 us; the launch traced here: 199 us
  waiting for transfers between devices  99.3 us (50%)
  matrix products  55.7 us (28%)
  local copies, waits for them, and re-layouts  17.9 us (9%)
  starting transfers between devices  16.4 us (8%)
  between operations  5.89 us (3%)
  other arithmetic  3.67 us (2%)
    all_to_all x3, waiting for transfers between devices, per_device(): lax.all_to_all(product, 'occ', split_axis=0, concat_axis=0, tiled=True)  99.3 us
    dot_general x3, matrix products, chunk_product(): lax.dot_general(rows, orbitals[:, bounds[c]:bounds[c + 1]], (((3,), (0,))...  28.7 us
    dot_general x3, matrix products, chunk_energies(): lax.dot_general(factors, blocks, (((0,), (0,)), ((), ())), preferred_elem...  23.2 us
    all_to_all x3, starting transfers between devices, per_device(): lax.all_to_all(product, 'occ', split_axis=0, concat_axis=0, tiled=True)  16.4 us
    dynamic_update_slice x2, local copies, waits for them, and re-layouts, per_device(): factors = lax.dynamic_update_slice(factors, got, (0, 0, bounds[c]))  6.44 us
  transfers between devices with their start and end apart: 3, of which 2 were waited for; matrix products, arithmetic and copies ran while one was open for 31% of the time, Pallas kernels for 0%

profile of v13, /device:TPU:13, one launch (start us, length us, event | category | flops | bytes accessed | tf_op | source)
XLA Modules:
  0.0 198.9 jit_solution(5359563864590074286)
XLA Ops:
  0.6 9.4 %fusion.21 = bf16[16,16,8,384]{3,2,1,0:T(8,128)(2,1)} fusion(bf16[2048,1536]{1,0:T(8,128)(2,1)} %param.7, bf16[16,128,2048]{2,1,0:T(8,128)(2,1)} %param.6), kind=kOutput, calls=%fused_computation.25 | convolution fusion | flops 3222011904 | bytes 11534336 | tf_op jit(solution)/shard_map/dot_general | solution.py:40
  10.1 6.6 %all-to-all-start = ((bf16[16,16,8,384]{3,2,1,0:T(8,128)(2,1)}), bf16[16,16,8,384]{3,2,1,0:T(8,128)(2,1)S(1)}, u32[]{:S(2)}, u32[]{:S(2)}) async-start(bf16[16,16,8,384]{3,2,1,0:T(8,128)(2,1)} %fusion.21), calls=%async_computation | async-start | bytes 3145728 | tf_op jit(solution)/shard_map/all_to_all | solution.py:82
  16.7 0.7 fusion.41
  21.9 2.6 %gather_fusion = bf16[8,16,2048]{2,0,1:T(8,128)(2,1)S(1)} fusion(bf16[16,128,2048]{2,1,0:T(8,128)(2,1)} %param.6, s32[1024]{0:T(1024)S(1)} %pad_clamp_fusion.1), kind=kCustom, calls=%fused_computation | custom fusion | bytes 1048608 | tf_op jit(solution)/shard_map/jit(_take)/gather | solution.py:47
  24.5 3.8 %fusion.20 = bf16[16,8,1536]{2,1,0:T(8,128)(2,1)S(1)} fusion(bf16[2048,1536]{1,0:T(8,128)(2,1)} %param.7, bf16[8,16,2048]{2,0,1:T(8,128)(2,1)S(1)} %gather_fusion, pred[128]{0:T(512)(128)(4,1)S(1)} %broadcast_in_dim.21), kind=kOutput, calls=%fused_computation.24 | convolution fusion | flops 805765120 | bytes 7209088 | tf_op jit(solution)/shard_map/dot_general | solution.py:48
  28.4 0.7 fusion.39
  30.5 0.2 stack.38
  30.7 12.3 %fusion.15 = bf16[16,16,8,896]{3,2,1,0:T(8,128)(2,1)S(1)} fusion(bf16[2048,1536]{1,0:T(8,128)(2,1)} %param.7, bf16[16,128,2048]{2,1,0:T(8,128)(2,1)} %param.6), kind=kOutput, calls=%fused_computation.22 | convolution fusion | flops 7518027776 | bytes 15728640 | tf_op jit(solution)/shard_map/dot_general | solution.py:40
  43.2 2.8 %pad_maximum_fusion = bf16[16,16,8,1088]{3,2,1,0:T(8,128)(2,1)} fusion(bf16[16,16,8,192]{3,2,1,0:T(8,128)(2,1)S(1)} %broadcast_in_dim.25, bf16[16,16,8,896]{3,2,1,0:T(8,128)(2,1)S(1)} %fusion.15), kind=kLoop, calls=%fused_computation.17 | loop fusion | flops 8912896 | bytes 8912896 | tf_op jit(solution)/shard_map/concatenate | solution.py:78
  45.9 6.9 %all-to-all-done = bf16[16,16,8,384]{3,2,1,0:T(8,128)(2,1)S(1)} async-done(((bf16[16,16,8,384]{3,2,1,0:T(8,128)(2,1)}), bf16[16,16,8,384]{3,2,1,0:T(8,128)(2,1)S(1)}, u32[]{:S(2)}, u32[]{:S(2)}) %all-to-all-start) | async-done | bytes 1572896 | tf_op jit(solution)/shard_map/all_to_all | solution.py:82
  52.8 4.9 %all-to-all-start.1 = ((bf16[16,16,8,1088]{3,2,1,0:T(8,128)(2,1)}), bf16[16,16,8,1088]{3,2,1,0:T(8,128)(2,1)}, u32[]{:S(2)}, u32[]{:S(2)}) async-start(bf16[16,16,8,1088]{3,2,1,0:T(8,128)(2,1)} %pad_maximum_fusion), calls=%async_computation.1 | async-start | bytes 9437184 | tf_op jit(solution)/shard_map/all_to_all | solution.py:82
  57.9 0.6 gather_fusion.1
  59.0 6.9 %fusion.27 = bf16[16,16,8,256]{3,2,1,0:T(8,128)(2,1)} fusion(bf16[2048,1536]{1,0:T(8,128)(2,1)} %param.7, bf16[16,128,2048]{2,1,0:T(8,128)(2,1)} %param.6), kind=kOutput, calls=%fused_computation.29 | convolution fusion | flops 2148007936 | bytes 10485760 | tf_op jit(solution)/shard_map/dot_general | solution.py:40
  65.9 3.2 %pad.5 = bf16[256,8,1536]{2,1,0:T(8,128)(2,1)} pad(bf16[256,8,384]{2,1,0:T(8,128)(2,1)S(1)} %bitcast.78, bf16[]{:T(256)} %constant.44.clone.1), padding=0_0x0_0x0_1152 | pad | bytes 7864322 | tf_op jit(solution)/shard_map/jit(_pad)/pad | solution.py:89
  69.0 92.4 %all-to-all-done.1 = bf16[16,16,8,1088]{3,2,1,0:T(8,128)(2,1)} async-done(((bf16[16,16,8,1088]{3,2,1,0:T(8,128)(2,1)}), bf16[16,16,8,1088]{3,2,1,0:T(8,128)(2,1)}, u32[]{:S(2)}, u32[]{:S(2)}) %all-to-all-start.1) | async-done | bytes 4456480 | tf_op jit(solution)/shard_map/all_to_all | solution.py:82
  161.4 4.9 %all-to-all-start.2 = ((bf16[16,16,8,256]{3,2,1,0:T(8,128)(2,1)}), bf16[16,16,8,256]{3,2,1,0:T(8,128)(2,1)}, u32[]{:S(2)}, u32[]{:S(2)}) async-start(bf16[16,16,8,256]{3,2,1,0:T(8,128)(2,1)} %fusion.27), calls=%async_computation.2 | async-start | bytes 2097152 | tf_op jit(solution)/shard_map/all_to_all | solution.py:82
  166.4 1.3 slice.117
  167.6 1.0 copy.30
  168.7 4.2 %slice_dynamic-update-slice_fusion = bf16[256,8,1536]{2,1,0:T(8,128)(2,1)} fusion(bf16[256,8,1536]{2,1,0:T(8,128)(2,1)} %pad.5, bf16[256,8,1088]{2,1,0:T(8,128)(2,1)} %bitcast.18), kind=kLoop, calls=%fused_computation.19 | loop fusion | bytes 7340032 | tf_op jit(solution)/shard_map/dynamic_update_slice | solution.py:91
  172.8 14.9 %fusion = f32[8,8]{1,0:T(8,128)S(1)} fusion(f32[8,192]{1,0:T(8,128)S(1)} %broadcast_subtract_fusion.3, f32[8,1088]{1,0:T(8,128)S(1)} %broadcast_subtract_fusion, bf16[256,8,1088,1]{2,1,0,3:T(8,128)(2,1)} %bitcast.32, bf16[256,8,192]{0,2,1:T(8,128)(2,1)S(1)} %copy.30), kind=kOutput, calls=%fused_computation.3 | convolution fusion | flops 6898581504 | bytes 5284096 | tf_op jit(solution)/shard_map/dot_general | solution.py:12
  187.7 4.1 %fusion.1 = f32[8,8]{1,0:T(8,128)S(1)} fusion(f32[8,192]{1,0:T(8,128)S(1)} %broadcast_subtract_fusion.3, f32[8,384]{1,0:T(8,128)S(1)} %broadcast_subtract_fusion.1, bf16[256,8,384,1]{2,1,0,3:T(8,128)(2,1)S(1)} %bitcast.79, bf16[256,8,192]{0,2,1:T(8,128)(2,1)S(1)} %copy.30), kind=kOutput, calls=%fused_computation.5 | convolution fusion | flops 2434793472 | bytes 2377984 | tf_op jit(solution)/shard_map/dot_general | solution.py:12
  191.8 2.3 %constant_dynamic-update-slice_fusion = bf16[256,8,1536]{2,1,0:T(8,128)(2,1)} fusion(bf16[256,8,1536]{2,1,0:T(8,128)(2,1)} %slice_dynamic-update-slice_fusion, bf16[256,8,256]{2,1,0:T(8,128)(2,1)} %bitcast.31), kind=kLoop, calls=%fused_computation.48 | loop fusion | bytes 2097152 | tf_op jit(solution)/shard_map/dynamic_update_slice | solution.py:91
  194.1 4.2 %fusion.2 = f32[8,8]{1,0:T(8,128)S(1)} fusion(f32[8,192]{1,0:T(8,128)S(1)} %broadcast_subtract_fusion.3, f32[8,256]{1,0:T(8,128)S(1)} %broadcast_subtract_fusion.2, bf16[256,8,256,1]{2,1,0,3:T(8,128)(2,1)} %bitcast.33, bf16[256,8,192]{0,2,1:T(8,128)(2,1)S(1)} %copy.30), kind=kOutput, calls=%fused_computation.7 | convolution fusion | flops 1623195648 | bytes 1849600 | tf_op jit(solution)/shard_map/dot_general | solution.py:12
  198.3 0.6 negate_multiply_fusion
  (36 shorter events, 1.5 us)
Async XLA Ops:
  0.6 21.1 %copy-start.3 = (s32[8]{0:T(128)S(1)}, s32[8]{0:T(128)}, u32[]{:S(2)}) copy-start(s32[8]{0:T(128)} %param.10) | copy-start | bytes 100
  0.6 16.0 %copy-start.1 = (s32[8]{0:T(128)S(1)}, s32[8]{0:T(128)}, u32[]{:S(2)}) copy-start(s32[8]{0:T(128)} %param.11) | copy-start | bytes 100
  10.1 42.7 %all-to-all-start = ((bf16[16,16,8,384]{3,2,1,0:T(8,128)(2,1)}), bf16[16,16,8,384]{3,2,1,0:T(8,128)(2,1)S(1)}, u32[]{:S(2)}, u32[]{:S(2)}) async-start(bf16[16,16,8,384]{3,2,1,0:T(8,128)(2,1)} %fusion.21), calls=%async_computation | async-start | bytes 3145728 | tf_op jit(solution)/shard_map/all_to_all | solution.py:82
  45.9 11.8 %copy-start.2 = (f32[1536]{0:T(1024)S(1)}, f32[1536]{0:T(1024)}, u32[]{:S(2)}) copy-start(f32[1536]{0:T(1024)} %param.9) | copy-start | bytes 18436
  45.9 11.8 %copy-start = (f32[128]{0:T(128)S(1)}, f32[128]{0:T(128)}, u32[]{:S(2)}) copy-start(f32[128]{0:T(128)} %param.8) | copy-start | bytes 1540
  45.9 12.8 %slice-start = ((f32[1536]{0:T(1024)}), f32[384]{0:T(512)S(1)}, s32[]{:S(2)}) async-start(f32[1536]{0:T(1024)} %param.9), calls=%async_computation.3 | async-start | bytes 4096 | tf_op jit(solution)/shard_map/slice | solution.py:99
  52.8 108.6 %all-to-all-start.1 = ((bf16[16,16,8,1088]{3,2,1,0:T(8,128)(2,1)}), bf16[16,16,8,1088]{3,2,1,0:T(8,128)(2,1)}, u32[]{:S(2)}, u32[]{:S(2)}) async-start(bf16[16,16,8,1088]{3,2,1,0:T(8,128)(2,1)} %pad_maximum_fusion), calls=%async_computation.1 | async-start | bytes 9437184 | tf_op jit(solution)/shard_map/all_to_all | solution.py:82
  161.4 30.4 %all-to-all-start.2 = ((bf16[16,16,8,256]{3,2,1,0:T(8,128)(2,1)}), bf16[16,16,8,256]{3,2,1,0:T(8,128)(2,1)}, u32[]{:S(2)}, u32[]{:S(2)}) async-start(bf16[16,16,8,256]{3,2,1,0:T(8,128)(2,1)} %fusion.27), calls=%async_computation.2 | async-start | bytes 2097152 | tf_op jit(solution)/shard_map/all_to_all | solution.py:82

commit v14 on v11

--- a/solution.py
+++ b/solution.py
@@ -60,9 +60,10 @@
     )
     scale = 1.0 / (aux_here * groups * nvir * VBLK)
 
-    carrier = min(1, chunks - 1) if ride else -1
-    if not ride:
-        blocks = lax.all_gather(pieces, "occ", axis=0, tiled=True)
+    carrier = -1
+    wide = -(-VBLK // 128) * 128
+    padded = jnp.pad(pieces, ((0, 0), (0, 0), (0, wide - VBLK)))
+    blocks = lax.all_gather(padded, "occ", axis=0, tiled=True)[:, :, :VBLK]
     raw = []
     sums = []
     made_at = {}

time: 198 us -> 211 us (1.066)
  between operations: 5.89 us -> 19.2 us
  matrix products: 58.1 us -> 52.8 us
  waiting for transfers between devices: 94.2 us -> 97.3 us
    all_gather x0 -> x1, waiting for transfers between devices: none -> 49.4 us  [per_device(): blocks = lax.all_gather(padded, 'occ', axis=0, tiled=True)[:, :, :VBLK]]
    all_to_all x3, waiting for transfers between devices: 94.2 us -> 47.9 us  [per_device(): lax.all_to_all(product, 'occ', split_axis=0, concat_axis=0, tiled=True)]
    dot_general x3, matrix products: 25.3 us -> 18.7 us  [chunk_energies(): lax.dot_general(factors, blocks, (((0,), (0,)), ((), ())), preferred_elem...]
    concatenate x1 -> x0, other arithmetic: 2.61 us -> none  [per_device(): product = jnp.concatenate([product, extra], axis=3)]
    slice x2 -> x0, local copies, waits for them, and re-layouts: 2.26 us -> none  [the longest x1 2.25 us: per_device(): blocks = got[:, :, span:]]
  transfers between devices with their start and end apart: 3 -> 4, of which waited for: 3 -> 3; matrix products, arithmetic and copies ran while one was open for 33% -> 26% of each run, Pallas kernels for 0% -> 0%
where the time goes in v14:
time: 211 us; the launch traced here: 210 us
  waiting for transfers between devices  97.3 us (46%)
  matrix products  52.8 us (25%)
  local copies, waits for them, and re-layouts  21 us (10%)
  between operations  19.2 us (9%)
  starting transfers between devices  17.8 us (8%)
    all_gather x1, waiting for transfers between devices, per_device(): blocks = lax.all_gather(padded, 'occ', axis=0, tiled=True)[:, :, :VBLK]  49.4 us
    all_to_all x3, waiting for transfers between devices, per_device(): lax.all_to_all(product, 'occ', split_axis=0, concat_axis=0, tiled=True)  47.9 us
    dot_general x3, matrix products, chunk_product(): lax.dot_general(rows, orbitals[:, bounds[c]:bounds[c + 1]], (((3,), (0,))...  30.1 us
    dot_general x3, matrix products, chunk_energies(): lax.dot_general(factors, blocks, (((0,), (0,)), ((), ())), preferred_elem...  18.7 us
    all_to_all x3, starting transfers between devices, per_device(): lax.all_to_all(product, 'occ', split_axis=0, concat_axis=0, tiled=True)  17.6 us
    pad x1, local copies, waits for them, and re-layouts, per_device(): factors = jnp.pad(got, ((0, 0), (0, 0), (0, nvir - span)))  4.71 us
    dynamic_update_slice x2, local copies, waits for them, and re-layouts, per_device(): factors = lax.dynamic_update_slice(factors, got, (0, 0, bounds[c]))  4.58 us
  transfers between devices with their start and end apart: 4, of which 3 were waited for; matrix products, arithmetic and copies ran while one was open for 26% of the time, Pallas kernels for 0%

profile of v14, /device:TPU:13, one launch (start us, length us, event | category | flops | bytes accessed | tf_op | source)
XLA Modules:
  0.0 210.1 jit_solution(2091273365233727544)
XLA Ops:
  7.2 9.4 %fusion.21 = bf16[16,16,8,384]{3,2,1,0:T(8,128)(2,1)} fusion(bf16[2048,1536]{1,0:T(8,128)(2,1)} %param.7, bf16[16,128,2048]{2,1,0:T(8,128)(2,1)} %param.6), kind=kOutput, calls=%fused_computation.23 | convolution fusion | flops 3222011904 | bytes 11534336 | tf_op jit(solution)/shard_map/dot_general | solution.py:38
  16.6 6.6 %all-to-all-start = ((bf16[16,16,8,384]{3,2,1,0:T(8,128)(2,1)}), bf16[16,16,8,384]{3,2,1,0:T(8,128)(2,1)S(1)}, u32[]{:S(2)}, u32[]{:S(2)}) async-start(bf16[16,16,8,384]{3,2,1,0:T(8,128)(2,1)} %fusion.21), calls=%async_computation | async-start | bytes 3145728 | tf_op jit(solution)/shard_map/all_to_all | solution.py:81
  23.7 3.4 %gather_fusion = bf16[8,16,2048]{2,0,1:T(8,128)(2,1)} fusion(bf16[16,128,2048]{2,1,0:T(8,128)(2,1)} %param.6, s32[1024]{0:T(1024)S(1)} %pad_clamp_fusion.1), kind=kCustom, calls=%fused_computation | custom fusion | bytes 1048608 | tf_op jit(solution)/shard_map/jit(_take)/gather | solution.py:45
  27.8 11.2 %fusion.16 = bf16[16,16,8,768]{3,2,1,0:T(8,128)(2,1)} fusion(bf16[2048,1536]{1,0:T(8,128)(2,1)} %param.7, bf16[16,128,2048]{2,1,0:T(8,128)(2,1)} %param.6), kind=kOutput, calls=%fused_computation.22 | convolution fusion | flops 6444023808 | bytes 14680064 | tf_op jit(solution)/shard_map/dot_general | solution.py:38
  38.9 20.4 %all-to-all-done = bf16[16,16,8,384]{3,2,1,0:T(8,128)(2,1)S(1)} async-done(((bf16[16,16,8,384]{3,2,1,0:T(8,128)(2,1)}), bf16[16,16,8,384]{3,2,1,0:T(8,128)(2,1)S(1)}, u32[]{:S(2)}, u32[]{:S(2)}) %all-to-all-start) | async-done | bytes 1572896 | tf_op jit(solution)/shard_map/all_to_all | solution.py:81
  59.4 1.2 copy-done.1
  60.5 4.9 %all-to-all-start.1 = ((bf16[16,16,8,768]{3,2,1,0:T(8,128)(2,1)}), bf16[16,16,8,768]{3,2,1,0:T(8,128)(2,1)S(1)}, u32[]{:S(2)}, u32[]{:S(2)}) async-start(bf16[16,16,8,768]{3,2,1,0:T(8,128)(2,1)} %fusion.16), calls=%async_computation.1 | async-start | bytes 6291456 | tf_op jit(solution)/shard_map/all_to_all | solution.py:81
  65.7 4.0 %fusion.15 = bf16[16,8,1536]{2,1,0:T(8,128)(2,1)S(1)} fusion(bf16[2048,1536]{1,0:T(8,128)(2,1)} %param.7, bf16[8,16,2048]{2,0,1:T(8,128)(2,1)} %gather_fusion, pred[128]{0:T(512)(128)(4,1)} %broadcast_in_dim.19), kind=kOutput, calls=%fused_computation.21 | convolution fusion | flops 805765120 | bytes 7209088 | tf_op jit(solution)/shard_map/dot_general | solution.py:46
  69.7 0.7 fusion.42
  75.4 0.7 fusion.39
  77.2 0.6 pad.9
  77.8 0.6 pad_clamp_fusion
  78.5 0.6 gather_fusion.1
  79.6 9.5 %fusion.24 = bf16[16,16,8,384]{3,2,1,0:T(8,128)(2,1)} fusion(bf16[2048,1536]{1,0:T(8,128)(2,1)} %param.7, bf16[16,128,2048]{2,1,0:T(8,128)(2,1)} %param.6), kind=kOutput, calls=%fused_computation.24 | convolution fusion | flops 3222011904 | bytes 11534336 | tf_op jit(solution)/shard_map/dot_general | solution.py:38
  89.0 49.4 %all-gather.2.cloned.1.call-done = bf16[256,8,256]{2,1,0:T(8,128)(2,1)} async-done(((bf16[16,8,256]{2,1,0:T(8,128)(2,1)}), bf16[256,8,256]{2,1,0:T(8,128)(2,1)}) %all-gather.2.cloned.1.call-update) | async-done | bytes 1048592 | tf_op jit(solution)/shard_map/all_gather | solution.py:66
  138.4 2.6 %copy.49 = bf16[256,8,192]{0,2,1:T(8,128)(2,1)} copy(bf16[256,8,192]{2,1,0:T(8,128)(2,1)} %bitcast.82) | data formatting | bytes 1572864
  141.1 4.7 %pad.8 = bf16[256,8,1536]{2,1,0:T(8,128)(2,1)} pad(bf16[256,8,384]{2,1,0:T(8,128)(2,1)} %bitcast.80, bf16[]{:T(256)} %constant.43.clone.1), padding=0_0x0_0x0_1152 | pad | bytes 7864322 | tf_op jit(solution)/shard_map/jit(_pad)/pad | solution.py:88
  145.8 4.1 %fusion.1 = f32[8,8]{1,0:T(8,128)S(1)} fusion(f32[8,192]{1,0:T(8,128)S(1)} %broadcast_subtract_fusion.3, f32[8,384]{1,0:T(8,128)S(1)} %get-tuple-element.37, bf16[256,8,384,1]{2,1,0,3:T(8,128)(2,1)S(1)} %bitcast.81, bf16[256,8,192]{0,2,1:T(8,128)(2,1)S(1)} %copy-done.3), kind=kOutput, calls=%fused_computation.6 | convolution fusion | flops 2434793472 | bytes 2377984 | tf_op jit(solution)/shard_map/dot_general | solution.py:11
  149.9 1.9 constant_dynamic-update-slice_fusion.1
  151.8 6.2 %all-to-all-start.2 = ((bf16[16,16,8,384]{3,2,1,0:T(8,128)(2,1)}), bf16[16,16,8,384]{3,2,1,0:T(8,128)(2,1)}, u32[]{:S(2)}, u32[]{:S(2)}) async-start(bf16[16,16,8,384]{3,2,1,0:T(8,128)(2,1)} %fusion.24), calls=%async_computation.2 | async-start | bytes 3145728 | tf_op jit(solution)/shard_map/all_to_all | solution.py:81
  157.9 8.9 %fusion = f32[8,8]{1,0:T(8,128)S(1)} fusion(f32[8,192]{1,0:T(8,128)S(1)} %broadcast_subtract_fusion.3, f32[8,768]{1,0:T(8,128)S(1)} %broadcast_subtract_fusion, bf16[256,8,768,1]{2,1,0,3:T(8,128)(2,1)S(1)} %bitcast.79, bf16[256,8,192]{0,2,1:T(8,128)(2,1)} %copy.49), kind=kOutput, calls=%fused_computation.3 | convolution fusion | flops 4869586944 | bytes 3963136 | tf_op jit(solution)/shard_map/dot_general | solution.py:11
  166.8 27.4 %all-to-all-done.2 = bf16[16,16,8,384]{3,2,1,0:T(8,128)(2,1)} async-done(((bf16[16,16,8,384]{3,2,1,0:T(8,128)(2,1)}), bf16[16,16,8,384]{3,2,1,0:T(8,128)(2,1)}, u32[]{:S(2)}, u32[]{:S(2)}) %all-to-all-start.2) | async-done | bytes 1572896 | tf_op jit(solution)/shard_map/all_to_all | solution.py:81
  194.2 2.7 %constant_dynamic-update-slice_fusion = bf16[256,8,1536]{2,1,0:T(8,128)(2,1)} fusion(bf16[256,8,1536]{2,1,0:T(8,128)(2,1)} %constant_dynamic-update-slice_fusion.1, bf16[256,8,384]{2,1,0:T(8,128)(2,1)} %bitcast.32), kind=kLoop, calls=%fused_computation.46 | loop fusion | bytes 3145728 | tf_op jit(solution)/shard_map/dynamic_update_slice | solution.py:90
  196.9 5.7 %fusion.2 = f32[8,8]{1,0:T(8,128)S(1)} fusion(f32[8,384]{1,0:T(8,128)S(1)} %get-tuple-element.36, f32[8,192]{1,0:T(8,128)S(1)} %broadcast_subtract_fusion.3, bf16[256,8,384,1]{2,1,0,3:T(8,128)(2,1)} %bitcast.33, bf16[256,8,192]{0,2,1:T(8,128)(2,1)} %copy.49), kind=kOutput, calls=%fused_computation.7 | convolution fusion | flops 2434793472 | bytes 2377984 | tf_op jit(solution)/shard_map/dot_general | solution.py:11
  (39 shorter events, 3.5 us)
Async XLA Ops:
  7.2 16.0 %copy-start.6 = (s32[8]{0:T(128)S(1)}, s32[8]{0:T(128)}, u32[]{:S(2)}) copy-start(s32[8]{0:T(128)} %param.10) | copy-start | bytes 100
  16.6 42.7 %all-to-all-start = ((bf16[16,16,8,384]{3,2,1,0:T(8,128)(2,1)}), bf16[16,16,8,384]{3,2,1,0:T(8,128)(2,1)S(1)}, u32[]{:S(2)}, u32[]{:S(2)}) async-start(bf16[16,16,8,384]{3,2,1,0:T(8,128)(2,1)} %fusion.21), calls=%async_computation | async-start | bytes 3145728 | tf_op jit(solution)/shard_map/all_to_all | solution.py:81
  38.9 30.8 %copy-start.5 = (s32[8]{0:T(128)S(1)}, s32[8]{0:T(128)}, u32[]{:S(2)}) copy-start(s32[8]{0:T(128)} %param.11) | copy-start | bytes 100
  59.4 1.2 copy-start.1
  60.5 89.4 %all-to-all-start.1 = ((bf16[16,16,8,768]{3,2,1,0:T(8,128)(2,1)}), bf16[16,16,8,768]{3,2,1,0:T(8,128)(2,1)S(1)}, u32[]{:S(2)}, u32[]{:S(2)}) async-start(bf16[16,16,8,768]{3,2,1,0:T(8,128)(2,1)} %fusion.16), calls=%async_computation.1 | async-start | bytes 6291456 | tf_op jit(solution)/shard_map/all_to_all | solution.py:81
  65.4 13.0 %copy-start = (f32[128]{0:T(128)S(1)}, f32[128]{0:T(128)}, u32[]{:S(2)}) copy-start(f32[128]{0:T(128)} %param.8) | copy-start | bytes 1540
  65.4 13.8 %copy-start.4 = (f32[1536]{0:T(1024)S(1)}, f32[1536]{0:T(1024)}, u32[]{:S(2)}) copy-start(f32[1536]{0:T(1024)} %param.9) | copy-start | bytes 18436
  65.4 73.0 %all-gather.2.cloned.1.call-start = ((), (), s32[]{:S(2)}) async-start(), calls=%async_computation.3 | async-start | bytes 1114112 | tf_op jit(solution)/shard_map/all_gather | solution.py:66
  141.1 4.7 %copy-start.2 = (bf16[16,16,8,384]{3,2,1,0:T(8,128)(2,1)S(1)}, bf16[16,16,8,384]{3,2,1,0:T(8,128)(2,1)}, u32[]{:S(2)}) copy-start(bf16[16,16,8,384]{3,2,1,0:T(8,128)(2,1)} %copy-done.1) | copy-start | bytes 4718596
  141.1 4.7 %copy-start.3 = (bf16[256,8,192]{0,2,1:T(8,128)(2,1)S(1)}, bf16[256,8,192]{0,2,1:T(8,128)(2,1)}, u32[]{:S(2)}) copy-start(bf16[256,8,192]{0,2,1:T(8,128)(2,1)} %copy.49) | copy-start | bytes 2359300
  151.8 42.5 %all-to-all-start.2 = ((bf16[16,16,8,384]{3,2,1,0:T(8,128)(2,1)}), bf16[16,16,8,384]{3,2,1,0:T(8,128)(2,1)}, u32[]{:S(2)}, u32[]{:S(2)}) async-start(bf16[16,16,8,384]{3,2,1,0:T(8,128)(2,1)} %fusion.24), calls=%async_computation.2 | async-start | bytes 3145728 | tf_op jit(solution)/shard_map/all_to_all | solution.py:81
Sparse Core Ops, SparseCore 0:
  78.0 60.4 all-gather.1

commit v15 on v12

--- a/solution.py
+++ b/solution.py
@@ -5,7 +5,7 @@
 
 VBLK = 192
 EDGE_PART = 4
-LEAD_PART = 6
+LEAD_PART = 3
 
 
 def chunk_energies(factors, blocks, occ_rows, occ_cols, vir_chunk, vir_blocks, scale):

time: 201 us -> 201 us (level)
  matrix products: 54.7 us -> 58.2 us
    dot_general x3, matrix products: 22.1 us -> 25.1 us  [chunk_energies(): lax.dot_general(factors, blocks, (((0,), (0,)), ((), ())), preferred_elem...]
    dynamic_update_slice x2, local copies, waits for them, and re-layouts: 4.01 us -> 6.16 us  [per_device(): factors = lax.dynamic_update_slice(factors, got, (0, 0, bounds[c]))]
    unnamed x17 -> x11, local copies, waits for them, and re-layouts: 3.74 us -> 1.72 us
  transfers between devices with their start and end apart: 3 -> 3, of which waited for: 2 -> 3; matrix products, arithmetic and copies ran while one was open for 30% -> 30% of each run, Pallas kernels for 0% -> 0%
where the time goes in v15:
time: 201 us
  waiting for transfers between devices  98.4 us (49%)
  matrix products  58.2 us (29%)
  local copies, waits for them, and re-layouts  18.4 us (9%)
  starting transfers between devices  16.4 us (8%)
  between operations  5.97 us (3%)
  other arithmetic  3.29 us (2%)
    all_to_all x3, waiting for transfers between devices, per_device(): lax.all_to_all(product, 'occ', split_axis=0, concat_axis=0, tiled=True)  98.4 us
    dot_general x3, matrix products, chunk_product(): lax.dot_general(rows, orbitals[:, bounds[c]:bounds[c + 1]], (((3,), (0,))...  29.2 us
    dot_general x3, matrix products, chunk_energies(): lax.dot_general(factors, blocks, (((0,), (0,)), ((), ())), preferred_elem...  25.1 us
    all_to_all x3, starting transfers between devices, per_device(): lax.all_to_all(product, 'occ', split_axis=0, concat_axis=0, tiled=True)  16.4 us
    dynamic_update_slice x2, local copies, waits for them, and re-layouts, per_device(): factors = lax.dynamic_update_slice(factors, got, (0, 0, bounds[c]))  6.16 us
  transfers between devices with their start and end apart: 3, of which 3 were waited for; matrix products, arithmetic and copies ran while one was open for 30% of the time, Pallas kernels for 0%

profile of v15, /device:TPU:13, one launch (start us, length us, event | category | flops | bytes accessed | tf_op | source)
XLA Modules:
  0.0 200.6 jit_solution(18169899553805676787)
XLA Ops:
  0.6 9.8 %fusion.24 = bf16[16,16,8,512]{3,2,1,0:T(8,128)(2,1)} fusion(bf16[2048,1536]{1,0:T(8,128)(2,1)} %param.7, bf16[16,128,2048]{2,1,0:T(8,128)(2,1)} %param.6), kind=kOutput, calls=%fused_computation.28 | convolution fusion | flops 4296015872 | bytes 12582912 | tf_op jit(solution)/shard_map/dot_general | solution.py:40
  10.5 6.6 %all-to-all-start = ((bf16[16,16,8,512]{3,2,1,0:T(8,128)(2,1)}), bf16[16,16,8,512]{3,2,1,0:T(8,128)(2,1)S(1)}, u32[]{:S(2)}, u32[]{:S(2)}) async-start(bf16[16,16,8,512]{3,2,1,0:T(8,128)(2,1)} %fusion.24), calls=%async_computation | async-start | bytes 4194304 | tf_op jit(solution)/shard_map/all_to_all | solution.py:82
  17.0 0.7 fusion.43
  22.9 2.6 %gather_fusion = bf16[8,16,2048]{2,0,1:T(8,128)(2,1)S(1)} fusion(bf16[16,128,2048]{2,1,0:T(8,128)(2,1)} %param.6, s32[1024]{0:T(1024)S(1)} %pad_clamp_fusion.1), kind=kCustom, calls=%fused_computation | custom fusion | bytes 1048608 | tf_op jit(solution)/shard_map/jit(_take)/gather | solution.py:47
  25.6 3.8 %fusion.15 = bf16[16,8,1536]{2,1,0:T(8,128)(2,1)S(1)} fusion(bf16[2048,1536]{1,0:T(8,128)(2,1)} %param.7, bf16[8,16,2048]{2,0,1:T(8,128)(2,1)S(1)} %gather_fusion, pred[128]{0:T(512)(128)(4,1)S(1)} %broadcast_in_dim.21), kind=kOutput, calls=%fused_computation.23 | convolution fusion | flops 805765120 | bytes 7209088 | tf_op jit(solution)/shard_map/dot_general | solution.py:48
  29.4 0.7 fusion.41
  31.2 9.9 %fusion.19 = bf16[16,16,8,640]{3,2,1,0:T(8,128)(2,1)S(1)} fusion(bf16[2048,1536]{1,0:T(8,128)(2,1)} %param.7, bf16[16,128,2048]{2,1,0:T(8,128)(2,1)} %param.6), kind=kOutput, calls=%fused_computation.27 | convolution fusion | flops 5370019840 | bytes 13631488 | tf_op jit(solution)/shard_map/dot_general | solution.py:40
  41.2 2.4 %pad_maximum_fusion = bf16[16,16,8,832]{3,2,1,0:T(8,128)(2,1)} fusion(bf16[16,16,8,192]{3,2,1,0:T(8,128)(2,1)S(1)} %broadcast_in_dim.25, bf16[16,16,8,640]{3,2,1,0:T(8,128)(2,1)S(1)} %fusion.19), kind=kLoop, calls=%fused_computation.17 | loop fusion | flops 6815744 | bytes 6815744 | tf_op jit(solution)/shard_map/concatenate | solution.py:78
  43.6 20.9 %all-to-all-done = bf16[16,16,8,512]{3,2,1,0:T(8,128)(2,1)S(1)} async-done(((bf16[16,16,8,512]{3,2,1,0:T(8,128)(2,1)}), bf16[16,16,8,512]{3,2,1,0:T(8,128)(2,1)S(1)}, u32[]{:S(2)}, u32[]{:S(2)}) %all-to-all-start) | async-done | bytes 2097184 | tf_op jit(solution)/shard_map/all_to_all | solution.py:82
  64.4 4.9 %all-to-all-start.1 = ((bf16[16,16,8,832]{3,2,1,0:T(8,128)(2,1)}), bf16[16,16,8,832]{3,2,1,0:T(8,128)(2,1)}, u32[]{:S(2)}, u32[]{:S(2)}) async-start(bf16[16,16,8,832]{3,2,1,0:T(8,128)(2,1)} %pad_maximum_fusion), calls=%async_computation.1 | async-start | bytes 7340032 | tf_op jit(solution)/shard_map/all_to_all | solution.py:82
  69.5 0.6 gather_fusion.1
  70.6 9.5 %fusion.29 = bf16[16,16,8,384]{3,2,1,0:T(8,128)(2,1)} fusion(bf16[2048,1536]{1,0:T(8,128)(2,1)} %param.7, bf16[16,128,2048]{2,1,0:T(8,128)(2,1)} %param.6), kind=kOutput, calls=%fused_computation.29 | convolution fusion | flops 3222011904 | bytes 11534336 | tf_op jit(solution)/shard_map/dot_general | solution.py:40
  80.1 3.1 %pad.5 = bf16[256,8,1536]{2,1,0:T(8,128)(2,1)} pad(bf16[256,8,512]{2,1,0:T(8,128)(2,1)S(1)} %bitcast.80, bf16[]{:T(256)} %constant.44.clone.1), padding=0_0x0_0x0_1024 | pad | bytes 8388610 | tf_op jit(solution)/shard_map/jit(_pad)/pad | solution.py:89
  83.2 67.4 %all-to-all-done.1 = bf16[16,16,8,832]{3,2,1,0:T(8,128)(2,1)} async-done(((bf16[16,16,8,832]{3,2,1,0:T(8,128)(2,1)}), bf16[16,16,8,832]{3,2,1,0:T(8,128)(2,1)}, u32[]{:S(2)}, u32[]{:S(2)}) %all-to-all-start.1) | async-done | bytes 3407904 | tf_op jit(solution)/shard_map/all_to_all | solution.py:82
  150.6 4.9 %all-to-all-start.2 = ((bf16[16,16,8,384]{3,2,1,0:T(8,128)(2,1)}), bf16[16,16,8,384]{3,2,1,0:T(8,128)(2,1)}, u32[]{:S(2)}, u32[]{:S(2)}) async-start(bf16[16,16,8,384]{3,2,1,0:T(8,128)(2,1)} %fusion.29), calls=%async_computation.2 | async-start | bytes 3145728 | tf_op jit(solution)/shard_map/all_to_all | solution.py:82
  155.5 1.3 slice.117
  156.8 1.7 copy.30
  158.5 3.5 %slice_dynamic-update-slice_fusion = bf16[256,8,1536]{2,1,0:T(8,128)(2,1)} fusion(bf16[256,8,1536]{2,1,0:T(8,128)(2,1)} %pad.5, bf16[256,8,832]{2,1,0:T(8,128)(2,1)} %bitcast.18), kind=kLoop, calls=%fused_computation.19 | loop fusion | bytes 5242880 | tf_op jit(solution)/shard_map/dynamic_update_slice | solution.py:91
  161.9 7.6 %fusion.1 = f32[8,8]{1,0:T(8,128)S(1)} fusion(f32[8,192]{1,0:T(8,128)S(1)} %broadcast_subtract_fusion.3, f32[8,512]{1,0:T(8,128)S(1)} %broadcast_subtract_fusion.1, bf16[256,8,512,1]{2,1,0,3:T(8,128)(2,1)S(1)} %bitcast.81, bf16[256,8,192]{0,2,1:T(8,128)(2,1)} %copy.30), kind=kOutput, calls=%fused_computation.5 | convolution fusion | flops 3246391296 | bytes 2906368 | tf_op jit(solution)/shard_map/dot_general | solution.py:12
  169.6 12.0 %fusion = f32[8,8]{1,0:T(8,128)S(1)} fusion(f32[8,192]{1,0:T(8,128)S(1)} %broadcast_subtract_fusion.3, f32[8,832]{1,0:T(8,128)S(1)} %broadcast_subtract_fusion, bf16[256,8,832,1]{2,1,0,3:T(8,128)(2,1)} %bitcast.32, bf16[256,8,192]{0,2,1:T(8,128)(2,1)S(1)} %copy-done.1), kind=kOutput, calls=%fused_computation.3 | convolution fusion | flops 5275385856 | bytes 4227328 | tf_op jit(solution)/shard_map/dot_general | solution.py:12
  181.6 10.2 %all-to-all-done.2 = bf16[16,16,8,384]{3,2,1,0:T(8,128)(2,1)} async-done(((bf16[16,16,8,384]{3,2,1,0:T(8,128)(2,1)}), bf16[16,16,8,384]{3,2,1,0:T(8,128)(2,1)}, u32[]{:S(2)}, u32[]{:S(2)}) %all-to-all-start.2) | async-done | bytes 1572896 | tf_op jit(solution)/shard_map/all_to_all | solution.py:82
  191.8 2.7 %constant_dynamic-update-slice_fusion = bf16[256,8,1536]{2,1,0:T(8,128)(2,1)} fusion(bf16[256,8,1536]{2,1,0:T(8,128)(2,1)} %slice_dynamic-update-slice_fusion, bf16[256,8,384]{2,1,0:T(8,128)(2,1)} %bitcast.31), kind=kLoop, calls=%fused_computation.48 | loop fusion | bytes 3145728 | tf_op jit(solution)/shard_map/dynamic_update_slice | solution.py:91
  194.5 5.5 %fusion.2 = f32[8,8]{1,0:T(8,128)S(1)} fusion(f32[8,192]{1,0:T(8,128)S(1)} %broadcast_subtract_fusion.3, f32[8,384]{1,0:T(8,128)S(1)} %broadcast_subtract_fusion.2, bf16[256,8,384,1]{2,1,0,3:T(8,128)(2,1)} %bitcast.33, bf16[256,8,192]{0,2,1:T(8,128)(2,1)S(1)} %copy-done.1), kind=kOutput, calls=%fused_computation.7 | convolution fusion | flops 2434793472 | bytes 2377984 | tf_op jit(solution)/shard_map/dot_general | solution.py:12
  200.0 0.6 negate_multiply_fusion
  (38 shorter events, 1.7 us)
Async XLA Ops:
  0.6 22.1 %copy-start.4 = (s32[8]{0:T(128)S(1)}, s32[8]{0:T(128)}, u32[]{:S(2)}) copy-start(s32[8]{0:T(128)} %param.10) | copy-start | bytes 100
  0.6 16.4 %copy-start.3 = (s32[8]{0:T(128)S(1)}, s32[8]{0:T(128)}, u32[]{:S(2)}) copy-start(s32[8]{0:T(128)} %param.11) | copy-start | bytes 100
  10.5 54.0 %all-to-all-start = ((bf16[16,16,8,512]{3,2,1,0:T(8,128)(2,1)}), bf16[16,16,8,512]{3,2,1,0:T(8,128)(2,1)S(1)}, u32[]{:S(2)}, u32[]{:S(2)}) async-start(bf16[16,16,8,512]{3,2,1,0:T(8,128)(2,1)} %fusion.24), calls=%async_computation | async-start | bytes 4194304 | tf_op jit(solution)/shard_map/all_to_all | solution.py:82
  41.2 28.2 %copy-start.2 = (f32[1536]{0:T(1024)S(1)}, f32[1536]{0:T(1024)}, u32[]{:S(2)}) copy-start(f32[1536]{0:T(1024)} %param.9) | copy-start | bytes 18436
  41.2 28.2 %copy-start = (f32[128]{0:T(128)S(1)}, f32[128]{0:T(128)}, u32[]{:S(2)}) copy-start(f32[128]{0:T(128)} %param.8) | copy-start | bytes 1540
  41.2 29.2 %slice-start = ((f32[1536]{0:T(1024)}), f32[512]{0:T(512)S(1)}, s32[]{:S(2)}) async-start(f32[1536]{0:T(1024)} %param.9), calls=%async_computation.3 | async-start | bytes 4096 | tf_op jit(solution)/shard_map/slice | solution.py:99
  64.4 86.1 %all-to-all-start.1 = ((bf16[16,16,8,832]{3,2,1,0:T(8,128)(2,1)}), bf16[16,16,8,832]{3,2,1,0:T(8,128)(2,1)}, u32[]{:S(2)}, u32[]{:S(2)}) async-start(bf16[16,16,8,832]{3,2,1,0:T(8,128)(2,1)} %pad_maximum_fusion), calls=%async_computation.1 | async-start | bytes 7340032 | tf_op jit(solution)/shard_map/all_to_all | solution.py:82
  150.6 41.2 %all-to-all-start.2 = ((bf16[16,16,8,384]{3,2,1,0:T(8,128)(2,1)}), bf16[16,16,8,384]{3,2,1,0:T(8,128)(2,1)}, u32[]{:S(2)}, u32[]{:S(2)}) async-start(bf16[16,16,8,384]{3,2,1,0:T(8,128)(2,1)} %fusion.29), calls=%async_computation.2 | async-start | bytes 3145728 | tf_op jit(solution)/shard_map/all_to_all | solution.py:82
  161.9 7.6 %copy-start.1 = (bf16[256,8,192]{0,2,1:T(8,128)(2,1)S(1)}, bf16[256,8,192]{0,2,1:T(8,128)(2,1)}, u32[]{:S(2)}) copy-start(bf16[256,8,192]{0,2,1:T(8,128)(2,1)} %copy.30) | copy-start | bytes 2359300

commit v16 on v11

--- a/solution.py
+++ b/solution.py
@@ -60,8 +60,15 @@
     )
     scale = 1.0 / (aux_here * groups * nvir * VBLK)
 
-    carrier = min(1, chunks - 1) if ride else -1
-    if not ride:
+    carrier = -1
+    if groups <= 16:
+        got_pieces = [pieces]
+        for shift in range(1, groups):
+            pairs = [(d, (d - shift) % groups) for d in range(groups)]
+            got_pieces.append(lax.ppermute(pieces, "occ", pairs))
+        stacked = jnp.stack(got_pieces)
+        blocks = jnp.roll(stacked, me, axis=0).reshape(groups * aux_here, step_count, VBLK)
+    else:
         blocks = lax.all_gather(pieces, "occ", axis=0, tiled=True)
     raw = []
     sums = []

time: 198 us -> 225 us (1.14)
  local copies, waits for them, and re-layouts: 19.3 us -> 51 us
  starting transfers between devices: 16.4 us -> 47.3 us
  waiting for transfers between devices: 94.2 us -> 65 us
  matrix products: 58.1 us -> 52.4 us
    ppermute x0 -> x15, starting transfers between devices: none -> 30.9 us  [per_device(): got_pieces.append(lax.ppermute(pieces, 'occ', pairs))]
    all_to_all x3, waiting for transfers between devices: 94.2 us -> 65 us  [per_device(): lax.all_to_all(product, 'occ', split_axis=0, concat_axis=0, tiled=True)]
    unnamed x13 -> x71, local copies, waits for them, and re-layouts: 2.67 us -> 28.5 us
    dot_general x3, matrix products: 25.3 us -> 18.5 us  [chunk_energies(): lax.dot_general(factors, blocks, (((0,), (0,)), ((), ())), preferred_elem...]
    reshape x0 -> x1, local copies, waits for them, and re-layouts: none -> 2.64 us  [per_device(): jnp.roll(stacked, me, axis=0).reshape(groups * aux_here, step_count, VBLK)]
    concatenate x1 -> x0, other arithmetic: 2.61 us -> none  [per_device(): product = jnp.concatenate([product, extra], axis=3)]
    dynamic_slice x0 -> x1, local copies, waits for them, and re-layouts: none -> 2.28 us  [per_device(): jnp.roll(stacked, me, axis=0).reshape(groups * aux_here, step_count, VBLK)]
    slice x2 -> x0, local copies, waits for them, and re-layouts: 2.26 us -> none  [the longest x1 2.25 us: per_device(): blocks = got[:, :, span:]]
  transfers between devices with their start and end apart: 3 -> 18, of which waited for: 3 -> 2; matrix products, arithmetic and copies ran while one was open for 33% -> 33% of each run, Pallas kernels for 0% -> 0%
where the time goes in v16:
time: 225 us; the launch traced here: 224 us
  waiting for transfers between devices  65 us (29%)
  matrix products  52.4 us (23%)
  local copies, waits for them, and re-layouts  51 us (23%)
  starting transfers between devices  47.3 us (21%)
  between operations  5.97 us (3%)
  other arithmetic  2.65 us (1%)
    all_to_all x3, waiting for transfers between devices, per_device(): lax.all_to_all(product, 'occ', split_axis=0, concat_axis=0, tiled=True)  65 us
    ppermute x15, starting transfers between devices, per_device(): got_pieces.append(lax.ppermute(pieces, 'occ', pairs))  30.9 us
    dot_general x3, matrix products, chunk_product(): lax.dot_general(rows, orbitals[:, bounds[c]:bounds[c + 1]], (((3,), (0,))...  30.1 us
    unnamed x71, local copies, waits for them, and re-layouts  28.5 us
    dot_general x3, matrix products, chunk_energies(): lax.dot_general(factors, blocks, (((0,), (0,)), ((), ())), preferred_elem...  18.5 us
    all_to_all x3, starting transfers between devices, per_device(): lax.all_to_all(product, 'occ', split_axis=0, concat_axis=0, tiled=True)  16.4 us
    pad x1, local copies, waits for them, and re-layouts, per_device(): factors = jnp.pad(got, ((0, 0), (0, 0), (0, nvir - span)))  4.71 us
    dynamic_update_slice x2, local copies, waits for them, and re-layouts, per_device(): factors = lax.dynamic_update_slice(factors, got, (0, 0, bounds[c]))  4.57 us
  transfers between devices with their start and end apart: 18, of which 2 were waited for; matrix products, arithmetic and copies ran while one was open for 33% of the time, Pallas kernels for 0%

profile of v16, /device:TPU:13, one launch (start us, length us, event | category | flops | bytes accessed | tf_op | source)
XLA Modules:
  0.0 224.4 jit_solution(16805223932277575389)
XLA Ops:
  7.3 9.5 %fusion.21 = bf16[16,16,8,384]{3,2,1,0:T(8,128)(2,1)} fusion(bf16[2048,1536]{1,0:T(8,128)(2,1)} %param.7, bf16[16,128,2048]{2,1,0:T(8,128)(2,1)} %param.6), kind=kOutput, calls=%fused_computation.23 | convolution fusion | flops 3222011904 | bytes 11534336 | tf_op jit(solution)/shard_map/dot_general | solution.py:38
  16.8 2.6 %gather_fusion = bf16[8,16,2048]{2,0,1:T(8,128)(2,1)S(1)} fusion(bf16[16,128,2048]{2,1,0:T(8,128)(2,1)} %param.6, s32[1024]{0:T(1024)S(1)} %pad_clamp_fusion.1), kind=kCustom, calls=%fused_computation | custom fusion | bytes 1048608 | tf_op jit(solution)/shard_map/jit(_take)/gather | solution.py:45
  19.5 3.8 %fusion.15 = bf16[16,8,1536]{2,1,0:T(8,128)(2,1)S(1)} fusion(bf16[2048,1536]{1,0:T(8,128)(2,1)} %param.7, bf16[8,16,2048]{2,0,1:T(8,128)(2,1)S(1)} %gather_fusion, pred[128]{0:T(512)(128)(4,1)S(1)} %broadcast_in_dim.19), kind=kOutput, calls=%fused_computation.21 | convolution fusion | flops 805765120 | bytes 7209088 | tf_op jit(solution)/shard_map/dot_general | solution.py:46
  27.5 3.3 %collective-permute-start.3 = (bf16[16,8,192]{2,1,0:T(8,128)(2,1)S(1)}, bf16[16,8,192]{2,1,0:T(8,128)(2,1)S(1)}, u32[]{:S(2)}, u32[]{:S(2)}) collective-permute-start(bf16[16,8,192]{2,1,0:T(8,128)(2,1)S(1)} %stack.87), channel_id=1, source_target_pairs={{0,12},{1,13},{2,14},{3,15},{4,0},{5,1},{6,2},{7,3},{8,4},{9,5},{1... | collective-permute-start | bytes 147464 | tf_op jit(solution)/shard_map/ppermute | solution.py:68
  30.9 7.1 %all-to-all-start = ((bf16[16,16,8,384]{3,2,1,0:T(8,128)(2,1)}), bf16[16,16,8,384]{3,2,1,0:T(8,128)(2,1)S(1)}, u32[]{:S(2)}, u32[]{:S(2)}) async-start(bf16[16,16,8,384]{3,2,1,0:T(8,128)(2,1)} %fusion.21), calls=%async_computation | async-start | bytes 3145728 | tf_op jit(solution)/shard_map/all_to_all | solution.py:87
  38.7 11.2 %fusion.16 = bf16[16,16,8,768]{3,2,1,0:T(8,128)(2,1)} fusion(bf16[2048,1536]{1,0:T(8,128)(2,1)} %param.7, bf16[16,128,2048]{2,1,0:T(8,128)(2,1)} %param.6), kind=kOutput, calls=%fused_computation.22 | convolution fusion | flops 6444023808 | bytes 14680064 | tf_op jit(solution)/shard_map/dot_general | solution.py:38
  49.9 9.4 %fusion.24 = bf16[16,16,8,384]{3,2,1,0:T(8,128)(2,1)} fusion(bf16[2048,1536]{1,0:T(8,128)(2,1)} %param.7, bf16[16,128,2048]{2,1,0:T(8,128)(2,1)} %param.6), kind=kOutput, calls=%fused_computation.24 | convolution fusion | flops 3222011904 | bytes 11534336 | tf_op jit(solution)/shard_map/dot_general | solution.py:38
  62.9 3.7 %collective-permute-start.6 = (bf16[16,8,192]{2,1,0:T(8,128)(2,1)S(1)}, bf16[16,8,192]{2,1,0:T(8,128)(2,1)S(1)}, u32[]{:S(2)}, u32[]{:S(2)}) collective-permute-start(bf16[16,8,192]{2,1,0:T(8,128)(2,1)S(1)} %stack.87), channel_id=1, source_target_pairs={{0,9},{1,10},{2,11},{3,12},{4,13},{5,14},{6,15},{7,0},{8,1},{9,2},... | collective-permute-start | bytes 147464 | tf_op jit(solution)/shard_map/ppermute | solution.py:68
  70.0 3.0 %collective-permute-start.9 = (bf16[16,8,192]{2,1,0:T(8,128)(2,1)S(1)}, bf16[16,8,192]{2,1,0:T(8,128)(2,1)S(1)}, u32[]{:S(2)}, u32[]{:S(2)}) collective-permute-start(bf16[16,8,192]{2,1,0:T(8,128)(2,1)S(1)} %stack.87), channel_id=1, source_target_pairs={{0,6},{1,7},{2,8},{3,9},{4,10},{5,11},{6,12},{7,13},{8,14},{9,15},... | collective-permute-start | bytes 147464 | tf_op jit(solution)/shard_map/ppermute | solution.py:68
  73.6 2.3 %collective-permute-start.10 = (bf16[16,8,192]{2,1,0:T(8,128)(2,1)S(1)}, bf16[16,8,192]{2,1,0:T(8,128)(2,1)S(1)}, u32[]{:S(2)}, u32[]{:S(2)}) collective-permute-start(bf16[16,8,192]{2,1,0:T(8,128)(2,1)S(1)} %stack.87), channel_id=1, source_target_pairs={{0,5},{1,6},{2,7},{3,8},{4,9},{5,10},{6,11},{7,12},{8,13},{9,14},{... | collective-permute-start | bytes 147464 | tf_op jit(solution)/shard_map/ppermute | solution.py:68
  76.6 4.5 %collective-permute-start.11 = (bf16[16,8,192]{2,1,0:T(8,128)(2,1)S(1)}, bf16[16,8,192]{2,1,0:T(8,128)(2,1)S(1)}, u32[]{:S(2)}, u32[]{:S(2)}) collective-permute-start(bf16[16,8,192]{2,1,0:T(8,128)(2,1)S(1)} %stack.87), channel_id=1, source_target_pairs={{0,4},{1,5},{2,6},{3,7},{4,8},{5,9},{6,10},{7,11},{8,12},{9,13},{1... | collective-permute-start | bytes 147464 | tf_op jit(solution)/shard_map/ppermute | solution.py:68
  81.7 6.8 %collective-permute-start.12 = (bf16[16,8,192]{2,1,0:T(8,128)(2,1)S(1)}, bf16[16,8,192]{2,1,0:T(8,128)(2,1)S(1)}, u32[]{:S(2)}, u32[]{:S(2)}) collective-permute-start(bf16[16,8,192]{2,1,0:T(8,128)(2,1)S(1)} %stack.87), channel_id=1, source_target_pairs={{0,3},{1,4},{2,5},{3,6},{4,7},{5,8},{6,9},{7,10},{8,11},{9,12},{10... | collective-permute-start | bytes 147464 | tf_op jit(solution)/shard_map/ppermute | solution.py:68
  98.2 4.4 %all-to-all-start.1 = ((bf16[16,16,8,768]{3,2,1,0:T(8,128)(2,1)}), bf16[16,16,8,768]{3,2,1,0:T(8,128)(2,1)S(1)}, u32[]{:S(2)}, u32[]{:S(2)}) async-start(bf16[16,16,8,768]{3,2,1,0:T(8,128)(2,1)} %fusion.16), calls=%async_computation.1 | async-start | bytes 6291456 | tf_op jit(solution)/shard_map/all_to_all | solution.py:87
  121.1 2.3 %constant_dynamic-slice_fusion = bf16[16,16,8,192]{3,2,1,0:T(8,128)(2,1)} fusion(bf16[32,16,8,192]{3,2,1,0:T(8,128)(2,1)} %constant_dynamic-update-slice_fusion, s32[]{:T(128)S(6)} %select_n.72), kind=kLoop, calls=%fused_computation.80 | loop fusion | bytes 1572868 | tf_op jit(solution)/shard_map/jit(_roll_dynamic)/dynamic_slice | solution.py:70
  123.4 2.6 %copy.15 = bf16[256,8,192]{0,2,1:T(8,128)(2,1)} copy(bf16[256,8,192]{2,1,0:T(8,128)(2,1)} %bitcast.132) | data formatting | bytes 1572864 | tf_op jit(solution)/shard_map/reshape | solution.py:70
  126.0 4.7 %pad.4 = bf16[256,8,1536]{2,1,0:T(8,128)(2,1)} pad(bf16[256,8,384]{2,1,0:T(8,128)(2,1)} %bitcast.130, bf16[]{:T(256)} %constant.61.clone.1), padding=0_0x0_0x0_1152 | pad | bytes 7864322 | tf_op jit(solution)/shard_map/jit(_pad)/pad | solution.py:94
  130.8 4.1 %fusion.1 = f32[8,8]{1,0:T(8,128)S(1)} fusion(f32[8,192]{1,0:T(8,128)S(1)} %copy-done.18, f32[8,384]{1,0:T(8,128)S(1)} %copy-done.17, bf16[256,8,384,1]{2,1,0,3:T(8,128)(2,1)S(1)} %bitcast.131, bf16[256,8,192]{0,2,1:T(8,128)(2,1)S(1)} %copy-done.3), kind=kOutput, calls=%fused_computation.6 | convolution fusion | flops 2434793472 | bytes 2377984 | tf_op jit(solution)/shard_map/dot_general | solution.py:11
  134.9 37.6 %all-to-all-done.1 = bf16[16,16,8,768]{3,2,1,0:T(8,128)(2,1)S(1)} async-done(((bf16[16,16,8,768]{3,2,1,0:T(8,128)(2,1)}), bf16[16,16,8,768]{3,2,1,0:T(8,128)(2,1)S(1)}, u32[]{:S(2)}, u32[]{:S(2)}) %all-to-all-start.1) | async-done | bytes 3145760 | tf_op jit(solution)/shard_map/all_to_all | solution.py:87
  172.5 1.9 constant_dynamic-update-slice_fusion.33
  174.3 4.9 %all-to-all-start.2 = ((bf16[16,16,8,384]{3,2,1,0:T(8,128)(2,1)}), bf16[16,16,8,384]{3,2,1,0:T(8,128)(2,1)}, u32[]{:S(2)}, u32[]{:S(2)}) async-start(bf16[16,16,8,384]{3,2,1,0:T(8,128)(2,1)} %fusion.24), calls=%async_computation.2 | async-start | bytes 3145728 | tf_op jit(solution)/shard_map/all_to_all | solution.py:87
  179.3 8.9 %fusion = f32[8,8]{1,0:T(8,128)S(1)} fusion(f32[8,192]{1,0:T(8,128)S(1)} %copy-done.18, f32[8,768]{1,0:T(8,128)S(1)} %copy-done.16, bf16[256,8,768,1]{2,1,0,3:T(8,128)(2,1)S(1)} %bitcast.129, bf16[256,8,192]{0,2,1:T(8,128)(2,1)} %copy.15), kind=kOutput, calls=%fused_computation.3 | convolution fusion | flops 4869586944 | bytes 3963136 | tf_op jit(solution)/shard_map/dot_general | solution.py:11
  188.2 27.4 %all-to-all-done.2 = bf16[16,16,8,384]{3,2,1,0:T(8,128)(2,1)} async-done(((bf16[16,16,8,384]{3,2,1,0:T(8,128)(2,1)}), bf16[16,16,8,384]{3,2,1,0:T(8,128)(2,1)}, u32[]{:S(2)}, u32[]{:S(2)}) %all-to-all-start.2) | async-done | bytes 1572896 | tf_op jit(solution)/shard_map/all_to_all | solution.py:87
  215.6 2.7 %constant_dynamic-update-slice_fusion.32 = bf16[256,8,1536]{2,1,0:T(8,128)(2,1)} fusion(bf16[256,8,1536]{2,1,0:T(8,128)(2,1)} %constant_dynamic-update-slice_fusion.33, bf16[256,8,384]{2,1,0:T(8,128)(2,1)} %bitcast.50), kind=kLoop, calls=%fused_computation.78 | loop fusion | bytes 3145728 | tf_op jit(solution)/shard_map/dynamic_update_slice | solution.py:96
  218.3 5.5 %fusion.2 = f32[8,8]{1,0:T(8,128)S(1)} fusion(f32[8,384]{1,0:T(8,128)S(1)} %get-tuple-element.36, f32[8,192]{1,0:T(8,128)S(1)} %copy-done.18, bf16[256,8,384,1]{2,1,0,3:T(8,128)(2,1)} %bitcast.51, bf16[256,8,192]{0,2,1:T(8,128)(2,1)S(1)} %copy-done.4), kind=kOutput, calls=%fused_computation.7 | convolution fusion | flops 2434793472 | bytes 2377984 | tf_op jit(solution)/shard_map/dot_general | solution.py:11
  (124 shorter events, 44.2 us)
Async XLA Ops:
  7.3 9.5 %copy-start.19 = (s32[8]{0:T(128)S(1)}, s32[8]{0:T(128)}, u32[]{:S(2)}) copy-start(s32[8]{0:T(128)} %param.10) | copy-start | bytes 100
  24.1 13.9 %copy-start.15 = (f32[1536]{0:T(1024)S(1)}, f32[1536]{0:T(1024)}, u32[]{:S(2)}) copy-start(f32[1536]{0:T(1024)} %param.9) | copy-start | bytes 18436
  25.2 37.0 %collective-permute-start = (bf16[16,8,192]{2,1,0:T(8,128)(2,1)S(1)}, bf16[16,8,192]{2,1,0:T(8,128)(2,1)S(1)}, u32[]{:S(2)}, u32[]{:S(2)}) collective-permute-start(bf16[16,8,192]{2,1,0:T(8,128)(2,1)S(1)} %stack.87), channel_id=1, source_target_pairs={{0,15},{1,0},{2,1},{3,2},{4,3},{5,4},{6,5},{7,6},{8,7},{9,8},{10,9... | collective-permute-start | bytes 147464 | tf_op jit(solution)/shard_map/ppermute | solution.py:68
  25.9 37.0 %collective-permute-start.1 = (bf16[16,8,192]{2,1,0:T(8,128)(2,1)S(1)}, bf16[16,8,192]{2,1,0:T(8,128)(2,1)S(1)}, u32[]{:S(2)}, u32[]{:S(2)}) collective-permute-start(bf16[16,8,192]{2,1,0:T(8,128)(2,1)S(1)} %stack.87), channel_id=1, source_target_pairs={{0,14},{1,15},{2,0},{3,1},{4,2},{5,3},{6,4},{7,5},{8,6},{9,7},{10,... | collective-permute-start | bytes 147464 | tf_op jit(solution)/shard_map/ppermute | solution.py:68
  26.1 41.1 %collective-permute-start.2 = (bf16[16,8,192]{2,1,0:T(8,128)(2,1)S(1)}, bf16[16,8,192]{2,1,0:T(8,128)(2,1)S(1)}, u32[]{:S(2)}, u32[]{:S(2)}) collective-permute-start(bf16[16,8,192]{2,1,0:T(8,128)(2,1)S(1)} %stack.87), channel_id=1, source_target_pairs={{0,13},{1,14},{2,15},{3,0},{4,1},{5,2},{6,3},{7,4},{8,5},{9,6},{10... | collective-permute-start | bytes 147464 | tf_op jit(solution)/shard_map/ppermute | solution.py:68
  27.5 40.6 %collective-permute-start.3 = (bf16[16,8,192]{2,1,0:T(8,128)(2,1)S(1)}, bf16[16,8,192]{2,1,0:T(8,128)(2,1)S(1)}, u32[]{:S(2)}, u32[]{:S(2)}) collective-permute-start(bf16[16,8,192]{2,1,0:T(8,128)(2,1)S(1)} %stack.87), channel_id=1, source_target_pairs={{0,12},{1,13},{2,14},{3,15},{4,0},{5,1},{6,2},{7,3},{8,4},{9,5},{1... | collective-permute-start | bytes 147464 | tf_op jit(solution)/shard_map/ppermute | solution.py:68
  30.8 39.2 %collective-permute-start.4 = (bf16[16,8,192]{2,1,0:T(8,128)(2,1)S(1)}, bf16[16,8,192]{2,1,0:T(8,128)(2,1)S(1)}, u32[]{:S(2)}, u32[]{:S(2)}) collective-permute-start(bf16[16,8,192]{2,1,0:T(8,128)(2,1)S(1)} %stack.87), channel_id=1, source_target_pairs={{0,11},{1,12},{2,13},{3,14},{4,15},{5,0},{6,1},{7,2},{8,3},{9,4},{... | collective-permute-start | bytes 147464 | tf_op jit(solution)/shard_map/ppermute | solution.py:68
  30.9 66.1 %all-to-all-start = ((bf16[16,16,8,384]{3,2,1,0:T(8,128)(2,1)}), bf16[16,16,8,384]{3,2,1,0:T(8,128)(2,1)S(1)}, u32[]{:S(2)}, u32[]{:S(2)}) async-start(bf16[16,16,8,384]{3,2,1,0:T(8,128)(2,1)} %fusion.21), calls=%async_computation | async-start | bytes 3145728 | tf_op jit(solution)/shard_map/all_to_all | solution.py:87
  62.1 11.5 %collective-permute-start.5 = (bf16[16,8,192]{2,1,0:T(8,128)(2,1)S(1)}, bf16[16,8,192]{2,1,0:T(8,128)(2,1)S(1)}, u32[]{:S(2)}, u32[]{:S(2)}) collective-permute-start(bf16[16,8,192]{2,1,0:T(8,128)(2,1)S(1)} %stack.87), channel_id=1, source_target_pairs={{0,10},{1,11},{2,12},{3,13},{4,14},{5,15},{6,0},{7,1},{8,2},{9,3},... | collective-permute-start | bytes 147464 | tf_op jit(solution)/shard_map/ppermute | solution.py:68
  62.9 13.7 %collective-permute-start.6 = (bf16[16,8,192]{2,1,0:T(8,128)(2,1)S(1)}, bf16[16,8,192]{2,1,0:T(8,128)(2,1)S(1)}, u32[]{:S(2)}, u32[]{:S(2)}) collective-permute-start(bf16[16,8,192]{2,1,0:T(8,128)(2,1)S(1)} %stack.87), channel_id=1, source_target_pairs={{0,9},{1,10},{2,11},{3,12},{4,13},{5,14},{6,15},{7,0},{8,1},{9,2},... | collective-permute-start | bytes 147464 | tf_op jit(solution)/shard_map/ppermute | solution.py:68
  67.2 14.5 %collective-permute-start.7 = (bf16[16,8,192]{2,1,0:T(8,128)(2,1)S(1)}, bf16[16,8,192]{2,1,0:T(8,128)(2,1)S(1)}, u32[]{:S(2)}, u32[]{:S(2)}) collective-permute-start(bf16[16,8,192]{2,1,0:T(8,128)(2,1)S(1)} %stack.87), channel_id=1, source_target_pairs={{0,8},{1,9},{2,10},{3,11},{4,12},{5,13},{6,14},{7,15},{8,0},{9,1},... | collective-permute-start | bytes 147464 | tf_op jit(solution)/shard_map/ppermute | solution.py:68
  68.1 21.0 %collective-permute-start.8 = (bf16[16,8,192]{2,1,0:T(8,128)(2,1)S(1)}, bf16[16,8,192]{2,1,0:T(8,128)(2,1)S(1)}, u32[]{:S(2)}, u32[]{:S(2)}) collective-permute-start(bf16[16,8,192]{2,1,0:T(8,128)(2,1)S(1)} %stack.87), channel_id=1, source_target_pairs={{0,7},{1,8},{2,9},{3,10},{4,11},{5,12},{6,13},{7,14},{8,15},{9,0},... | collective-permute-start | bytes 147464 | tf_op jit(solution)/shard_map/ppermute | solution.py:68
  70.0 21.3 %collective-permute-start.9 = (bf16[16,8,192]{2,1,0:T(8,128)(2,1)S(1)}, bf16[16,8,192]{2,1,0:T(8,128)(2,1)S(1)}, u32[]{:S(2)}, u32[]{:S(2)}) collective-permute-start(bf16[16,8,192]{2,1,0:T(8,128)(2,1)S(1)} %stack.87), channel_id=1, source_target_pairs={{0,6},{1,7},{2,8},{3,9},{4,10},{5,11},{6,12},{7,13},{8,14},{9,15},... | collective-permute-start | bytes 147464 | tf_op jit(solution)/shard_map/ppermute | solution.py:68
  73.6 23.4 %copy-start.5 = (bf16[16,8,192]{2,1,0:T(8,128)(2,1)}, bf16[16,8,192]{2,1,0:T(8,128)(2,1)S(1)}, u32[]{:S(2)}) copy-start(bf16[16,8,192]{2,1,0:T(8,128)(2,1)S(1)} %collective-permute-done.5) | copy-start | bytes 147460
  73.6 20.1 %collective-permute-start.10 = (bf16[16,8,192]{2,1,0:T(8,128)(2,1)S(1)}, bf16[16,8,192]{2,1,0:T(8,128)(2,1)S(1)}, u32[]{:S(2)}, u32[]{:S(2)}) collective-permute-start(bf16[16,8,192]{2,1,0:T(8,128)(2,1)S(1)} %stack.87), channel_id=1, source_target_pairs={{0,5},{1,6},{2,7},{3,8},{4,9},{5,10},{6,11},{7,12},{8,13},{9,14},{... | collective-permute-start | bytes 147464 | tf_op jit(solution)/shard_map/ppermute | solution.py:68
  76.6 20.4 %copy-start.6 = (bf16[16,8,192]{2,1,0:T(8,128)(2,1)}, bf16[16,8,192]{2,1,0:T(8,128)(2,1)S(1)}, u32[]{:S(2)}) copy-start(bf16[16,8,192]{2,1,0:T(8,128)(2,1)S(1)} %collective-permute-done.6) | copy-start | bytes 147460
  76.6 17.8 %collective-permute-start.11 = (bf16[16,8,192]{2,1,0:T(8,128)(2,1)S(1)}, bf16[16,8,192]{2,1,0:T(8,128)(2,1)S(1)}, u32[]{:S(2)}, u32[]{:S(2)}) collective-permute-start(bf16[16,8,192]{2,1,0:T(8,128)(2,1)S(1)} %stack.87), channel_id=1, source_target_pairs={{0,4},{1,5},{2,6},{3,7},{4,8},{5,9},{6,10},{7,11},{8,12},{9,13},{1... | collective-permute-start | bytes 147464 | tf_op jit(solution)/shard_map/ppermute | solution.py:68
  81.7 15.3 %copy-start.7 = (bf16[16,8,192]{2,1,0:T(8,128)(2,1)}, bf16[16,8,192]{2,1,0:T(8,128)(2,1)S(1)}, u32[]{:S(2)}) copy-start(bf16[16,8,192]{2,1,0:T(8,128)(2,1)S(1)} %collective-permute-done.7) | copy-start | bytes 147460
  81.7 13.3 %collective-permute-start.12 = (bf16[16,8,192]{2,1,0:T(8,128)(2,1)S(1)}, bf16[16,8,192]{2,1,0:T(8,128)(2,1)S(1)}, u32[]{:S(2)}, u32[]{:S(2)}) collective-permute-start(bf16[16,8,192]{2,1,0:T(8,128)(2,1)S(1)} %stack.87), channel_id=1, source_target_pairs={{0,3},{1,4},{2,5},{3,6},{4,7},{5,8},{6,9},{7,10},{8,11},{9,12},{10... | collective-permute-start | bytes 147464 | tf_op jit(solution)/shard_map/ppermute | solution.py:68
  89.1 6.6 %collective-permute-start.13 = (bf16[16,8,192]{2,1,0:T(8,128)(2,1)S(1)}, bf16[16,8,192]{2,1,0:T(8,128)(2,1)S(1)}, u32[]{:S(2)}, u32[]{:S(2)}) collective-permute-start(bf16[16,8,192]{2,1,0:T(8,128)(2,1)S(1)} %stack.87), channel_id=1, source_target_pairs={{0,2},{1,3},{2,4},{3,5},{4,6},{5,7},{6,8},{7,9},{8,10},{9,11},{10,... | collective-permute-start | bytes 147464 | tf_op jit(solution)/shard_map/ppermute | solution.py:68
  91.3 5.0 %collective-permute-start.14 = (bf16[16,8,192]{2,1,0:T(8,128)(2,1)S(1)}, bf16[16,8,192]{2,1,0:T(8,128)(2,1)S(1)}, u32[]{:S(2)}, u32[]{:S(2)}) collective-permute-start(bf16[16,8,192]{2,1,0:T(8,128)(2,1)S(1)} %stack.87), channel_id=1, source_target_pairs={{0,1},{1,2},{2,3},{3,4},{4,5},{5,6},{6,7},{7,8},{8,9},{9,10},{10,1... | collective-permute-start | bytes 147464 | tf_op jit(solution)/shard_map/ppermute | solution.py:68
  98.2 74.3 %all-to-all-start.1 = ((bf16[16,16,8,768]{3,2,1,0:T(8,128)(2,1)}), bf16[16,16,8,768]{3,2,1,0:T(8,128)(2,1)S(1)}, u32[]{:S(2)}, u32[]{:S(2)}) async-start(bf16[16,16,8,768]{3,2,1,0:T(8,128)(2,1)} %fusion.16), calls=%async_computation.1 | async-start | bytes 6291456 | tf_op jit(solution)/shard_map/all_to_all | solution.py:87
  174.3 41.2 %all-to-all-start.2 = ((bf16[16,16,8,384]{3,2,1,0:T(8,128)(2,1)}), bf16[16,16,8,384]{3,2,1,0:T(8,128)(2,1)}, u32[]{:S(2)}, u32[]{:S(2)}) async-start(bf16[16,16,8,384]{3,2,1,0:T(8,128)(2,1)} %fusion.24), calls=%async_computation.2 | async-start | bytes 3145728 | tf_op jit(solution)/shard_map/all_to_all | solution.py:87
  188.2 30.1 %copy-start.4 = (bf16[256,8,192]{0,2,1:T(8,128)(2,1)S(1)}, bf16[256,8,192]{0,2,1:T(8,128)(2,1)}, u32[]{:S(2)}) copy-start(bf16[256,8,192]{0,2,1:T(8,128)(2,1)} %copy.15) | copy-start | bytes 2359300
  (14 other events, 58.2 us)

commit v17 on v15

--- a/solution.py
+++ b/solution.py
@@ -5,7 +5,7 @@
 
 VBLK = 192
 EDGE_PART = 4
-LEAD_PART = 3
+LEAD_PART = 12
 
 
 def chunk_energies(factors, blocks, occ_rows, occ_cols, vir_chunk, vir_blocks, scale):

time: 201 us -> 216 us (1.075)
  waiting for transfers between devices: 98.4 us -> 110 us
  other arithmetic: 3.29 us -> 6.12 us
    all_to_all x3, waiting for transfers between devices: 98.4 us -> 110 us  [per_device(): lax.all_to_all(product, 'occ', split_axis=0, concat_axis=0, tiled=True)]
    concatenate x1, other arithmetic: 2.38 us -> 5.21 us  [per_device(): product = jnp.concatenate([product, extra], axis=3)]
    unnamed x11 -> x15, local copies, waits for them, and re-layouts: 1.72 us -> 4.44 us
    dot_general x3, matrix products: 25.1 us -> 22.8 us  [chunk_energies(): lax.dot_general(factors, blocks, (((0,), (0,)), ((), ())), preferred_elem...]
    dynamic_update_slice x2, local copies, waits for them, and re-layouts: 6.16 us -> 4 us  [per_device(): factors = lax.dynamic_update_slice(factors, got, (0, 0, bounds[c]))]
  transfers between devices with their start and end apart: 3 -> 3, of which waited for: 3 -> 2; matrix products, arithmetic and copies ran while one was open for 30% -> 31% of each run, Pallas kernels for 0% -> 0%
where the time goes in v17:
time: 216 us; the launch traced here: 215 us
  waiting for transfers between devices  110 us (51%)
  matrix products  56.4 us (26%)
  local copies, waits for them, and re-layouts  18.9 us (9%)
  starting transfers between devices  17.6 us (8%)
  other arithmetic  6.12 us (3%)
  between operations  5.87 us (3%)
    all_to_all x3, waiting for transfers between devices, per_device(): lax.all_to_all(product, 'occ', split_axis=0, concat_axis=0, tiled=True)  110 us
    dot_general x3, matrix products, chunk_product(): lax.dot_general(rows, orbitals[:, bounds[c]:bounds[c + 1]], (((3,), (0,))...  29.8 us
    dot_general x3, matrix products, chunk_energies(): lax.dot_general(factors, blocks, (((0,), (0,)), ((), ())), preferred_elem...  22.8 us
    all_to_all x3, starting transfers between devices, per_device(): lax.all_to_all(product, 'occ', split_axis=0, concat_axis=0, tiled=True)  17.6 us
    concatenate x1, other arithmetic, per_device(): product = jnp.concatenate([product, extra], axis=3)  5.21 us
    unnamed x15, local copies, waits for them, and re-layouts  4.44 us
  transfers between devices with their start and end apart: 3, of which 2 were waited for; matrix products, arithmetic and copies ran while one was open for 31% of the time, Pallas kernels for 0%

profile of v17, /device:TPU:13, one launch (start us, length us, event | category | flops | bytes accessed | tf_op | source)
XLA Modules:
  0.0 215.2 jit_solution(7181187438665503983)
XLA Ops:
  0.6 6.6 %fusion.27 = bf16[16,16,8,128]{3,2,1,0:T(8,128)(2,1)} fusion(bf16[2048,1536]{1,0:T(8,128)(2,1)} %param.7, bf16[16,128,2048]{2,1,0:T(8,128)(2,1)} %param.6), kind=kOutput, calls=%fused_computation.29 | convolution fusion | flops 1074003968 | bytes 9437184 | tf_op jit(solution)/shard_map/dot_general | solution.py:40
  7.2 6.6 %all-to-all-start = ((bf16[16,16,8,128]{3,2,1,0:T(8,128)(2,1)}), bf16[16,16,8,128]{3,2,1,0:T(8,128)(2,1)S(1)}, u32[]{:S(2)}, u32[]{:S(2)}) async-start(bf16[16,16,8,128]{3,2,1,0:T(8,128)(2,1)} %fusion.27), calls=%async_computation | async-start | bytes 1048576 | tf_op jit(solution)/shard_map/all_to_all | solution.py:82
  13.8 0.7 fusion.41
  19.5 13.8 %fusion.15 = bf16[16,16,8,1024]{3,2,1,0:T(8,128)(2,1)} fusion(bf16[2048,1536]{1,0:T(8,128)(2,1)} %param.7, bf16[16,128,2048]{2,1,0:T(8,128)(2,1)} %param.6), kind=kOutput, calls=%fused_computation.22 | convolution fusion | flops 8592031744 | bytes 16777216 | tf_op jit(solution)/shard_map/dot_general | solution.py:40
  33.4 2.6 %gather_fusion = bf16[8,16,2048]{2,0,1:T(8,128)(2,1)S(1)} fusion(bf16[16,128,2048]{2,1,0:T(8,128)(2,1)} %param.6, s32[1024]{0:T(1024)S(1)} %pad_clamp_fusion.1), kind=kCustom, calls=%fused_computation | custom fusion | bytes 1048608 | tf_op jit(solution)/shard_map/jit(_take)/gather | solution.py:47
  36.0 3.8 %fusion.20 = bf16[16,8,1536]{2,1,0:T(8,128)(2,1)S(1)} fusion(bf16[2048,1536]{1,0:T(8,128)(2,1)} %param.7, bf16[8,16,2048]{2,0,1:T(8,128)(2,1)S(1)} %gather_fusion, pred[128]{0:T(512)(128)(4,1)S(1)} %broadcast_in_dim.21), kind=kOutput, calls=%fused_computation.24 | convolution fusion | flops 805765120 | bytes 7209088 | tf_op jit(solution)/shard_map/dot_general | solution.py:48
  39.8 0.7 fusion.39
  41.7 5.2 %pad_maximum_fusion = bf16[16,16,8,1216]{3,2,1,0:T(8,128)(2,1)} fusion(bf16[16,16,8,192]{3,2,1,0:T(8,128)(2,1)S(1)} %broadcast_in_dim.25, bf16[16,16,8,1024]{3,2,1,0:T(8,128)(2,1)} %fusion.15), kind=kLoop, calls=%fused_computation.17 | loop fusion | flops 9961472 | bytes 9961472 | tf_op jit(solution)/shard_map/concatenate | solution.py:78
  47.0 6.2 %all-to-all-start.1 = ((bf16[16,16,8,1216]{3,2,1,0:T(8,128)(2,1)}), bf16[16,16,8,1216]{3,2,1,0:T(8,128)(2,1)}, u32[]{:S(2)}, u32[]{:S(2)}) async-start(bf16[16,16,8,1216]{3,2,1,0:T(8,128)(2,1)} %pad_maximum_fusion), calls=%async_computation.1 | async-start | bytes 10485760 | tf_op jit(solution)/shard_map/all_to_all | solution.py:82
  53.2 0.6 gather_fusion.1
  54.3 9.4 %fusion.21 = bf16[16,16,8,384]{3,2,1,0:T(8,128)(2,1)} fusion(bf16[2048,1536]{1,0:T(8,128)(2,1)} %param.7, bf16[16,128,2048]{2,1,0:T(8,128)(2,1)} %param.6), kind=kOutput, calls=%fused_computation.25 | convolution fusion | flops 3222011904 | bytes 11534336 | tf_op jit(solution)/shard_map/dot_general | solution.py:40
  63.8 3.1 %pad.5 = bf16[256,8,1536]{2,1,0:T(8,128)(2,1)} pad(bf16[256,8,128]{2,1,0:T(8,128)(2,1)S(1)} %bitcast.80, bf16[]{:T(256)} %constant.43.clone.1), padding=0_0x0_0x0_1408 | pad | bytes 6815746 | tf_op jit(solution)/shard_map/jit(_pad)/pad | solution.py:89
  66.9 101.1 %all-to-all-done.1 = bf16[16,16,8,1216]{3,2,1,0:T(8,128)(2,1)} async-done(((bf16[16,16,8,1216]{3,2,1,0:T(8,128)(2,1)}), bf16[16,16,8,1216]{3,2,1,0:T(8,128)(2,1)}, u32[]{:S(2)}, u32[]{:S(2)}) %all-to-all-start.1) | async-done | bytes 4980768 | tf_op jit(solution)/shard_map/all_to_all | solution.py:82
  168.1 4.9 %all-to-all-start.2 = ((bf16[16,16,8,384]{3,2,1,0:T(8,128)(2,1)}), bf16[16,16,8,384]{3,2,1,0:T(8,128)(2,1)S(1)}, u32[]{:S(2)}, u32[]{:S(2)}) async-start(bf16[16,16,8,384]{3,2,1,0:T(8,128)(2,1)} %fusion.21), calls=%async_computation.2 | async-start | bytes 3145728 | tf_op jit(solution)/shard_map/all_to_all | solution.py:82
  173.0 1.3 slice.117
  174.3 1.7 copy.30
  176.0 17.3 %fusion = f32[8,8]{1,0:T(8,128)S(1)} fusion(f32[8,192]{1,0:T(8,128)S(1)} %broadcast_subtract_fusion.2, f32[8,1216]{1,0:T(8,128)S(1)} %broadcast_subtract_fusion, bf16[256,8,1216,1]{2,1,0,3:T(8,128)(2,1)} %bitcast.32, bf16[256,8,192]{0,2,1:T(8,128)(2,1)} %copy.30), kind=kOutput, calls=%fused_computation.3 | convolution fusion | flops 7710179328 | bytes 5812480 | tf_op jit(solution)/shard_map/dot_general | solution.py:12
  193.3 2.7 %slice_dynamic-update-slice_fusion = bf16[256,8,1536]{2,1,0:T(8,128)(2,1)S(1)} fusion(bf16[256,8,1536]{2,1,0:T(8,128)(2,1)S(1)} %copy-done.1, bf16[256,8,1216]{2,1,0:T(8,128)(2,1)} %bitcast.18), kind=kLoop, calls=%fused_computation.19 | loop fusion | bytes 8388608 | tf_op jit(solution)/shard_map/dynamic_update_slice | solution.py:91
  196.0 2.7 %copy-done.2 = bf16[256,8,1536]{2,1,0:T(8,128)(2,1)} copy-done((bf16[256,8,1536]{2,1,0:T(8,128)(2,1)}, bf16[256,8,1536]{2,1,0:T(8,128)(2,1)S(1)}, u32[]{:S(2)}) %copy-start.2) | copy-done | bytes 6291480
  198.7 1.4 fusion.11
  200.1 9.1 %all-to-all-done.2 = bf16[16,16,8,384]{3,2,1,0:T(8,128)(2,1)S(1)} async-done(((bf16[16,16,8,384]{3,2,1,0:T(8,128)(2,1)}), bf16[16,16,8,384]{3,2,1,0:T(8,128)(2,1)S(1)}, u32[]{:S(2)}, u32[]{:S(2)}) %all-to-all-start.2) | async-done | bytes 1572896 | tf_op jit(solution)/shard_map/all_to_all | solution.py:82
  209.1 1.3 constant_dynamic-update-slice_fusion
  210.4 4.1 %fusion.1 = f32[8,8]{1,0:T(8,128)S(1)} fusion(f32[8,192]{1,0:T(8,128)S(1)} %broadcast_subtract_fusion.2, f32[8,384]{1,0:T(8,128)S(1)} %broadcast_subtract_fusion.1, bf16[256,8,384,1]{2,1,0,3:T(8,128)(2,1)S(1)} %bitcast.79, bf16[256,8,192]{0,2,1:T(8,128)(2,1)S(1)} %copy-done.3), kind=kOutput, calls=%fused_computation.5 | convolution fusion | flops 2434793472 | bytes 2377984 | tf_op jit(solution)/shard_map/dot_general | solution.py:12
  214.6 0.6 negate_multiply_fusion
  (42 shorter events, 1.8 us)
Async XLA Ops:
  0.6 18.8 %copy-start.6 = (s32[8]{0:T(128)S(1)}, s32[8]{0:T(128)}, u32[]{:S(2)}) copy-start(s32[8]{0:T(128)} %param.10) | copy-start | bytes 100
  0.6 13.1 %copy-start.4 = (s32[8]{0:T(128)S(1)}, s32[8]{0:T(128)}, u32[]{:S(2)}) copy-start(s32[8]{0:T(128)} %param.11) | copy-start | bytes 100
  7.2 39.7 %all-to-all-start = ((bf16[16,16,8,128]{3,2,1,0:T(8,128)(2,1)}), bf16[16,16,8,128]{3,2,1,0:T(8,128)(2,1)S(1)}, u32[]{:S(2)}, u32[]{:S(2)}) async-start(bf16[16,16,8,128]{3,2,1,0:T(8,128)(2,1)} %fusion.27), calls=%async_computation | async-start | bytes 1048576 | tf_op jit(solution)/shard_map/all_to_all | solution.py:82
  46.9 6.2 %copy-start.5 = (f32[1536]{0:T(1024)S(1)}, f32[1536]{0:T(1024)}, u32[]{:S(2)}) copy-start(f32[1536]{0:T(1024)} %param.9) | copy-start | bytes 18436
  46.9 6.2 %copy-start = (f32[128]{0:T(128)S(1)}, f32[128]{0:T(128)}, u32[]{:S(2)}) copy-start(f32[128]{0:T(128)} %param.8) | copy-start | bytes 1540
  46.9 7.1 %slice-start = ((f32[1536]{0:T(1024)}), f32[128]{0:T(128)S(1)}, s32[]{:S(2)}) async-start(f32[1536]{0:T(1024)} %param.9), calls=%async_computation.3 | async-start | bytes 1024 | tf_op jit(solution)/shard_map/slice | solution.py:99
  47.0 121.1 %all-to-all-start.1 = ((bf16[16,16,8,1216]{3,2,1,0:T(8,128)(2,1)}), bf16[16,16,8,1216]{3,2,1,0:T(8,128)(2,1)}, u32[]{:S(2)}, u32[]{:S(2)}) async-start(bf16[16,16,8,1216]{3,2,1,0:T(8,128)(2,1)} %pad_maximum_fusion), calls=%async_computation.1 | async-start | bytes 10485760 | tf_op jit(solution)/shard_map/all_to_all | solution.py:82
  168.1 41.1 %all-to-all-start.2 = ((bf16[16,16,8,384]{3,2,1,0:T(8,128)(2,1)}), bf16[16,16,8,384]{3,2,1,0:T(8,128)(2,1)S(1)}, u32[]{:S(2)}, u32[]{:S(2)}) async-start(bf16[16,16,8,384]{3,2,1,0:T(8,128)(2,1)} %fusion.21), calls=%async_computation.2 | async-start | bytes 3145728 | tf_op jit(solution)/shard_map/all_to_all | solution.py:82
  176.0 17.3 %copy-start.1 = (bf16[256,8,1536]{2,1,0:T(8,128)(2,1)S(1)}, bf16[256,8,1536]{2,1,0:T(8,128)(2,1)}, u32[]{:S(2)}) copy-start(bf16[256,8,1536]{2,1,0:T(8,128)(2,1)} %pad.5) | copy-start | bytes 18874372
  193.3 5.4 %copy-start.3 = (bf16[256,8,192]{0,2,1:T(8,128)(2,1)S(1)}, bf16[256,8,192]{0,2,1:T(8,128)(2,1)}, u32[]{:S(2)}) copy-start(bf16[256,8,192]{0,2,1:T(8,128)(2,1)} %copy.30) | copy-start | bytes 2359300
  196.0 2.7 %copy-start.2 = (bf16[256,8,1536]{2,1,0:T(8,128)(2,1)}, bf16[256,8,1536]{2,1,0:T(8,128)(2,1)S(1)}, u32[]{:S(2)}) copy-start(bf16[256,8,1536]{2,1,0:T(8,128)(2,1)S(1)} %slice_dynamic-update-slice_fusion) | copy-start | bytes 18874372
